TPU v7x, 128 devices: a whole 4x4x4 slice. The times are simulated.
128 devices in a mesh: lon: 16 (over y_hi, z, core), lat: 8 (over y_lo, x).
Axes of the slice: x: 4, y: 4 (y_hi: 2, y_lo: 2; y = y_hi * 2 + y_lo), z: 4, core: 2. Of those that a mesh axis runs over, the one named last changes fastest.
Arguments:
- zonal_current: float32 [32, 512, 2048], P(None, 'lat', 'lon'), may hold values from -6 to 6
- meridional_current: float32 [32, 512, 2048], P(None, 'lat', 'lon'), may hold values from -6 to 6
- warmth_anomaly: float32 [32, 512, 2048], P(None, 'lat', 'lon'), may hold values from -6 to 6
- brine_anomaly: float32 [32, 512, 2048], P(None, 'lat', 'lon'), may hold values from -6 to 6
- marine_indicator: int32 [512, 2048], P('lat', 'lon'), may hold values 0 or 1
- retained_tile_indicator: int32 [32, 128], P('lat', 'lon'), may hold values 0 or 1
- seabed_thickness: float32 [512, 2048], P('lat', 'lon'), may hold values from 0.25 to 2.5
- elevation_pivot_entry: float32 [512, 2048], P('lat', 'lon'), may hold values from 0.1 to 1
Outputs:
- zonal_next: float32 [32, 512, 2048], P(None, 'lat', 'lon')
- meridional_next: float32 [32, 512, 2048], P(None, 'lat', 'lon')
- temperature_next: float32 [32, 512, 2048], P(None, 'lat', 'lon')
- salinity_next: float32 [32, 512, 2048], P(None, 'lat', 'lon')
- surface_pressure: float32 [512, 2048], P('lat', 'lon')
- pressure_residual: float32 [512, 2048], P('lat', 'lon')
All inputs are finite; a program needn't handle non-finite values. No bound on the sum of `marine_indicator` or of `retained_tile_indicator` on one device may be relied on, other than what follows from the above.
Results may differ from a plain program's by a relative error of at most 0.0003.
Values sent between devices are 32-bit elements; how exact they have to be, the bound alone decides.
No kernel may reach another device: no remote copies, remote signals or barrier semaphores. Data moves between devices by JAX's collectives and lax.ppermute only.
A program may use at most 128 MiB of HBM per device.

v0:
```python
import jax
import jax.numpy as jnp
from jax import lax
from jax.sharding import PartitionSpec as P

BLK = 16
ITERS = 3


time_step = 0.1
viscosity = 0.2
diffusivity = 0.15
thermal = 0.2
haline = 0.8
source_gain = 8.0


def allsum(value):
    count = lax.axis_size("lon") * lax.axis_size("lat")
    spread = jnp.broadcast_to(value, (count,) + jnp.shape(value))
    gathered = lax.all_to_all(spread, ("lon", "lat"), 0, 0, tiled=True)
    return jnp.sum(gathered, axis=0)


def halos(cells, parity):
    if not isinstance(cells, (list, tuple)):
        cells = [cells]
    lon_count = lax.axis_size("lon")
    lat_count = lax.axis_size("lat")

    def edge(index):
        return jnp.concatenate([item[index] for item in cells], axis=0)

    first_col = edge((Ellipsis, slice(None), slice(0, 1)))
    last_col = edge((Ellipsis, slice(None), slice(-1, None)))
    first_row = edge((Ellipsis, slice(0, 1), slice(None)))
    last_row = edge((Ellipsis, slice(-1, None), slice(None)))
    east = lax.ppermute(first_col, "lon", [((i + 1) % lon_count, i) for i in range(lon_count)])
    west = lax.ppermute(last_col, "lon", [(i, (i + 1) % lon_count) for i in range(lon_count)])
    north = lax.ppermute(first_row, "lat", [(i + 1, i) for i in range(lat_count - 1)])
    south = lax.ppermute(last_row, "lat", [(i, i + 1) for i in range(lat_count - 1)])
    mirror = lax.ppermute(last_row, "lon", [(i, lon_count - 1 - i) for i in range(lon_count)])
    folded = parity * mirror[..., ::-1]
    north = jnp.where(lax.axis_index("lat") == lat_count - 1, folded, north)
    return east, west, north, south


def around(cells, halo):
    east, west, north, south = halo
    return (
        jnp.concatenate([cells[..., :, 1:], east], axis=-1),
        jnp.concatenate([west, cells[..., :, :-1]], axis=-1),
        jnp.concatenate([cells[..., 1:, :], north], axis=-2),
        jnp.concatenate([south, cells[..., :-1, :]], axis=-2),
    )


def laplace(field, near):
    return near[0] + near[1] + near[2] + near[3] - 4.0 * field


def local(
    zonal_current,
    meridional_current,
    warmth_anomaly,
    brine_anomaly,
    marine_indicator,
    retained_tile_indicator,
    seabed_thickness,
    elevation_pivot_entry,
):
    level_fields, height, breadth = zonal_current.shape
    marine_snapshot = marine_indicator.astype(jnp.float32)
    zonal = zonal_current * marine_snapshot
    merid = meridional_current * marine_snapshot
    enthalpy_content = warmth_anomaly * marine_snapshot
    salt = brine_anomaly * marine_snapshot
    kept = jnp.repeat(
        jnp.repeat(retained_tile_indicator.astype(jnp.float32), BLK, axis=0), BLK, axis=1
    )
    open_cells = marine_snapshot * kept
    column = seabed_thickness * open_cells

    stack = [zonal, merid, enthalpy_content, salt, column[None]]
    parity = jnp.concatenate(
        [
            -jnp.ones((2 * level_fields,), jnp.float32),
            jnp.ones((2 * level_fields + 1,), jnp.float32),
        ]
    )[:, None, None]
    halo_all = halos(stack, parity)

    def part(first, count):
        return tuple(item[first : first + count] for item in halo_all)

    near_u = around(zonal, part(0, level_fields))
    near_v = around(merid, part(level_fields, level_fields))
    halo_t = part(2 * level_fields, level_fields)
    halo_s = part(3 * level_fields, level_fields)
    near_t = around(enthalpy_content, halo_t)
    near_s = around(salt, halo_s)
    halo_c = tuple(item[4 * level_fields] for item in halo_all)
    near_c = around(column, halo_c)

    pressure = jnp.cumsum(haline * salt - thermal * enthalpy_content, axis=0)
    halo_p = tuple(
        jnp.cumsum(haline * halo_s[side] - thermal * halo_t[side], axis=0) for side in range(4)
    )
    near_p = around(pressure, halo_p)

    total_rows = height * lax.axis_size("lat")
    rows_global = (lax.axis_index("lat") * height + jnp.arange(height)).astype(jnp.float32)
    coriolis = (2.0 * (rows_global + 0.5) / total_rows - 1.0)[:, None]
    zonal_next = marine_snapshot * (
        zonal
        + time_step
        * (coriolis * merid - 0.5 * (near_p[0] - near_p[1]) + viscosity * laplace(zonal, near_u))
    )
    merid_next = marine_snapshot * (
        merid
        + time_step
        * (-coriolis * zonal - 0.5 * (near_p[2] - near_p[3]) + viscosity * laplace(merid, near_v))
    )
    tracers = []
    for tracer, near_q in ((enthalpy_content, near_t), (salt, near_s)):
        flux = 0.5 * (
            near_u[0] * near_q[0]
            - near_u[1] * near_q[1]
            + near_v[2] * near_q[2]
            - near_v[3] * near_q[3]
        )
        tracers.append(
            marine_snapshot * (tracer + time_step * (-flux + diffusivity * laplace(tracer, near_q)))
        )
    zonal_mean = jnp.sum(zonal_next, axis=0) / level_fields
    merid_mean = jnp.sum(merid_next, axis=0) / level_fields

    means = jnp.stack([zonal_mean, merid_mean], axis=0)
    halo_m = halos([zonal_mean[None], merid_mean[None]], -jnp.ones((2, 1, 1), jnp.float32))
    near_m = around(means, halo_m)
    rhs = (
        -source_gain
        * open_cells
        * 0.5
        * (near_m[0][0] - near_m[1][0] + near_m[2][1] - near_m[3][1])
    )
    weights = [0.5 * (column + near_c[side]) for side in range(4)]
    diag = elevation_pivot_entry + weights[0] + weights[1] + weights[2] + weights[3]
    unit = jnp.ones((), jnp.float32)

    def apply(direction, halo_d):
        near_x = around(direction, halo_d)
        return open_cells * (
            diag * direction
            - weights[0] * near_x[0]
            - weights[1] * near_x[1]
            - weights[2] * near_x[2]
            - weights[3] * near_x[3]
        )

    solution = jnp.zeros_like(rhs)
    residual = rhs
    precond = residual / diag
    direction = precond
    halo_d = halos(direction, unit)
    image = apply(direction, halo_d)
    pair = allsum(jnp.stack([jnp.sum(residual * precond), jnp.sum(direction * image)]))
    product_now = pair[0]
    curvature = pair[1]
    for step in range(ITERS):
        alpha = product_now / curvature
        solution = solution + alpha * direction
        residual = residual - alpha * image
        if step + 1 < ITERS:
            precond = residual / diag
            halo_z = halos(precond, unit)
            product_next = allsum(jnp.sum(residual * precond))
            beta = product_next / product_now
            direction = precond + beta * direction
            halo_d = tuple(hz + beta * hd for hz, hd in zip(halo_z, halo_d))
            product_now = product_next
            image = apply(direction, halo_d)
            curvature = allsum(jnp.sum(direction * image))
    return (zonal_next, merid_next, tracers[0], tracers[1], solution, residual)


def solution(mesh):
    in_specs = (
        P(None, "lat", "lon"),
        P(None, "lat", "lon"),
        P(None, "lat", "lon"),
        P(None, "lat", "lon"),
        P("lat", "lon"),
        P("lat", "lon"),
        P("lat", "lon"),
        P("lat", "lon"),
    )
    out_specs = (
        P(None, "lat", "lon"),
        P(None, "lat", "lon"),
        P(None, "lat", "lon"),
        P(None, "lat", "lon"),
        P("lat", "lon"),
        P("lat", "lon"),
    )
    return jax.shard_map(local, mesh=mesh, in_specs=in_specs, out_specs=out_specs, check_vma=False)
```

profile of v0, /device:TPU:1, one launch (start us, length us, event | category | flops | bytes accessed | tf_op | source)
XLA Modules:
  0.0 276.8 jit_solution(10545668337968932446)
XLA Ops:
  1.4 4.0 %broadcast_multiply_fusion.1 = (f32[32,64,128]{2,1,0:T(8,128)S(1)}, f32[32,64,128]{2,1,0:T(8,128)S(1)}, f32[32,64,128]{2,1,0:T(8,128)}, f32[32,64,128]{2,1,0:T(8,128)S(1)}) fusion(f32[32,64,128]{2,1,0:T(8,128)} %param.11, f32[64,128]{1,0:T(8,128)S(1)} %convert_element_type.17, f32[32,64,128]{2,1,0:T(8,128)} %param.10, f32[32,64,128]{2,1,0:T(8,128)} %param.9, ...), kind=kLoop, calls=%fused_computation.44 | loop fusion | flops 1048576 | bytes 8421376 | tf_op jit(solution)/shard_map/mul | solution.py:77
  10.5 7.8 %collective-permute-start.2 = (f32[129,1,128]{2,1,0:T(1,128)}, f32[129,1,128]{2,1,0:T(1,128)}, u32[]{:S(2)}, u32[]{:S(2)}) collective-permute-start(f32[129,1,128]{2,1,0:T(1,128)} %get-tuple-element.125), channel_id=1, source_target_pairs={{0,120},{8,112},{16,104},{24,96},{32,88},{40,80},{48,72},{56,64},{... | collective-permute-start | bytes 198152 | tf_op jit(solution)/shard_map/ppermute | solution.py:42
  18.3 3.7 %collective-permute-start.4 = (f32[129,1,128]{2,1,0:T(1,128)}, f32[129,1,128]{2,1,0:T(1,128)}, u32[]{:S(2)}, u32[]{:S(2)}) collective-permute-start(f32[129,1,128]{2,1,0:T(1,128)} %get-tuple-element.125), channel_id=1, source_target_pairs={{0,1},{1,2},{2,3},{3,4},{4,5},{5,6},{6,7},{8,9},{9,10},{10,11},{11... | collective-permute-start | bytes 198152 | tf_op jit(solution)/shard_map/ppermute | solution.py:41
  23.3 2.7 fusion.100
  26.0 2.7 fusion.102
  28.8 1.8 copy.119
  30.6 1.8 copy.120
  32.3 1.8 copy.117
  36.2 1.8 copy.127
  37.9 1.8 copy.128
  39.7 1.8 copy.125
  41.5 1.8 copy.126
  48.5 2.1 fusion.95
  50.6 2.6 fusion.98
  56.0 2.8 fusion.91
  66.1 1.8 copy.135
  67.9 1.8 copy.136
  69.7 1.9 copy.133
  71.6 1.8 copy.134
  79.7 6.0 %fusion.88 = (f32[64,128]{1,0:T(8,128)S(1)}, f32[32,64,128]{2,1,0:T(8,128)}) fusion(f32[32,63,128]{2,1,0:T(8,128)S(1)} %copy-done.2, f32[32,1,128]{2,1,0:T(1,128)S(1)} %get-tuple-element.73, f32[32,1,128]{2,1,0:T(1,128)S(1)} %get-tuple-element.69, f32[32,63,128]{2,1,0:T(8,128)} %get-tuple-element.143, f32[32,64,127]{2,1,0:T(8,128)} %get-tuple-element.43, ...), kind=kLoop, calls=%fused_computation.179 | loop fusion | flops 6021120 | bytes 9502976 | tf_op jit(solution)/shard_map/reduce_sum | solution.py:136
  87.0 3.8 %fusion.86 = (f32[64,128]{1,0:T(8,128)S(1)}, f32[32,64,128]{2,1,0:T(8,128)}) fusion(f32[32,63,128]{2,1,0:T(8,128)S(1)} %copy-done.13, f32[32,1,128]{2,1,0:T(1,128)S(1)} %get-tuple-element.75, f32[32,1,128]{2,1,0:T(1,128)S(1)} %get-tuple-element.71, f32[32,63,128]{2,1,0:T(8,128)S(1)} %copy-done.12, f32[32,64,127]{2,1,0:T(8,128)S(1)} %copy-done.6, ...), kind=kLoop, calls=%fused_computation.178 | loop fusion | flops 6021120 | bytes 9502976 | tf_op jit(solution)/shard_map/reduce_sum | solution.py:135
  92.4 4.0 %collective-permute-start.9 = (f32[2,1,128]{2,1,0:T(1,128)S(1)}, f32[2,1,128]{2,1,0:T(1,128)S(1)}, u32[]{:S(2)}, u32[]{:S(2)}) collective-permute-start(f32[2,1,128]{2,1,0:T(1,128)S(1)} %pad_maximum_fusion.19), channel_id=1, source_target_pairs={{0,1},{1,2},{2,3},{3,4},{4,5},{5,6},{6,7},{8,9},{9,10},{10,11},{11... | collective-permute-start | bytes 3080 | tf_op jit(solution)/shard_map/ppermute | solution.py:41
  97.6 4.3 %collective-permute-start.5 = (f32[2,64,1]{2,1,0:T(8,128)}, f32[2,64,1]{2,1,0:T(8,128)S(1)}, u32[]{:S(2)}, u32[]{:S(2)}) collective-permute-start(f32[2,64,1]{2,1,0:T(8,128)} %pad_maximum_fusion.12), channel_id=1, source_target_pairs={{8,0},{16,8},{24,16},{32,24},{40,32},{48,40},{56,48},{64,56},{72,6... | collective-permute-start | bytes 1544 | tf_op jit(solution)/shard_map/ppermute | solution.py:38
  105.0 1.8 collective-permute-done.8
  111.7 3.0 %collective-permute-start.12 = (f32[1,128]{1,0:T(1,128)}, f32[1,128]{1,0:T(1,128)}, u32[]{:S(2)}, u32[]{:S(2)}) collective-permute-start(f32[1,128]{1,0:T(1,128)} %get-tuple-element.109), channel_id=1, source_target_pairs={{0,120},{8,112},{16,104},{24,96},{32,88},{40,80},{48,72},{56,64},{... | collective-permute-start | bytes 1544 | tf_op jit(solution)/shard_map/ppermute | solution.py:42
  116.7 4.5 %collective-permute-start.14 = (f32[1,128]{1,0:T(1,128)}, f32[1,128]{1,0:T(1,128)}, u32[]{:S(2)}, u32[]{:S(2)}) collective-permute-start(f32[1,128]{1,0:T(1,128)} %get-tuple-element.109), channel_id=1, source_target_pairs={{0,1},{1,2},{2,3},{3,4},{4,5},{5,6},{6,7},{8,9},{9,10},{10,11},{11... | collective-permute-start | bytes 1544 | tf_op jit(solution)/shard_map/ppermute | solution.py:41
  121.2 3.1 %collective-permute-start.10 = (f32[64,1]{1,0:T(8,128)}, f32[64,1]{1,0:T(8,128)S(1)}, u32[]{:S(2)}, u32[]{:S(2)}) collective-permute-start(f32[64,1]{1,0:T(8,128)} %get-tuple-element.104), channel_id=1, source_target_pairs={{8,0},{16,8},{24,16},{32,24},{40,32},{48,40},{56,48},{64,56},{72,6... | collective-permute-start | bytes 776 | tf_op jit(solution)/shard_map/ppermute | solution.py:38
  127.9 2.1 multiply_reduce_fusion.5
  132.0 14.8 %all-to-all-start = ((f32[128,1,2]{2,1,0:T(1,128)}), f32[128,1,2]{2,1,0:T(1,128)}, u32[]{:S(2)}, u32[]{:S(2)}) async-start(f32[128,1,2]{2,1,0:T(1,128)} %broadcast_in_dim.19), calls=%async_computation | async-start | bytes 131072 | tf_op jit(solution)/shard_map/all_to_all | solution.py:21
  146.8 2.2 fusion.92
  149.0 1.8 copy.139
  150.8 1.8 copy.140
  152.6 1.9 copy.137
  154.5 1.8 copy.138
  162.5 10.2 %all-to-all-start.1 = ((f32[128,1,1]{2,1,0:T(1,128)}), f32[128,1,1]{2,1,0:T(1,128)}, u32[]{:S(2)}, u32[]{:S(2)}) async-start(f32[128,1,1]{2,1,0:T(1,128)} %broadcast_in_dim.40), calls=%async_computation.1 | async-start | bytes 131072 | tf_op jit(solution)/shard_map/all_to_all | solution.py:21
  173.3 6.0 %collective-permute-start.17 = (f32[1,128]{1,0:T(1,128)}, f32[1,128]{1,0:T(1,128)}, u32[]{:S(2)}, u32[]{:S(2)}) collective-permute-start(f32[1,128]{1,0:T(1,128)} %get-tuple-element.101), channel_id=1, source_target_pairs={{0,120},{8,112},{16,104},{24,96},{32,88},{40,80},{48,72},{56,64},{... | collective-permute-start | bytes 1544 | tf_op jit(solution)/shard_map/ppermute | solution.py:42
  179.3 3.7 %collective-permute-start.19 = (f32[1,128]{1,0:T(1,128)}, f32[1,128]{1,0:T(1,128)}, u32[]{:S(2)}, u32[]{:S(2)}) collective-permute-start(f32[1,128]{1,0:T(1,128)} %get-tuple-element.101), channel_id=1, source_target_pairs={{0,1},{1,2},{2,3},{3,4},{4,5},{5,6},{6,7},{8,9},{9,10},{10,11},{11... | collective-permute-start | bytes 1544 | tf_op jit(solution)/shard_map/ppermute | solution.py:41
  195.8 2.1 multiply_reduce_fusion.2
  199.2 8.4 %all-to-all-start.2 = ((f32[128,1,1]{2,1,0:T(1,128)}), f32[128,1,1]{2,1,0:T(1,128)}, u32[]{:S(2)}, u32[]{:S(2)}) async-start(f32[128,1,1]{2,1,0:T(1,128)} %broadcast_in_dim.41), calls=%async_computation.2 | async-start | bytes 131072 | tf_op jit(solution)/shard_map/all_to_all | solution.py:21
  207.7 6.0 %add_multiply_fusion = f32[32,64,128]{2,1,0:T(8,128)} fusion(f32[32,64,128]{2,1,0:T(8,128)S(1)} %get-tuple-element.126, f32[32,63,128]{2,1,0:T(8,128)} %get-tuple-element.35, f32[32,1,128]{2,1,0:T(1,128)S(1)} %copy-done.39, f32[32,1,128]{2,1,0:T(1,128)S(1)} %copy-done.38, f32[32,63,128]{2,1,0:T(8,128)} %get-tuple-element.34, ...), kind=kLoop, calls=%fused_computation.35 | loop fusion | flops 7077888 | bytes 10518528 | tf_op jit(solution)/shard_map/mul | solution.py:133
  213.7 3.5 %all-to-all-done.2 = f32[128,1,1]{2,1,0:T(1,128)} async-done(((f32[128,1,1]{2,1,0:T(1,128)}), f32[128,1,1]{2,1,0:T(1,128)}, u32[]{:S(2)}, u32[]{:S(2)}) %all-to-all-start.2) | async-done | bytes 544 | tf_op jit(solution)/shard_map/all_to_all | solution.py:21
  220.1 2.0 multiply_reduce_fusion.1
  224.1 6.8 %all-to-all-start.3 = ((f32[128,1,1]{2,1,0:T(1,128)}), f32[128,1,1]{2,1,0:T(1,128)}, u32[]{:S(2)}, u32[]{:S(2)}) async-start(f32[128,1,1]{2,1,0:T(1,128)} %broadcast_in_dim.42), calls=%async_computation.3 | async-start | bytes 131072 | tf_op jit(solution)/shard_map/all_to_all | solution.py:21
  231.5 6.0 %collective-permute-start.22 = (f32[1,128]{1,0:T(1,128)}, f32[1,128]{1,0:T(1,128)}, u32[]{:S(2)}, u32[]{:S(2)}) collective-permute-start(f32[1,128]{1,0:T(1,128)} %get-tuple-element.93), channel_id=1, source_target_pairs={{0,120},{8,112},{16,104},{24,96},{32,88},{40,80},{48,72},{56,64},{... | collective-permute-start | bytes 1544 | tf_op jit(solution)/shard_map/ppermute | solution.py:42
  237.6 3.6 %collective-permute-start.24 = (f32[1,128]{1,0:T(1,128)}, f32[1,128]{1,0:T(1,128)}, u32[]{:S(2)}, u32[]{:S(2)}) collective-permute-start(f32[1,128]{1,0:T(1,128)} %get-tuple-element.93), channel_id=1, source_target_pairs={{0,1},{1,2},{2,3},{3,4},{4,5},{5,6},{6,7},{8,9},{9,10},{10,11},{11... | collective-permute-start | bytes 1544 | tf_op jit(solution)/shard_map/ppermute | solution.py:41
  256.0 7.8 %all-to-all-start.4 = ((f32[128,1,1]{2,1,0:T(1,128)}), f32[128,1,1]{2,1,0:T(1,128)S(1)}, u32[]{:S(2)}, u32[]{:S(2)}) async-start(f32[128,1,1]{2,1,0:T(1,128)} %broadcast_in_dim.43), calls=%async_computation.4 | async-start | bytes 131072 | tf_op jit(solution)/shard_map/all_to_all | solution.py:21
  263.9 5.7 %add_multiply_fusion.1 = f32[32,64,128]{2,1,0:T(8,128)} fusion(f32[32,64,128]{2,1,0:T(8,128)S(1)} %get-tuple-element.127, f32[32,63,128]{2,1,0:T(8,128)} %get-tuple-element.134, f32[32,1,128]{2,1,0:T(1,128)S(1)} %copy-done.37, f32[32,1,128]{2,1,0:T(1,128)S(1)} %copy-done.36, f32[32,63,128]{2,1,0:T(8,128)} %get-tuple-element.135, ...), kind=kLoop, calls=%fused_computation.36 | loop fusion | flops 7077888 | bytes 10518528 | tf_op jit(solution)/shard_map/mul | solution.py:133
  269.6 3.9 %all-to-all-done.4 = f32[128,1,1]{2,1,0:T(1,128)S(1)} async-done(((f32[128,1,1]{2,1,0:T(1,128)}), f32[128,1,1]{2,1,0:T(1,128)S(1)}, u32[]{:S(2)}, u32[]{:S(2)}) %all-to-all-start.4) | async-done | bytes 544 | tf_op jit(solution)/shard_map/all_to_all | solution.py:21
  (254 shorter events, 88.1 us)
Async XLA Ops:
  10.5 62.9 %collective-permute-start.2 = (f32[129,1,128]{2,1,0:T(1,128)}, f32[129,1,128]{2,1,0:T(1,128)}, u32[]{:S(2)}, u32[]{:S(2)}) collective-permute-start(f32[129,1,128]{2,1,0:T(1,128)} %get-tuple-element.125), channel_id=1, source_target_pairs={{0,120},{8,112},{16,104},{24,96},{32,88},{40,80},{48,72},{56,64},{... | collective-permute-start | bytes 198152 | tf_op jit(solution)/shard_map/ppermute | solution.py:42
  18.3 58.4 %collective-permute-start.4 = (f32[129,1,128]{2,1,0:T(1,128)}, f32[129,1,128]{2,1,0:T(1,128)}, u32[]{:S(2)}, u32[]{:S(2)}) collective-permute-start(f32[129,1,128]{2,1,0:T(1,128)} %get-tuple-element.125), channel_id=1, source_target_pairs={{0,1},{1,2},{2,3},{3,4},{4,5},{5,6},{6,7},{8,9},{9,10},{10,11},{11... | collective-permute-start | bytes 198152 | tf_op jit(solution)/shard_map/ppermute | solution.py:41
  22.0 52.9 %collective-permute-start.3 = (f32[129,1,128]{2,1,0:T(1,128)}, f32[129,1,128]{2,1,0:T(1,128)}, u32[]{:S(2)}, u32[]{:S(2)}) collective-permute-start(f32[129,1,128]{2,1,0:T(1,128)} %get-tuple-element.124), channel_id=1, source_target_pairs={{1,0},{2,1},{3,2},{4,3},{5,4},{6,5},{7,6},{9,8},{10,9},{11,10},{12... | collective-permute-start | bytes 198152 | tf_op jit(solution)/shard_map/ppermute | solution.py:40
  36.0 23.9 %collective-permute-start = (f32[129,64,1]{0,1,2:T(8,128)S(1)}, f32[129,64,1]{0,1,2:T(8,128)S(1)}, u32[]{:S(2)}, u32[]{:S(2)}) collective-permute-start(f32[129,64,1]{0,1,2:T(8,128)S(1)} %concatenate.144), channel_id=1, source_target_pairs={{8,0},{16,8},{24,16},{32,24},{40,32},{48,40},{56,48},{64,56},{72,6... | collective-permute-start | bytes 99080 | tf_op jit(solution)/shard_map/ppermute | solution.py:38
  44.0 18.1 %collective-permute-start.1 = (f32[129,64,1]{0,1,2:T(8,128)}, f32[129,64,1]{0,1,2:T(8,128)S(1)}, u32[]{:S(2)}, u32[]{:S(2)}) collective-permute-start(f32[129,64,1]{0,1,2:T(8,128)} %concatenate.146), channel_id=1, source_target_pairs={{0,8},{8,16},{16,24},{24,32},{32,40},{40,48},{48,56},{56,64},{64,7... | collective-permute-start | bytes 99080 | tf_op jit(solution)/shard_map/ppermute | solution.py:39
  71.6 7.4 %copy-start.2 = (f32[32,63,128]{2,1,0:T(8,128)S(1)}, f32[32,63,128]{2,1,0:T(8,128)}, u32[]{:S(2)}) copy-start(f32[32,63,128]{2,1,0:T(8,128)} %get-tuple-element.142) | copy-start | bytes 3096580
  79.6 6.2 %copy-start.6 = (f32[32,64,127]{2,1,0:T(8,128)S(1)}, f32[32,64,127]{2,1,0:T(8,128)}, u32[]{:S(2)}) copy-start(f32[32,64,127]{2,1,0:T(8,128)} %get-tuple-element.140) | copy-start | bytes 3121156
  79.6 6.2 %copy-start.7 = (f32[32,64,127]{2,1,0:T(8,128)S(1)}, f32[32,64,127]{2,1,0:T(8,128)}, u32[]{:S(2)}) copy-start(f32[32,64,127]{2,1,0:T(8,128)} %get-tuple-element.141) | copy-start | bytes 3121156
  79.6 6.2 %copy-start.8 = (f32[32,64,128]{2,1,0:T(8,128)S(1)}, f32[32,64,128]{2,1,0:T(8,128)}, u32[]{:S(2)}) copy-start(f32[32,64,128]{2,1,0:T(8,128)} %param.9) | copy-start | bytes 3145732
  79.6 6.2 %copy-start.9 = (f32[32,64,128]{2,1,0:T(8,128)S(1)}, f32[32,64,128]{2,1,0:T(8,128)}, u32[]{:S(2)}) copy-start(f32[32,64,128]{2,1,0:T(8,128)} %param.8) | copy-start | bytes 3145732
  79.6 6.2 %copy-start.10 = (f32[32,64,1]{2,1,0:T(8,128)S(1)}, f32[32,64,1]{2,1,0:T(8,128)}, u32[]{:S(2)}) copy-start(f32[32,64,1]{2,1,0:T(8,128)} %fusion.128) | copy-start | bytes 24580
  79.6 6.3 %copy-start.11 = (f32[32,64,1]{2,1,0:T(8,128)S(1)}, f32[32,64,1]{2,1,0:T(8,128)}, u32[]{:S(2)}) copy-start(f32[32,64,1]{2,1,0:T(8,128)} %fusion.129) | copy-start | bytes 24580
  79.6 6.8 %copy-start.12 = (f32[32,63,128]{2,1,0:T(8,128)S(1)}, f32[32,63,128]{2,1,0:T(8,128)}, u32[]{:S(2)}) copy-start(f32[32,63,128]{2,1,0:T(8,128)} %get-tuple-element.58) | copy-start | bytes 3096580
  79.7 7.1 %copy-start.13 = (f32[32,63,128]{2,1,0:T(8,128)S(1)}, f32[32,63,128]{2,1,0:T(8,128)}, u32[]{:S(2)}) copy-start(f32[32,63,128]{2,1,0:T(8,128)} %get-tuple-element.59) | copy-start | bytes 3096580
  79.7 7.4 %copy-start.14 = (f32[32,64,127]{2,1,0:T(8,128)S(1)}, f32[32,64,127]{2,1,0:T(8,128)}, u32[]{:S(2)}) copy-start(f32[32,64,127]{2,1,0:T(8,128)} %get-tuple-element.46) | copy-start | bytes 3121156
  92.3 12.6 %collective-permute-start.7 = (f32[2,1,128]{2,1,0:T(1,128)S(1)}, f32[2,1,128]{2,1,0:T(1,128)S(1)}, u32[]{:S(2)}, u32[]{:S(2)}) collective-permute-start(f32[2,1,128]{2,1,0:T(1,128)S(1)} %pad_maximum_fusion.19), channel_id=1, source_target_pairs={{0,120},{8,112},{16,104},{24,96},{32,88},{40,80},{48,72},{56,64},{... | collective-permute-start | bytes 3080 | tf_op jit(solution)/shard_map/ppermute | solution.py:42
  92.4 14.4 %collective-permute-start.9 = (f32[2,1,128]{2,1,0:T(1,128)S(1)}, f32[2,1,128]{2,1,0:T(1,128)S(1)}, u32[]{:S(2)}, u32[]{:S(2)}) collective-permute-start(f32[2,1,128]{2,1,0:T(1,128)S(1)} %pad_maximum_fusion.19), channel_id=1, source_target_pairs={{0,1},{1,2},{2,3},{3,4},{4,5},{5,6},{6,7},{8,9},{9,10},{10,11},{11... | collective-permute-start | bytes 3080 | tf_op jit(solution)/shard_map/ppermute | solution.py:41
  97.6 9.2 %collective-permute-start.5 = (f32[2,64,1]{2,1,0:T(8,128)}, f32[2,64,1]{2,1,0:T(8,128)S(1)}, u32[]{:S(2)}, u32[]{:S(2)}) collective-permute-start(f32[2,64,1]{2,1,0:T(8,128)} %pad_maximum_fusion.12), channel_id=1, source_target_pairs={{8,0},{16,8},{24,16},{32,24},{40,32},{48,40},{56,48},{64,56},{72,6... | collective-permute-start | bytes 1544 | tf_op jit(solution)/shard_map/ppermute | solution.py:38
  102.5 4.3 %collective-permute-start.6 = (f32[2,64,1]{2,1,0:T(8,128)}, f32[2,64,1]{2,1,0:T(8,128)}, u32[]{:S(2)}, u32[]{:S(2)}) collective-permute-start(f32[2,64,1]{2,1,0:T(8,128)} %pad_maximum_fusion.13), channel_id=1, source_target_pairs={{0,8},{8,16},{16,24},{24,32},{32,40},{40,48},{48,56},{56,64},{64,7... | collective-permute-start | bytes 1544 | tf_op jit(solution)/shard_map/ppermute | solution.py:39
  102.5 4.3 %collective-permute-start.8 = (f32[2,1,128]{2,1,0:T(1,128)S(1)}, f32[2,1,128]{2,1,0:T(1,128)S(1)}, u32[]{:S(2)}, u32[]{:S(2)}) collective-permute-start(f32[2,1,128]{2,1,0:T(1,128)S(1)} %pad_maximum_fusion.20), channel_id=1, source_target_pairs={{1,0},{2,1},{3,2},{4,3},{5,4},{6,5},{7,6},{9,8},{10,9},{11,10},{12... | collective-permute-start | bytes 3080 | tf_op jit(solution)/shard_map/ppermute | solution.py:40
  111.7 12.6 %collective-permute-start.12 = (f32[1,128]{1,0:T(1,128)}, f32[1,128]{1,0:T(1,128)}, u32[]{:S(2)}, u32[]{:S(2)}) collective-permute-start(f32[1,128]{1,0:T(1,128)} %get-tuple-element.109), channel_id=1, source_target_pairs={{0,120},{8,112},{16,104},{24,96},{32,88},{40,80},{48,72},{56,64},{... | collective-permute-start | bytes 1544 | tf_op jit(solution)/shard_map/ppermute | solution.py:42
  114.7 10.9 %collective-permute-start.13 = (f32[1,128]{1,0:T(1,128)}, f32[1,128]{1,0:T(1,128)}, u32[]{:S(2)}, u32[]{:S(2)}) collective-permute-start(f32[1,128]{1,0:T(1,128)} %get-tuple-element.108), channel_id=1, source_target_pairs={{1,0},{2,1},{3,2},{4,3},{5,4},{6,5},{7,6},{9,8},{10,9},{11,10},{12... | collective-permute-start | bytes 1544 | tf_op jit(solution)/shard_map/ppermute | solution.py:40
  116.0 11.9 %copy-start.23 = (f32[64,128]{1,0:T(8,128)S(1)}, f32[64,128]{1,0:T(8,128)}, u32[]{:S(2)}) copy-start(f32[64,128]{1,0:T(8,128)} %get-tuple-element.25) | copy-start | bytes 98308
  116.7 11.2 %collective-permute-start.14 = (f32[1,128]{1,0:T(1,128)}, f32[1,128]{1,0:T(1,128)}, u32[]{:S(2)}, u32[]{:S(2)}) collective-permute-start(f32[1,128]{1,0:T(1,128)} %get-tuple-element.109), channel_id=1, source_target_pairs={{0,1},{1,2},{2,3},{3,4},{4,5},{5,6},{6,7},{8,9},{9,10},{10,11},{11... | collective-permute-start | bytes 1544 | tf_op jit(solution)/shard_map/ppermute | solution.py:41
  121.2 5.1 %collective-permute-start.10 = (f32[64,1]{1,0:T(8,128)}, f32[64,1]{1,0:T(8,128)S(1)}, u32[]{:S(2)}, u32[]{:S(2)}) collective-permute-start(f32[64,1]{1,0:T(8,128)} %get-tuple-element.104), channel_id=1, source_target_pairs={{8,0},{16,8},{24,16},{32,24},{40,32},{48,40},{56,48},{64,56},{72,6... | collective-permute-start | bytes 776 | tf_op jit(solution)/shard_map/ppermute | solution.py:38
  124.3 3.6 %collective-permute-start.11 = (f32[64,1]{1,0:T(8,128)}, f32[64,1]{1,0:T(8,128)S(1)}, u32[]{:S(2)}, u32[]{:S(2)}) collective-permute-start(f32[64,1]{1,0:T(8,128)} %get-tuple-element.105), channel_id=1, source_target_pairs={{0,8},{8,16},{16,24},{24,32},{32,40},{40,48},{48,56},{56,64},{64,7... | collective-permute-start | bytes 776 | tf_op jit(solution)/shard_map/ppermute | solution.py:39
  132.0 24.4 %all-to-all-start = ((f32[128,1,2]{2,1,0:T(1,128)}), f32[128,1,2]{2,1,0:T(1,128)}, u32[]{:S(2)}, u32[]{:S(2)}) async-start(f32[128,1,2]{2,1,0:T(1,128)} %broadcast_in_dim.19), calls=%async_computation | async-start | bytes 131072 | tf_op jit(solution)/shard_map/all_to_all | solution.py:21
  162.5 23.6 %all-to-all-start.1 = ((f32[128,1,1]{2,1,0:T(1,128)}), f32[128,1,1]{2,1,0:T(1,128)}, u32[]{:S(2)}, u32[]{:S(2)}) async-start(f32[128,1,1]{2,1,0:T(1,128)} %broadcast_in_dim.40), calls=%async_computation.1 | async-start | bytes 131072 | tf_op jit(solution)/shard_map/all_to_all | solution.py:21
  173.3 19.8 %collective-permute-start.17 = (f32[1,128]{1,0:T(1,128)}, f32[1,128]{1,0:T(1,128)}, u32[]{:S(2)}, u32[]{:S(2)}) collective-permute-start(f32[1,128]{1,0:T(1,128)} %get-tuple-element.101), channel_id=1, source_target_pairs={{0,120},{8,112},{16,104},{24,96},{32,88},{40,80},{48,72},{56,64},{... | collective-permute-start | bytes 1544 | tf_op jit(solution)/shard_map/ppermute | solution.py:42
  179.3 12.6 %collective-permute-start.19 = (f32[1,128]{1,0:T(1,128)}, f32[1,128]{1,0:T(1,128)}, u32[]{:S(2)}, u32[]{:S(2)}) collective-permute-start(f32[1,128]{1,0:T(1,128)} %get-tuple-element.101), channel_id=1, source_target_pairs={{0,1},{1,2},{2,3},{3,4},{4,5},{5,6},{6,7},{8,9},{9,10},{10,11},{11... | collective-permute-start | bytes 1544 | tf_op jit(solution)/shard_map/ppermute | solution.py:41
  183.0 7.2 %collective-permute-start.15 = (f32[64,1]{1,0:T(8,128)S(1)}, f32[64,1]{1,0:T(8,128)}, u32[]{:S(2)}, u32[]{:S(2)}) collective-permute-start(f32[64,1]{1,0:T(8,128)S(1)} %get-tuple-element.96), channel_id=1, source_target_pairs={{8,0},{16,8},{24,16},{32,24},{40,32},{48,40},{56,48},{64,56},{72,6... | collective-permute-start | bytes 776 | tf_op jit(solution)/shard_map/ppermute | solution.py:38
  183.4 7.7 %collective-permute-start.16 = (f32[64,1]{1,0:T(8,128)}, f32[64,1]{1,0:T(8,128)}, u32[]{:S(2)}, u32[]{:S(2)}) collective-permute-start(f32[64,1]{1,0:T(8,128)} %get-tuple-element.97), channel_id=1, source_target_pairs={{0,8},{8,16},{16,24},{24,32},{32,40},{40,48},{48,56},{56,64},{64,7... | collective-permute-start | bytes 776 | tf_op jit(solution)/shard_map/ppermute | solution.py:39
  184.7 9.7 %collective-permute-start.18 = (f32[1,128]{1,0:T(1,128)}, f32[1,128]{1,0:T(1,128)}, u32[]{:S(2)}, u32[]{:S(2)}) collective-permute-start(f32[1,128]{1,0:T(1,128)} %get-tuple-element.100), channel_id=1, source_target_pairs={{1,0},{2,1},{3,2},{4,3},{5,4},{6,5},{7,6},{9,8},{10,9},{11,10},{12... | collective-permute-start | bytes 1544 | tf_op jit(solution)/shard_map/ppermute | solution.py:40
  199.2 8.5 %copy-start.25 = (f32[32,1,128]{2,1,0:T(1,128)S(1)}, f32[32,1,128]{2,1,0:T(1,128)}, u32[]{:S(2)}) copy-start(f32[32,1,128]{2,1,0:T(1,128)} %copy-done.24) | copy-start | bytes 49156
  199.2 8.5 %copy-start.38 = (f32[32,1,128]{2,1,0:T(1,128)S(1)}, f32[32,1,128]{2,1,0:T(1,128)}, u32[]{:S(2)}) copy-start(f32[32,1,128]{2,1,0:T(1,128)} %get-tuple-element.68) | copy-start | bytes 49156
  199.2 8.5 %copy-start.39 = (f32[32,1,128]{2,1,0:T(1,128)S(1)}, f32[32,1,128]{2,1,0:T(1,128)}, u32[]{:S(2)}) copy-start(f32[32,1,128]{2,1,0:T(1,128)} %get-tuple-element.72) | copy-start | bytes 49156
  199.2 18.0 %all-to-all-start.2 = ((f32[128,1,1]{2,1,0:T(1,128)}), f32[128,1,1]{2,1,0:T(1,128)}, u32[]{:S(2)}, u32[]{:S(2)}) async-start(f32[128,1,1]{2,1,0:T(1,128)} %broadcast_in_dim.41), calls=%async_computation.2 | async-start | bytes 131072 | tf_op jit(solution)/shard_map/all_to_all | solution.py:21
  213.7 50.1 %copy-start.3 = (f32[32,63,128]{2,1,0:T(8,128)S(1)}, f32[32,63,128]{2,1,0:T(8,128)}, u32[]{:S(2)}) copy-start(f32[32,63,128]{2,1,0:T(8,128)} %get-tuple-element.143) | copy-start | bytes 3096580
  224.1 20.1 %all-to-all-start.3 = ((f32[128,1,1]{2,1,0:T(1,128)}), f32[128,1,1]{2,1,0:T(1,128)}, u32[]{:S(2)}, u32[]{:S(2)}) async-start(f32[128,1,1]{2,1,0:T(1,128)} %broadcast_in_dim.42), calls=%async_computation.3 | async-start | bytes 131072 | tf_op jit(solution)/shard_map/all_to_all | solution.py:21
  231.5 20.3 %collective-permute-start.22 = (f32[1,128]{1,0:T(1,128)}, f32[1,128]{1,0:T(1,128)}, u32[]{:S(2)}, u32[]{:S(2)}) collective-permute-start(f32[1,128]{1,0:T(1,128)} %get-tuple-element.93), channel_id=1, source_target_pairs={{0,120},{8,112},{16,104},{24,96},{32,88},{40,80},{48,72},{56,64},{... | collective-permute-start | bytes 1544 | tf_op jit(solution)/shard_map/ppermute | solution.py:42
  237.6 13.6 %collective-permute-start.24 = (f32[1,128]{1,0:T(1,128)}, f32[1,128]{1,0:T(1,128)}, u32[]{:S(2)}, u32[]{:S(2)}) collective-permute-start(f32[1,128]{1,0:T(1,128)} %get-tuple-element.93), channel_id=1, source_target_pairs={{0,1},{1,2},{2,3},{3,4},{4,5},{5,6},{6,7},{8,9},{9,10},{10,11},{11... | collective-permute-start | bytes 1544 | tf_op jit(solution)/shard_map/ppermute | solution.py:41
  241.2 7.2 %collective-permute-start.20 = (f32[64,1]{1,0:T(8,128)}, f32[64,1]{1,0:T(8,128)}, u32[]{:S(2)}, u32[]{:S(2)}) collective-permute-start(f32[64,1]{1,0:T(8,128)} %get-tuple-element.88), channel_id=1, source_target_pairs={{8,0},{16,8},{24,16},{32,24},{40,32},{48,40},{56,48},{64,56},{72,6... | collective-permute-start | bytes 776 | tf_op jit(solution)/shard_map/ppermute | solution.py:38
  241.6 8.2 %collective-permute-start.21 = (f32[64,1]{1,0:T(8,128)}, f32[64,1]{1,0:T(8,128)}, u32[]{:S(2)}, u32[]{:S(2)}) collective-permute-start(f32[64,1]{1,0:T(8,128)} %get-tuple-element.89), channel_id=1, source_target_pairs={{0,8},{8,16},{16,24},{24,32},{32,40},{40,48},{48,56},{56,64},{64,7... | collective-permute-start | bytes 776 | tf_op jit(solution)/shard_map/ppermute | solution.py:39
  242.9 9.6 %collective-permute-start.23 = (f32[1,128]{1,0:T(1,128)}, f32[1,128]{1,0:T(1,128)}, u32[]{:S(2)}, u32[]{:S(2)}) collective-permute-start(f32[1,128]{1,0:T(1,128)} %get-tuple-element.92), channel_id=1, source_target_pairs={{1,0},{2,1},{3,2},{4,3},{5,4},{6,5},{7,6},{9,8},{10,9},{11,10},{12... | collective-permute-start | bytes 1544 | tf_op jit(solution)/shard_map/ppermute | solution.py:40
  256.0 7.9 %copy-start.26 = (f32[32,1,128]{2,1,0:T(1,128)S(1)}, f32[32,1,128]{2,1,0:T(1,128)}, u32[]{:S(2)}) copy-start(f32[32,1,128]{2,1,0:T(1,128)} %copy-done.24) | copy-start | bytes 49156
  256.0 7.9 %copy-start.36 = (f32[32,1,128]{2,1,0:T(1,128)S(1)}, f32[32,1,128]{2,1,0:T(1,128)}, u32[]{:S(2)}) copy-start(f32[32,1,128]{2,1,0:T(1,128)} %get-tuple-element.70) | copy-start | bytes 49156
  256.0 7.9 %copy-start.37 = (f32[32,1,128]{2,1,0:T(1,128)S(1)}, f32[32,1,128]{2,1,0:T(1,128)}, u32[]{:S(2)}) copy-start(f32[32,1,128]{2,1,0:T(1,128)} %get-tuple-element.74) | copy-start | bytes 49156
  256.0 17.5 %all-to-all-start.4 = ((f32[128,1,1]{2,1,0:T(1,128)}), f32[128,1,1]{2,1,0:T(1,128)S(1)}, u32[]{:S(2)}, u32[]{:S(2)}) async-start(f32[128,1,1]{2,1,0:T(1,128)} %broadcast_in_dim.43), calls=%async_computation.4 | async-start | bytes 131072 | tf_op jit(solution)/shard_map/all_to_all | solution.py:21
  (37 other events, 61.0 us)
where the time goes:
time: 280 us; the launch traced here: 277 us
  starting transfers between devices  110 us (39%)
  local copies, waits for them, and re-layouts  86.4 us (31%)
  other arithmetic  62.2 us (22%)
  waiting for transfers between devices  10.8 us (4%)
  between operations  7.66 us (3%)
    all_to_all x5, starting transfers between devices, allsum(): gathered = lax.all_to_all(spread, ('lon', 'lat'), 0, 0, tiled=True)  48.2 us
    slice x21, local copies, waits for them, and re-layouts, edge(): return jnp.concatenate([item[index] for item in cells], axis=0)  23.6 us
    ppermute x5, starting transfers between devices, halos(): lax.ppermute(last_row, 'lon', [(i, lon_count - 1 - i) for i in range(lon_...  22.9 us
    ppermute x5, starting transfers between devices, halos(): lax.ppermute(last_row, 'lat', [(i, i + 1) for i in range(lat_count - 1)])  19.5 us
    slice x12, local copies, waits for them, and re-layouts, part(): return tuple((item[first:first + count] for item in halo_all))  17.5 us
    mul x2, other arithmetic, local(): marine_snapshot * (tracer + time_step * (-flux + diffusivity * laplace(tr...  11.7 us
    unnamed x118, local copies, waits for them, and re-layouts  10.6 us
    slice x7, local copies, waits for them, and re-layouts, around(): cells[..., :, 1:]  9.74 us
  transfers between devices with their start and end apart: 30, of which 4 were waited for; matrix products, arithmetic and copies ran while one was open for 33% of the time, Pallas kernels for 0%

commit v1 on v0

--- a/solution.py
+++ b/solution.py
@@ -162,8 +162,7 @@
     residual = rhs
     precond = residual / diag
     direction = precond
-    halo_d = halos(direction, unit)
-    image = apply(direction, halo_d)
+    image = apply(direction, halos(direction, unit))
     pair = allsum(jnp.stack([jnp.sum(residual * precond), jnp.sum(direction * image)]))
     product_now = pair[0]
     curvature = pair[1]
@@ -173,14 +172,23 @@
         residual = residual - alpha * image
         if step + 1 < ITERS:
             precond = residual / diag
-            halo_z = halos(precond, unit)
-            product_next = allsum(jnp.sum(residual * precond))
+            image_z = apply(precond, halos(precond, unit))
+            sums = allsum(
+                jnp.stack(
+                    [
+                        jnp.sum(residual * precond),
+                        jnp.sum(precond * image_z),
+                        jnp.sum(precond * image),
+                        jnp.sum(direction * image_z),
+                    ]
+                )
+            )
+            product_next = sums[0]
             beta = product_next / product_now
+            curvature = sums[1] + beta * (sums[2] + sums[3]) + beta * beta * curvature
             direction = precond + beta * direction
-            halo_d = tuple(hz + beta * hd for hz, hd in zip(halo_z, halo_d))
+            image = image_z + beta * image
             product_now = product_next
-            image = apply(direction, halo_d)
-            curvature = allsum(jnp.sum(direction * image))
     return (zonal_next, merid_next, tracers[0], tracers[1], solution, residual)
 
 

time: 280 us -> 259 us (0.925)
  starting transfers between devices: 110 us -> 97.2 us
  other arithmetic: 62.2 us -> 54.7 us
  local copies, waits for them, and re-layouts: 86.4 us -> 81.7 us
  between operations: 7.66 us -> 11 us
    all_to_all x5 -> x3, starting transfers between devices: 48.2 us -> 38 us  [allsum(): gathered = lax.all_to_all(spread, ('lon', 'lat'), 0, 0, tiled=True)]
    add x10 -> x0, other arithmetic: 7.48 us -> none  [the longest x8 7.46 us: local(): halo_d = tuple((hz + beta * hd for hz, hd in zip(halo_z, halo_d)))]
    reduce_sum x4 -> x0, other arithmetic: 6.9 us -> none  [the longest x2 3.68 us: local(): curvature = allsum(jnp.sum(direction * image))]
    another operation x0 -> x2, other arithmetic: none -> 5.15 us  [local(): jnp.stack([jnp.sum(residual * precond), jnp.sum(precond * image_z), jnp.s...]
    reduce_sum x5 -> x3, other arithmetic: 6.51 us -> 2.14 us  [allsum(): return jnp.sum(gathered, axis=0)]
    broadcast_in_dim x5 -> x3, local copies, waits for them, and re-layouts: 5.87 us -> 1.99 us  [allsum(): spread = jnp.broadcast_to(value, (count,) + jnp.shape(value))]
    ppermute x5, starting transfers between devices: 22.9 us -> 19.5 us  [halos(): lax.ppermute(last_row, 'lon', [(i, lon_count - 1 - i) for i in range(lon_...]
    reduce_sum x1 -> x3, other arithmetic: 2.13 us -> 5.35 us  [local(): jnp.sum(residual * precond)]
  transfers between devices with their start and end apart: 30 -> 28, of which waited for: 4 -> 5; matrix products, arithmetic and copies ran while one was open for 33% -> 32% of each run, Pallas kernels for 0% -> 0%
where the time goes in v1:
time: 259 us; the launch traced here: 257 us
  starting transfers between devices  97.2 us (38%)
  local copies, waits for them, and re-layouts  81.7 us (32%)
  other arithmetic  54.7 us (21%)
  waiting for transfers between devices  12.5 us (5%)
  between operations  11 us (4%)
    all_to_all x3, starting transfers between devices, allsum(): gathered = lax.all_to_all(spread, ('lon', 'lat'), 0, 0, tiled=True)  38 us
    slice x21, local copies, waits for them, and re-layouts, edge(): return jnp.concatenate([item[index] for item in cells], axis=0)  23.5 us
    ppermute x5, starting transfers between devices, halos(): lax.ppermute(last_row, 'lat', [(i, i + 1) for i in range(lat_count - 1)])  20.7 us
    ppermute x5, starting transfers between devices, halos(): lax.ppermute(last_row, 'lon', [(i, lon_count - 1 - i) for i in range(lon_...  19.5 us
    slice x12, local copies, waits for them, and re-layouts, part(): return tuple((item[first:first + count] for item in halo_all))  16.8 us
    mul x2, other arithmetic, local(): marine_snapshot * (tracer + time_step * (-flux + diffusivity * laplace(tr...  11.7 us
    unnamed x92, local copies, waits for them, and re-layouts  9.2 us
    ppermute x5, starting transfers between devices, halos(): lax.ppermute(first_col, 'lon', [((i + 1) % lon_count, i) for i in range(l...  8.88 us
  transfers between devices with their start and end apart: 28, of which 5 were waited for; matrix products, arithmetic and copies ran while one was open for 32% of the time, Pallas kernels for 0%

profile of v1, /device:TPU:1, one launch (start us, length us, event | category | flops | bytes accessed | tf_op | source)
XLA Modules:
  0.0 257.1 jit_solution(4867552204335880727)
XLA Ops:
  1.4 3.8 %broadcast_multiply_fusion.1 = (f32[32,64,128]{2,1,0:T(8,128)S(1)}, f32[32,64,128]{2,1,0:T(8,128)S(1)}, f32[32,64,128]{2,1,0:T(8,128)}, f32[32,64,128]{2,1,0:T(8,128)S(1)}) fusion(f32[32,64,128]{2,1,0:T(8,128)} %param.11, f32[64,128]{1,0:T(8,128)S(1)} %convert_element_type.17, f32[32,64,128]{2,1,0:T(8,128)} %param.10, f32[32,64,128]{2,1,0:T(8,128)} %param.9, ...), kind=kLoop, calls=%fused_computation.44 | loop fusion | flops 1048576 | bytes 8421376 | tf_op jit(solution)/shard_map/mul | solution.py:77
  10.4 7.8 %collective-permute-start.2 = (f32[129,1,128]{2,1,0:T(1,128)}, f32[129,1,128]{2,1,0:T(1,128)}, u32[]{:S(2)}, u32[]{:S(2)}) collective-permute-start(f32[129,1,128]{2,1,0:T(1,128)} %get-tuple-element.129), channel_id=1, source_target_pairs={{0,120},{8,112},{16,104},{24,96},{32,88},{40,80},{48,72},{56,64},{... | collective-permute-start | bytes 198152 | tf_op jit(solution)/shard_map/ppermute | solution.py:42
  18.1 3.1 %collective-permute-start.4 = (f32[129,1,128]{2,1,0:T(1,128)}, f32[129,1,128]{2,1,0:T(1,128)S(1)}, u32[]{:S(2)}, u32[]{:S(2)}) collective-permute-start(f32[129,1,128]{2,1,0:T(1,128)} %get-tuple-element.129), channel_id=1, source_target_pairs={{0,1},{1,2},{2,3},{3,4},{4,5},{5,6},{6,7},{8,9},{9,10},{10,11},{11... | collective-permute-start | bytes 198152 | tf_op jit(solution)/shard_map/ppermute | solution.py:41
  22.6 2.7 %fusion.100 = (f32[32,64,1]{2,1,0:T(8,128)}, f32[32,64,1]{2,1,0:T(8,128)}, f32[32,64,1]{2,1,0:T(8,128)}, f32[32,64,1]{2,1,0:T(8,128)}) fusion(f32[32,64,128]{2,1,0:T(8,128)S(1)} %get-tuple-element.130, f32[32,64,128]{2,1,0:T(8,128)S(1)} %get-tuple-element.131), kind=kLoop, calls=%fused_computation.190 | loop fusion | bytes 65536 | tf_op jit(solution)/shard_map/slice | solution.py:32
  25.2 2.7 %fusion.102 = (f32[32,64,1]{2,1,0:T(8,128)}, f32[32,64,1]{2,1,0:T(8,128)}, f32[32,64,1]{2,1,0:T(8,128)}, f32[32,64,1]{2,1,0:T(8,128)}) fusion(f32[32,64,128]{2,1,0:T(8,128)S(1)} %copy-done, f32[32,64,128]{2,1,0:T(8,128)S(1)} %get-tuple-element.133), kind=kLoop, calls=%fused_computation.192 | loop fusion | bytes 65536 | tf_op jit(solution)/shard_map/slice | solution.py:32
  28.0 1.8 copy.117
  29.8 1.8 copy.118
  31.6 1.8 copy.115
  33.3 1.8 copy.116
  35.9 1.8 copy.125
  37.7 1.8 copy.126
  39.5 1.8 copy.123
  41.2 1.8 copy.124
  48.2 2.1 fusion.95
  50.3 2.7 %fusion.98 = (f32[32,64,127]{2,1,0:T(8,128)}, f32[32,64,127]{2,1,0:T(8,128)}, f32[32,64,127]{2,1,0:T(8,128)}, f32[32,64,127]{2,1,0:T(8,128)}) fusion(f32[32,64,128]{2,1,0:T(8,128)S(1)} %fusion.19, f32[32,64,128]{2,1,0:T(8,128)S(1)} %get-tuple-element.133), kind=kLoop, calls=%fused_computation.188 | loop fusion | bytes 8323072 | tf_op jit(solution)/shard_map/slice | solution.py:51
  55.8 2.8 %fusion.91 = (f32[32,64,127]{2,1,0:T(8,128)}, f32[32,64,127]{2,1,0:T(8,128)}, f32[32,64,127]{2,1,0:T(8,128)}, f32[32,64,127]{2,1,0:T(8,128)}) fusion(f32[32,64,128]{2,1,0:T(8,128)S(1)} %get-tuple-element.130, f32[32,64,128]{2,1,0:T(8,128)S(1)} %get-tuple-element.131), kind=kLoop, calls=%fused_computation.181 | loop fusion | bytes 8323072 | tf_op jit(solution)/shard_map/slice | solution.py:51
  68.5 1.8 copy.133
  70.4 1.9 copy.134
  72.2 1.8 copy.131
  74.1 1.8 copy.132
  80.6 6.0 %fusion.88 = (f32[64,128]{1,0:T(8,128)S(1)}, f32[32,64,128]{2,1,0:T(8,128)}) fusion(f32[32,63,128]{2,1,0:T(8,128)S(1)} %copy-done.2, f32[32,1,128]{2,1,0:T(1,128)S(1)} %get-tuple-element.77, f32[32,1,128]{2,1,0:T(1,128)S(1)} %get-tuple-element.73, f32[32,63,128]{2,1,0:T(8,128)} %get-tuple-element.155, f32[32,64,127]{2,1,0:T(8,128)} %get-tuple-element.47, ...), kind=kLoop, calls=%fused_computation.179 | loop fusion | flops 6021120 | bytes 9502976 | tf_op jit(solution)/shard_map/reduce_sum | solution.py:136
  88.0 3.8 %fusion.86 = (f32[64,128]{1,0:T(8,128)S(1)}, f32[32,64,128]{2,1,0:T(8,128)}) fusion(f32[32,63,128]{2,1,0:T(8,128)S(1)} %copy-done.13, f32[32,1,128]{2,1,0:T(1,128)S(1)} %get-tuple-element.79, f32[32,1,128]{2,1,0:T(1,128)S(1)} %get-tuple-element.75, f32[32,63,128]{2,1,0:T(8,128)S(1)} %copy-done.12, f32[32,64,127]{2,1,0:T(8,128)S(1)} %copy-done.6, ...), kind=kLoop, calls=%fused_computation.178 | loop fusion | flops 6021120 | bytes 9502976 | tf_op jit(solution)/shard_map/reduce_sum | solution.py:135
  93.4 4.0 %collective-permute-start.9 = (f32[2,1,128]{2,1,0:T(1,128)S(1)}, f32[2,1,128]{2,1,0:T(1,128)S(1)}, u32[]{:S(2)}, u32[]{:S(2)}) collective-permute-start(f32[2,1,128]{2,1,0:T(1,128)S(1)} %pad_maximum_fusion.19), channel_id=1, source_target_pairs={{0,1},{1,2},{2,3},{3,4},{4,5},{5,6},{6,7},{8,9},{9,10},{10,11},{11... | collective-permute-start | bytes 3080 | tf_op jit(solution)/shard_map/ppermute | solution.py:41
  98.0 4.3 %collective-permute-start.5 = (f32[2,64,1]{2,1,0:T(8,128)}, f32[2,64,1]{2,1,0:T(8,128)S(1)}, u32[]{:S(2)}, u32[]{:S(2)}) collective-permute-start(f32[2,64,1]{2,1,0:T(8,128)} %pad_maximum_fusion.12), channel_id=1, source_target_pairs={{8,0},{16,8},{24,16},{32,24},{40,32},{48,40},{56,48},{64,56},{72,6... | collective-permute-start | bytes 1544 | tf_op jit(solution)/shard_map/ppermute | solution.py:38
  104.3 2.9 %collective-permute-done.8 = f32[2,1,128]{2,1,0:T(1,128)S(1)} collective-permute-done((f32[2,1,128]{2,1,0:T(1,128)S(1)}, f32[2,1,128]{2,1,0:T(1,128)S(1)}, u32[]{:S(2)}, u32[]{:S(2)}) %collective-permute-start.8) | collective-permute-done | bytes 1056 | tf_op jit(solution)/shard_map/ppermute | solution.py:40
  107.8 1.7 fusion.80
  110.8 3.0 %collective-permute-start.12 = (f32[1,128]{1,0:T(1,128)}, f32[1,128]{1,0:T(1,128)}, u32[]{:S(2)}, u32[]{:S(2)}) collective-permute-start(f32[1,128]{1,0:T(1,128)} %get-tuple-element.113), channel_id=1, source_target_pairs={{0,120},{8,112},{16,104},{24,96},{32,88},{40,80},{48,72},{56,64},{... | collective-permute-start | bytes 1544 | tf_op jit(solution)/shard_map/ppermute | solution.py:42
  115.7 4.5 %collective-permute-start.14 = (f32[1,128]{1,0:T(1,128)}, f32[1,128]{1,0:T(1,128)}, u32[]{:S(2)}, u32[]{:S(2)}) collective-permute-start(f32[1,128]{1,0:T(1,128)} %get-tuple-element.113), channel_id=1, source_target_pairs={{0,1},{1,2},{2,3},{3,4},{4,5},{5,6},{6,7},{8,9},{9,10},{10,11},{11... | collective-permute-start | bytes 1544 | tf_op jit(solution)/shard_map/ppermute | solution.py:41
  120.2 3.1 %collective-permute-start.10 = (f32[64,1]{1,0:T(8,128)}, f32[64,1]{1,0:T(8,128)}, u32[]{:S(2)}, u32[]{:S(2)}) collective-permute-start(f32[64,1]{1,0:T(8,128)} %get-tuple-element.108), channel_id=1, source_target_pairs={{8,0},{16,8},{24,16},{32,24},{40,32},{48,40},{56,48},{64,56},{72,6... | collective-permute-start | bytes 776 | tf_op jit(solution)/shard_map/ppermute | solution.py:38
  129.8 16.0 %all-to-all-start = ((f32[128,1,2]{2,1,0:T(1,128)}), f32[128,1,2]{2,1,0:T(1,128)}, u32[]{:S(2)}, u32[]{:S(2)}) async-start(f32[128,1,2]{2,1,0:T(1,128)} %broadcast_in_dim.15), calls=%async_computation | async-start | bytes 131072 | tf_op jit(solution)/shard_map/all_to_all | solution.py:21
  145.8 2.1 fusion.92
  147.9 1.8 copy.137
  149.7 1.8 copy.138
  151.5 1.9 copy.135
  153.4 1.8 copy.136
  160.0 6.0 %collective-permute-start.17 = (f32[1,128]{1,0:T(1,128)}, f32[1,128]{1,0:T(1,128)}, u32[]{:S(2)}, u32[]{:S(2)}) collective-permute-start(f32[1,128]{1,0:T(1,128)} %get-tuple-element.105), channel_id=1, source_target_pairs={{0,120},{8,112},{16,104},{24,96},{32,88},{40,80},{48,72},{56,64},{... | collective-permute-start | bytes 1544 | tf_op jit(solution)/shard_map/ppermute | solution.py:42
  168.1 4.6 %collective-permute-start.19 = (f32[1,128]{1,0:T(1,128)}, f32[1,128]{1,0:T(1,128)}, u32[]{:S(2)}, u32[]{:S(2)}) collective-permute-start(f32[1,128]{1,0:T(1,128)} %get-tuple-element.105), channel_id=1, source_target_pairs={{0,1},{1,2},{2,3},{3,4},{4,5},{5,6},{6,7},{8,9},{9,10},{10,11},{11... | collective-permute-start | bytes 1544 | tf_op jit(solution)/shard_map/ppermute | solution.py:41
  176.3 2.2 multiply_reduce_fusion.7
  178.5 2.6 pad_maximum_fusion.22
  181.7 11.5 %all-to-all-start.1 = ((f32[128,1,4]{2,1,0:T(1,128)}), f32[128,1,4]{2,1,0:T(1,128)}, u32[]{:S(2)}, u32[]{:S(2)}) async-start(f32[128,1,4]{2,1,0:T(1,128)} %broadcast_in_dim.16), calls=%async_computation.1 | async-start | bytes 131072 | tf_op jit(solution)/shard_map/all_to_all | solution.py:21
  193.3 6.0 %add_multiply_fusion = f32[32,64,128]{2,1,0:T(8,128)} fusion(f32[32,64,128]{2,1,0:T(8,128)S(1)} %get-tuple-element.130, f32[32,63,128]{2,1,0:T(8,128)} %get-tuple-element.39, f32[32,1,128]{2,1,0:T(1,128)} %get-tuple-element.76, f32[32,1,128]{2,1,0:T(1,128)S(1)} %copy-done.34, f32[32,63,128]{2,1,0:T(8,128)} %get-tuple-element.38, ...), kind=kLoop, calls=%fused_computation.35 | loop fusion | flops 7077888 | bytes 10518528 | tf_op jit(solution)/shard_map/mul | solution.py:133
  199.3 3.5 %all-to-all-done.1 = f32[128,1,4]{2,1,0:T(1,128)} async-done(((f32[128,1,4]{2,1,0:T(1,128)}), f32[128,1,4]{2,1,0:T(1,128)}, u32[]{:S(2)}, u32[]{:S(2)}) %all-to-all-start.1) | async-done | bytes 2080 | tf_op jit(solution)/shard_map/all_to_all | solution.py:21
  212.3 2.6 %collective-permute-start.22 = (f32[1,128]{1,0:T(1,128)}, f32[1,128]{1,0:T(1,128)}, u32[]{:S(2)}, u32[]{:S(2)}) collective-permute-start(f32[1,128]{1,0:T(1,128)} %get-tuple-element.97), channel_id=1, source_target_pairs={{0,120},{8,112},{16,104},{24,96},{32,88},{40,80},{48,72},{56,64},{... | collective-permute-start | bytes 1544 | tf_op jit(solution)/shard_map/ppermute | solution.py:42
  216.9 4.5 %collective-permute-start.24 = (f32[1,128]{1,0:T(1,128)}, f32[1,128]{1,0:T(1,128)}, u32[]{:S(2)}, u32[]{:S(2)}) collective-permute-start(f32[1,128]{1,0:T(1,128)} %get-tuple-element.97), channel_id=1, source_target_pairs={{0,1},{1,2},{2,3},{3,4},{4,5},{5,6},{6,7},{8,9},{9,10},{10,11},{11... | collective-permute-start | bytes 1544 | tf_op jit(solution)/shard_map/ppermute | solution.py:41
  227.7 2.6 %pad_maximum_fusion.23 = f32[4]{0:T(128)S(1)} fusion(f32[1]{0:T(128)} %bitcast.25, f32[1]{0:T(128)} %bitcast.24, f32[1]{0:T(128)} %bitcast.23, f32[1]{0:T(128)} %bitcast.22), kind=kLoop, calls=%fused_computation.162 | loop fusion | flops 12 | bytes 32 | tf_op jit(solution)/shard_map/stack | solution.py:177
  231.0 10.4 %all-to-all-start.2 = ((f32[128,1,4]{2,1,0:T(1,128)}), f32[128,1,4]{2,1,0:T(1,128)S(1)}, u32[]{:S(2)}, u32[]{:S(2)}) async-start(f32[128,1,4]{2,1,0:T(1,128)} %broadcast_in_dim.17), calls=%async_computation.2 | async-start | bytes 131072 | tf_op jit(solution)/shard_map/all_to_all | solution.py:21
  241.4 5.7 %add_multiply_fusion.1 = f32[32,64,128]{2,1,0:T(8,128)} fusion(f32[32,64,128]{2,1,0:T(8,128)S(1)} %get-tuple-element.131, f32[32,63,128]{2,1,0:T(8,128)} %get-tuple-element.146, f32[32,1,128]{2,1,0:T(1,128)S(1)} %copy-done.33, f32[32,1,128]{2,1,0:T(1,128)S(1)} %copy-done.32, f32[32,63,128]{2,1,0:T(8,128)} %get-tuple-element.147, ...), kind=kLoop, calls=%fused_computation.36 | loop fusion | flops 7077888 | bytes 10518528 | tf_op jit(solution)/shard_map/mul | solution.py:133
  247.1 3.9 %all-to-all-done.2 = f32[128,1,4]{2,1,0:T(1,128)S(1)} async-done(((f32[128,1,4]{2,1,0:T(1,128)}), f32[128,1,4]{2,1,0:T(1,128)S(1)}, u32[]{:S(2)}, u32[]{:S(2)}) %all-to-all-start.2) | async-done | bytes 2080 | tf_op jit(solution)/shard_map/all_to_all | solution.py:21
  (216 shorter events, 72.1 us)
Async XLA Ops:
  10.4 65.5 %collective-permute-start.2 = (f32[129,1,128]{2,1,0:T(1,128)}, f32[129,1,128]{2,1,0:T(1,128)}, u32[]{:S(2)}, u32[]{:S(2)}) collective-permute-start(f32[129,1,128]{2,1,0:T(1,128)} %get-tuple-element.129), channel_id=1, source_target_pairs={{0,120},{8,112},{16,104},{24,96},{32,88},{40,80},{48,72},{56,64},{... | collective-permute-start | bytes 198152 | tf_op jit(solution)/shard_map/ppermute | solution.py:42
  18.1 61.0 %collective-permute-start.4 = (f32[129,1,128]{2,1,0:T(1,128)}, f32[129,1,128]{2,1,0:T(1,128)S(1)}, u32[]{:S(2)}, u32[]{:S(2)}) collective-permute-start(f32[129,1,128]{2,1,0:T(1,128)} %get-tuple-element.129), channel_id=1, source_target_pairs={{0,1},{1,2},{2,3},{3,4},{4,5},{5,6},{6,7},{8,9},{9,10},{10,11},{11... | collective-permute-start | bytes 198152 | tf_op jit(solution)/shard_map/ppermute | solution.py:41
  21.3 56.2 %collective-permute-start.3 = (f32[129,1,128]{2,1,0:T(1,128)}, f32[129,1,128]{2,1,0:T(1,128)}, u32[]{:S(2)}, u32[]{:S(2)}) collective-permute-start(f32[129,1,128]{2,1,0:T(1,128)} %get-tuple-element.128), channel_id=1, source_target_pairs={{1,0},{2,1},{3,2},{4,3},{5,4},{6,5},{7,6},{9,8},{10,9},{11,10},{12... | collective-permute-start | bytes 198152 | tf_op jit(solution)/shard_map/ppermute | solution.py:40
  35.8 23.9 %collective-permute-start = (f32[129,64,1]{0,1,2:T(8,128)}, f32[129,64,1]{0,1,2:T(8,128)S(1)}, u32[]{:S(2)}, u32[]{:S(2)}) collective-permute-start(f32[129,64,1]{0,1,2:T(8,128)} %concatenate.144), channel_id=1, source_target_pairs={{8,0},{16,8},{24,16},{32,24},{40,32},{48,40},{56,48},{64,56},{72,6... | collective-permute-start | bytes 99080 | tf_op jit(solution)/shard_map/ppermute | solution.py:38
  43.7 19.5 %collective-permute-start.1 = (f32[129,64,1]{0,1,2:T(8,128)}, f32[129,64,1]{0,1,2:T(8,128)S(1)}, u32[]{:S(2)}, u32[]{:S(2)}) collective-permute-start(f32[129,64,1]{0,1,2:T(8,128)} %concatenate.146), channel_id=1, source_target_pairs={{0,8},{8,16},{16,24},{24,32},{32,40},{40,48},{48,56},{56,64},{64,7... | collective-permute-start | bytes 99080 | tf_op jit(solution)/shard_map/ppermute | solution.py:39
  74.0 6.4 %copy-start.2 = (f32[32,63,128]{2,1,0:T(8,128)S(1)}, f32[32,63,128]{2,1,0:T(8,128)}, u32[]{:S(2)}) copy-start(f32[32,63,128]{2,1,0:T(8,128)} %get-tuple-element.154) | copy-start | bytes 3096580
  80.5 6.2 %copy-start.4 = (f32[32,64,1]{2,1,0:T(8,128)S(1)}, f32[32,64,1]{2,1,0:T(8,128)}, u32[]{:S(2)}) copy-start(f32[32,64,1]{2,1,0:T(8,128)} %copy.131) | copy-start | bytes 24580
  80.5 6.2 %copy-start.5 = (f32[32,64,1]{2,1,0:T(8,128)S(1)}, f32[32,64,1]{2,1,0:T(8,128)}, u32[]{:S(2)}) copy-start(f32[32,64,1]{2,1,0:T(8,128)} %copy.132) | copy-start | bytes 24580
  80.5 6.2 %copy-start.6 = (f32[32,64,127]{2,1,0:T(8,128)S(1)}, f32[32,64,127]{2,1,0:T(8,128)}, u32[]{:S(2)}) copy-start(f32[32,64,127]{2,1,0:T(8,128)} %get-tuple-element.152) | copy-start | bytes 3121156
  80.5 6.2 %copy-start.7 = (f32[32,64,127]{2,1,0:T(8,128)S(1)}, f32[32,64,127]{2,1,0:T(8,128)}, u32[]{:S(2)}) copy-start(f32[32,64,127]{2,1,0:T(8,128)} %get-tuple-element.153) | copy-start | bytes 3121156
  80.5 6.2 %copy-start.8 = (f32[32,64,128]{2,1,0:T(8,128)S(1)}, f32[32,64,128]{2,1,0:T(8,128)}, u32[]{:S(2)}) copy-start(f32[32,64,128]{2,1,0:T(8,128)} %param.9) | copy-start | bytes 3145732
  80.5 6.2 %copy-start.9 = (f32[32,64,128]{2,1,0:T(8,128)S(1)}, f32[32,64,128]{2,1,0:T(8,128)}, u32[]{:S(2)}) copy-start(f32[32,64,128]{2,1,0:T(8,128)} %param.8) | copy-start | bytes 3145732
  80.6 6.2 %copy-start.10 = (f32[32,64,1]{2,1,0:T(8,128)S(1)}, f32[32,64,1]{2,1,0:T(8,128)}, u32[]{:S(2)}) copy-start(f32[32,64,1]{2,1,0:T(8,128)} %fusion.130) | copy-start | bytes 24580
  80.6 6.4 %copy-start.11 = (f32[32,64,1]{2,1,0:T(8,128)S(1)}, f32[32,64,1]{2,1,0:T(8,128)}, u32[]{:S(2)}) copy-start(f32[32,64,1]{2,1,0:T(8,128)} %fusion.131) | copy-start | bytes 24580
  80.6 6.8 %copy-start.12 = (f32[32,63,128]{2,1,0:T(8,128)S(1)}, f32[32,63,128]{2,1,0:T(8,128)}, u32[]{:S(2)}) copy-start(f32[32,63,128]{2,1,0:T(8,128)} %get-tuple-element.62) | copy-start | bytes 3096580
  80.6 7.1 %copy-start.13 = (f32[32,63,128]{2,1,0:T(8,128)S(1)}, f32[32,63,128]{2,1,0:T(8,128)}, u32[]{:S(2)}) copy-start(f32[32,63,128]{2,1,0:T(8,128)} %get-tuple-element.63) | copy-start | bytes 3096580
  80.6 7.4 %copy-start.14 = (f32[32,64,127]{2,1,0:T(8,128)S(1)}, f32[32,64,127]{2,1,0:T(8,128)}, u32[]{:S(2)}) copy-start(f32[32,64,127]{2,1,0:T(8,128)} %get-tuple-element.50) | copy-start | bytes 3121156
  93.3 10.9 %collective-permute-start.7 = (f32[2,1,128]{2,1,0:T(1,128)S(1)}, f32[2,1,128]{2,1,0:T(1,128)S(1)}, u32[]{:S(2)}, u32[]{:S(2)}) collective-permute-start(f32[2,1,128]{2,1,0:T(1,128)S(1)} %pad_maximum_fusion.19), channel_id=1, source_target_pairs={{0,120},{8,112},{16,104},{24,96},{32,88},{40,80},{48,72},{56,64},{... | collective-permute-start | bytes 3080 | tf_op jit(solution)/shard_map/ppermute | solution.py:42
  93.4 13.9 %collective-permute-start.9 = (f32[2,1,128]{2,1,0:T(1,128)S(1)}, f32[2,1,128]{2,1,0:T(1,128)S(1)}, u32[]{:S(2)}, u32[]{:S(2)}) collective-permute-start(f32[2,1,128]{2,1,0:T(1,128)S(1)} %pad_maximum_fusion.19), channel_id=1, source_target_pairs={{0,1},{1,2},{2,3},{3,4},{4,5},{5,6},{6,7},{8,9},{9,10},{10,11},{11... | collective-permute-start | bytes 3080 | tf_op jit(solution)/shard_map/ppermute | solution.py:41
  98.0 9.2 %collective-permute-start.5 = (f32[2,64,1]{2,1,0:T(8,128)}, f32[2,64,1]{2,1,0:T(8,128)S(1)}, u32[]{:S(2)}, u32[]{:S(2)}) collective-permute-start(f32[2,64,1]{2,1,0:T(8,128)} %pad_maximum_fusion.12), channel_id=1, source_target_pairs={{8,0},{16,8},{24,16},{32,24},{40,32},{48,40},{56,48},{64,56},{72,6... | collective-permute-start | bytes 1544 | tf_op jit(solution)/shard_map/ppermute | solution.py:38
  102.9 4.3 %collective-permute-start.6 = (f32[2,64,1]{2,1,0:T(8,128)}, f32[2,64,1]{2,1,0:T(8,128)}, u32[]{:S(2)}, u32[]{:S(2)}) collective-permute-start(f32[2,64,1]{2,1,0:T(8,128)} %pad_maximum_fusion.13), channel_id=1, source_target_pairs={{0,8},{8,16},{16,24},{24,32},{32,40},{40,48},{48,56},{56,64},{64,7... | collective-permute-start | bytes 1544 | tf_op jit(solution)/shard_map/ppermute | solution.py:39
  102.9 4.3 %collective-permute-start.8 = (f32[2,1,128]{2,1,0:T(1,128)S(1)}, f32[2,1,128]{2,1,0:T(1,128)S(1)}, u32[]{:S(2)}, u32[]{:S(2)}) collective-permute-start(f32[2,1,128]{2,1,0:T(1,128)S(1)} %pad_maximum_fusion.20), channel_id=1, source_target_pairs={{1,0},{2,1},{3,2},{4,3},{5,4},{6,5},{7,6},{9,8},{10,9},{11,10},{12... | collective-permute-start | bytes 3080 | tf_op jit(solution)/shard_map/ppermute | solution.py:40
  110.8 12.6 %collective-permute-start.12 = (f32[1,128]{1,0:T(1,128)}, f32[1,128]{1,0:T(1,128)}, u32[]{:S(2)}, u32[]{:S(2)}) collective-permute-start(f32[1,128]{1,0:T(1,128)} %get-tuple-element.113), channel_id=1, source_target_pairs={{0,120},{8,112},{16,104},{24,96},{32,88},{40,80},{48,72},{56,64},{... | collective-permute-start | bytes 1544 | tf_op jit(solution)/shard_map/ppermute | solution.py:42
  113.8 10.7 %collective-permute-start.13 = (f32[1,128]{1,0:T(1,128)}, f32[1,128]{1,0:T(1,128)}, u32[]{:S(2)}, u32[]{:S(2)}) collective-permute-start(f32[1,128]{1,0:T(1,128)} %get-tuple-element.112), channel_id=1, source_target_pairs={{1,0},{2,1},{3,2},{4,3},{5,4},{6,5},{7,6},{9,8},{10,9},{11,10},{12... | collective-permute-start | bytes 1544 | tf_op jit(solution)/shard_map/ppermute | solution.py:40
  115.1 11.2 %copy-start.24 = (f32[64,128]{1,0:T(8,128)S(1)}, f32[64,128]{1,0:T(8,128)}, u32[]{:S(2)}) copy-start(f32[64,128]{1,0:T(8,128)} %get-tuple-element.24) | copy-start | bytes 98308
  115.7 10.6 %collective-permute-start.14 = (f32[1,128]{1,0:T(1,128)}, f32[1,128]{1,0:T(1,128)}, u32[]{:S(2)}, u32[]{:S(2)}) collective-permute-start(f32[1,128]{1,0:T(1,128)} %get-tuple-element.113), channel_id=1, source_target_pairs={{0,1},{1,2},{2,3},{3,4},{4,5},{5,6},{6,7},{8,9},{9,10},{10,11},{11... | collective-permute-start | bytes 1544 | tf_op jit(solution)/shard_map/ppermute | solution.py:41
  120.2 5.0 %collective-permute-start.10 = (f32[64,1]{1,0:T(8,128)}, f32[64,1]{1,0:T(8,128)}, u32[]{:S(2)}, u32[]{:S(2)}) collective-permute-start(f32[64,1]{1,0:T(8,128)} %get-tuple-element.108), channel_id=1, source_target_pairs={{8,0},{16,8},{24,16},{32,24},{40,32},{48,40},{56,48},{64,56},{72,6... | collective-permute-start | bytes 776 | tf_op jit(solution)/shard_map/ppermute | solution.py:38
  123.4 3.0 %collective-permute-start.11 = (f32[64,1]{1,0:T(8,128)S(1)}, f32[64,1]{1,0:T(8,128)}, u32[]{:S(2)}, u32[]{:S(2)}) collective-permute-start(f32[64,1]{1,0:T(8,128)S(1)} %get-tuple-element.109), channel_id=1, source_target_pairs={{0,8},{8,16},{16,24},{24,32},{32,40},{40,48},{48,56},{56,64},{64,7... | collective-permute-start | bytes 776 | tf_op jit(solution)/shard_map/ppermute | solution.py:39
  129.8 25.5 %all-to-all-start = ((f32[128,1,2]{2,1,0:T(1,128)}), f32[128,1,2]{2,1,0:T(1,128)}, u32[]{:S(2)}, u32[]{:S(2)}) async-start(f32[128,1,2]{2,1,0:T(1,128)} %broadcast_in_dim.15), calls=%async_computation | async-start | bytes 131072 | tf_op jit(solution)/shard_map/all_to_all | solution.py:21
  155.3 2.9 %copy-start.25 = (f32[64,128]{1,0:T(8,128)S(1)}, f32[64,128]{1,0:T(8,128)}, u32[]{:S(2)}) copy-start(f32[64,128]{1,0:T(8,128)} %get-tuple-element.24) | copy-start | bytes 98308
  160.0 14.3 %collective-permute-start.17 = (f32[1,128]{1,0:T(1,128)}, f32[1,128]{1,0:T(1,128)}, u32[]{:S(2)}, u32[]{:S(2)}) collective-permute-start(f32[1,128]{1,0:T(1,128)} %get-tuple-element.105), channel_id=1, source_target_pairs={{0,120},{8,112},{16,104},{24,96},{32,88},{40,80},{48,72},{56,64},{... | collective-permute-start | bytes 1544 | tf_op jit(solution)/shard_map/ppermute | solution.py:42
  166.1 9.6 %collective-permute-start.18 = (f32[1,128]{1,0:T(1,128)}, f32[1,128]{1,0:T(1,128)}, u32[]{:S(2)}, u32[]{:S(2)}) collective-permute-start(f32[1,128]{1,0:T(1,128)} %get-tuple-element.104), channel_id=1, source_target_pairs={{1,0},{2,1},{3,2},{4,3},{5,4},{6,5},{7,6},{9,8},{10,9},{11,10},{12... | collective-permute-start | bytes 1544 | tf_op jit(solution)/shard_map/ppermute | solution.py:40
  168.1 8.2 %collective-permute-start.19 = (f32[1,128]{1,0:T(1,128)}, f32[1,128]{1,0:T(1,128)}, u32[]{:S(2)}, u32[]{:S(2)}) collective-permute-start(f32[1,128]{1,0:T(1,128)} %get-tuple-element.105), channel_id=1, source_target_pairs={{0,1},{1,2},{2,3},{3,4},{4,5},{5,6},{6,7},{8,9},{9,10},{10,11},{11... | collective-permute-start | bytes 1544 | tf_op jit(solution)/shard_map/ppermute | solution.py:41
  172.6 3.7 %collective-permute-start.15 = (f32[64,1]{1,0:T(8,128)}, f32[64,1]{1,0:T(8,128)}, u32[]{:S(2)}, u32[]{:S(2)}) collective-permute-start(f32[64,1]{1,0:T(8,128)} %get-tuple-element.100), channel_id=1, source_target_pairs={{8,0},{16,8},{24,16},{32,24},{40,32},{48,40},{56,48},{64,56},{72,6... | collective-permute-start | bytes 776 | tf_op jit(solution)/shard_map/ppermute | solution.py:38
  173.3 3.0 %collective-permute-start.16 = (f32[64,1]{1,0:T(8,128)}, f32[64,1]{1,0:T(8,128)}, u32[]{:S(2)}, u32[]{:S(2)}) collective-permute-start(f32[64,1]{1,0:T(8,128)} %get-tuple-element.101), channel_id=1, source_target_pairs={{0,8},{8,16},{16,24},{24,32},{32,40},{40,48},{48,56},{56,64},{64,7... | collective-permute-start | bytes 776 | tf_op jit(solution)/shard_map/ppermute | solution.py:39
  181.7 11.6 %copy-start.27 = (f32[32,1,128]{2,1,0:T(1,128)S(1)}, f32[32,1,128]{2,1,0:T(1,128)}, u32[]{:S(2)}) copy-start(f32[32,1,128]{2,1,0:T(1,128)} %copy-done.26) | copy-start | bytes 49156
  181.7 11.6 %copy-start.34 = (f32[32,1,128]{2,1,0:T(1,128)S(1)}, f32[32,1,128]{2,1,0:T(1,128)}, u32[]{:S(2)}) copy-start(f32[32,1,128]{2,1,0:T(1,128)} %get-tuple-element.72) | copy-start | bytes 49156
  181.7 21.1 %all-to-all-start.1 = ((f32[128,1,4]{2,1,0:T(1,128)}), f32[128,1,4]{2,1,0:T(1,128)}, u32[]{:S(2)}, u32[]{:S(2)}) async-start(f32[128,1,4]{2,1,0:T(1,128)} %broadcast_in_dim.16), calls=%async_computation.1 | async-start | bytes 131072 | tf_op jit(solution)/shard_map/all_to_all | solution.py:21
  199.3 42.1 %copy-start.3 = (f32[32,63,128]{2,1,0:T(8,128)S(1)}, f32[32,63,128]{2,1,0:T(8,128)}, u32[]{:S(2)}) copy-start(f32[32,63,128]{2,1,0:T(8,128)} %get-tuple-element.155) | copy-start | bytes 3096580
  212.3 10.8 %collective-permute-start.22 = (f32[1,128]{1,0:T(1,128)}, f32[1,128]{1,0:T(1,128)}, u32[]{:S(2)}, u32[]{:S(2)}) collective-permute-start(f32[1,128]{1,0:T(1,128)} %get-tuple-element.97), channel_id=1, source_target_pairs={{0,120},{8,112},{16,104},{24,96},{32,88},{40,80},{48,72},{56,64},{... | collective-permute-start | bytes 1544 | tf_op jit(solution)/shard_map/ppermute | solution.py:42
  214.9 9.4 %collective-permute-start.23 = (f32[1,128]{1,0:T(1,128)}, f32[1,128]{1,0:T(1,128)}, u32[]{:S(2)}, u32[]{:S(2)}) collective-permute-start(f32[1,128]{1,0:T(1,128)} %get-tuple-element.96), channel_id=1, source_target_pairs={{1,0},{2,1},{3,2},{4,3},{5,4},{6,5},{7,6},{9,8},{10,9},{11,10},{12... | collective-permute-start | bytes 1544 | tf_op jit(solution)/shard_map/ppermute | solution.py:40
  216.9 9.2 %collective-permute-start.24 = (f32[1,128]{1,0:T(1,128)}, f32[1,128]{1,0:T(1,128)}, u32[]{:S(2)}, u32[]{:S(2)}) collective-permute-start(f32[1,128]{1,0:T(1,128)} %get-tuple-element.97), channel_id=1, source_target_pairs={{0,1},{1,2},{2,3},{3,4},{4,5},{5,6},{6,7},{8,9},{9,10},{10,11},{11... | collective-permute-start | bytes 1544 | tf_op jit(solution)/shard_map/ppermute | solution.py:41
  221.4 3.6 %collective-permute-start.20 = (f32[64,1]{1,0:T(8,128)}, f32[64,1]{1,0:T(8,128)S(1)}, u32[]{:S(2)}, u32[]{:S(2)}) collective-permute-start(f32[64,1]{1,0:T(8,128)} %get-tuple-element.92), channel_id=1, source_target_pairs={{8,0},{16,8},{24,16},{32,24},{40,32},{48,40},{56,48},{64,56},{72,6... | collective-permute-start | bytes 776 | tf_op jit(solution)/shard_map/ppermute | solution.py:38
  222.1 3.9 %collective-permute-start.21 = (f32[64,1]{1,0:T(8,128)}, f32[64,1]{1,0:T(8,128)}, u32[]{:S(2)}, u32[]{:S(2)}) collective-permute-start(f32[64,1]{1,0:T(8,128)} %get-tuple-element.93), channel_id=1, source_target_pairs={{0,8},{8,16},{16,24},{24,32},{32,40},{40,48},{48,56},{56,64},{64,7... | collective-permute-start | bytes 776 | tf_op jit(solution)/shard_map/ppermute | solution.py:39
  231.0 10.5 %copy-start.28 = (f32[32,1,128]{2,1,0:T(1,128)S(1)}, f32[32,1,128]{2,1,0:T(1,128)}, u32[]{:S(2)}) copy-start(f32[32,1,128]{2,1,0:T(1,128)} %copy-done.26) | copy-start | bytes 49156
  231.0 10.5 %copy-start.32 = (f32[32,1,128]{2,1,0:T(1,128)S(1)}, f32[32,1,128]{2,1,0:T(1,128)}, u32[]{:S(2)}) copy-start(f32[32,1,128]{2,1,0:T(1,128)} %get-tuple-element.74) | copy-start | bytes 49156
  231.0 10.5 %copy-start.33 = (f32[32,1,128]{2,1,0:T(1,128)S(1)}, f32[32,1,128]{2,1,0:T(1,128)}, u32[]{:S(2)}) copy-start(f32[32,1,128]{2,1,0:T(1,128)} %get-tuple-element.78) | copy-start | bytes 49156
  231.0 20.1 %all-to-all-start.2 = ((f32[128,1,4]{2,1,0:T(1,128)}), f32[128,1,4]{2,1,0:T(1,128)S(1)}, u32[]{:S(2)}, u32[]{:S(2)}) async-start(f32[128,1,4]{2,1,0:T(1,128)} %broadcast_in_dim.17), calls=%async_computation.2 | async-start | bytes 131072 | tf_op jit(solution)/shard_map/all_to_all | solution.py:21
  (22 other events, 26.4 us)

commit v2 on v1

--- a/solution.py
+++ b/solution.py
@@ -31,25 +31,30 @@
     def edge(index):
         return jnp.concatenate([item[index] for item in cells], axis=0)
 
-    first_col = edge((Ellipsis, slice(None), slice(0, 1)))
-    last_col = edge((Ellipsis, slice(None), slice(-1, None)))
+    first_col = edge((Ellipsis, slice(None), 0))
+    last_col = edge((Ellipsis, slice(None), -1))
     first_row = edge((Ellipsis, slice(0, 1), slice(None)))
     last_row = edge((Ellipsis, slice(-1, None), slice(None)))
     east = lax.ppermute(first_col, "lon", [((i + 1) % lon_count, i) for i in range(lon_count)])
     west = lax.ppermute(last_col, "lon", [(i, (i + 1) % lon_count) for i in range(lon_count)])
     north = lax.ppermute(first_row, "lat", [(i + 1, i) for i in range(lat_count - 1)])
     south = lax.ppermute(last_row, "lat", [(i, i + 1) for i in range(lat_count - 1)])
-    mirror = lax.ppermute(last_row, "lon", [(i, lon_count - 1 - i) for i in range(lon_count)])
+    top = lat_count - 1
+    mirror = lax.ppermute(
+        last_row,
+        ("lon", "lat"),
+        [(i * lat_count + top, (lon_count - 1 - i) * lat_count + top) for i in range(lon_count)],
+    )
     folded = parity * mirror[..., ::-1]
-    north = jnp.where(lax.axis_index("lat") == lat_count - 1, folded, north)
+    north = jnp.where(lax.axis_index("lat") == top, folded, north)
     return east, west, north, south
 
 
 def around(cells, halo):
     east, west, north, south = halo
     return (
-        jnp.concatenate([cells[..., :, 1:], east], axis=-1),
-        jnp.concatenate([west, cells[..., :, :-1]], axis=-1),
+        jnp.concatenate([cells[..., :, 1:], east[..., None]], axis=-1),
+        jnp.concatenate([west[..., None], cells[..., :, :-1]], axis=-1),
         jnp.concatenate([cells[..., 1:, :], north], axis=-2),
         jnp.concatenate([south, cells[..., :-1, :]], axis=-2),
     )

time: 259 us -> 243 us (0.938)
  local copies, waits for them, and re-layouts: 81.7 us -> 73.9 us
  starting transfers between devices: 97.2 us -> 91.1 us
    broadcast_in_dim x0 -> x16, local copies, waits for them, and re-layouts: none -> 17.1 us  [the longest x8 9.2 us: around(): west[..., None]]
    slice x12 -> x2, local copies, waits for them, and re-layouts: 16.8 us -> 1.23 us  [part(): return tuple((item[first:first + count] for item in halo_all))]
    slice x21 -> x13, local copies, waits for them, and re-layouts: 23.5 us -> 8.32 us  [edge(): return jnp.concatenate([item[index] for item in cells], axis=0)]
    ppermute x5, starting transfers between devices: 19.5 us -> 4.94 us  [halos(): lax.ppermute(last_row, ('lon', 'lat'), [(i * lat_count + top, (lon_count...]
    unnamed x92 -> x94, local copies, waits for them, and re-layouts: 9.2 us -> 13.7 us
    ppermute x5, starting transfers between devices: 8.88 us -> 13.2 us  [halos(): lax.ppermute(first_col, 'lon', [((i + 1) % lon_count, i) for i in range(l...]
    all_to_all x3, starting transfers between devices: 38 us -> 41.7 us  [allsum(): gathered = lax.all_to_all(spread, ('lon', 'lat'), 0, 0, tiled=True)]
    ppermute x5, waiting for transfers between devices: 2.91 us -> 0.01 us  [halos(): lax.ppermute(first_row, 'lat', [(i + 1, i) for i in range(lat_count - 1)])]
  transfers between devices with their start and end apart: 28 -> 28, of which waited for: 5 -> 5; matrix products, arithmetic and copies ran while one was open for 32% -> 29% of each run, Pallas kernels for 0% -> 0%
where the time goes in v2:
time: 243 us; the launch traced here: 241 us
  starting transfers between devices  91.1 us (37%)
  local copies, waits for them, and re-layouts  73.9 us (30%)
  other arithmetic  53.4 us (22%)
  waiting for transfers between devices  12.3 us (5%)
  between operations  10.7 us (4%)
    all_to_all x3, starting transfers between devices, allsum(): gathered = lax.all_to_all(spread, ('lon', 'lat'), 0, 0, tiled=True)  41.7 us
    ppermute x5, starting transfers between devices, halos(): lax.ppermute(last_row, 'lat', [(i, i + 1) for i in range(lat_count - 1)])  21.6 us
    unnamed x94, local copies, waits for them, and re-layouts  13.7 us
    ppermute x5, starting transfers between devices, halos(): lax.ppermute(first_col, 'lon', [((i + 1) % lon_count, i) for i in range(l...  13.2 us
    mul x2, other arithmetic, local(): marine_snapshot * (tracer + time_step * (-flux + diffusivity * laplace(tr...  11.7 us
    broadcast_in_dim x8, local copies, waits for them, and re-layouts, around(): west[..., None]  9.2 us
    slice x6, local copies, waits for them, and re-layouts, around(): cells[..., :, 1:]  9.13 us
    all_to_all x3, waiting for transfers between devices, allsum(): gathered = lax.all_to_all(spread, ('lon', 'lat'), 0, 0, tiled=True)  8.8 us
  transfers between devices with their start and end apart: 28, of which 5 were waited for; matrix products, arithmetic and copies ran while one was open for 29% of the time, Pallas kernels for 0%

profile of v2, /device:TPU:1, one launch (start us, length us, event | category | flops | bytes accessed | tf_op | source)
XLA Modules:
  0.0 241.4 jit_solution(12558865792529400419)
XLA Ops:
  1.4 4.0 %broadcast_multiply_fusion.1 = (f32[32,64,128]{2,1,0:T(8,128)S(1)}, f32[32,64,128]{2,1,0:T(8,128)S(1)}, f32[32,64,128]{2,1,0:T(8,128)}, f32[32,64,128]{2,1,0:T(8,128)S(1)}) fusion(f32[32,64,128]{2,1,0:T(8,128)} %param.11, f32[64,128]{1,0:T(8,128)S(1)} %convert_element_type.17, f32[32,64,128]{2,1,0:T(8,128)} %param.10, f32[32,64,128]{2,1,0:T(8,128)} %param.9, ...), kind=kLoop, calls=%fused_computation.52 | loop fusion | flops 1048576 | bytes 8421376 | tf_op jit(solution)/shard_map/mul | solution.py:82
  7.1 1.6 constant_dynamic-update-slice_fusion.16
  11.8 3.9 %collective-permute-start.4 = (f32[129,1,128]{2,1,0:T(1,128)}, f32[129,1,128]{2,1,0:T(1,128)S(1)}, u32[]{:S(2)}, u32[]{:S(2)}) collective-permute-start(f32[129,1,128]{2,1,0:T(1,128)} %get-tuple-element.131), channel_id=1, source_target_pairs={{0,1},{1,2},{2,3},{3,4},{4,5},{5,6},{6,7},{8,9},{9,10},{10,11},{11... | collective-permute-start | bytes 198152 | tf_op jit(solution)/shard_map/ppermute | solution.py:41
  17.0 3.3 %slice_reduce_fusion.2 = (f32[32,64]{1,0:T(8,128)S(1)}, f32[32,64]{1,0:T(8,128)S(1)}, f32[32,64]{1,0:T(8,128)S(1)}, f32[32,64]{1,0:T(8,128)S(1)}) fusion(f32[32,64,128]{2,1,0:T(8,128)} %get-tuple-element.134, f32[32,64,128]{2,1,0:T(8,128)S(1)} %get-tuple-element.135), kind=kLoop, calls=%fused_computation.2 | loop fusion | bytes 65536 | tf_op jit(solution)/shard_map/slice | solution.py:32
  20.3 1.7 slice_reduce_fusion
  28.7 1.5 collective-permute-start.1
  31.5 1.7 fusion.96
  33.2 2.1 fusion.95
  35.3 2.6 %fusion.98 = (f32[32,64,127]{2,1,0:T(8,128)}, f32[32,64,127]{2,1,0:T(8,128)}, f32[32,64,127]{2,1,0:T(8,128)}, f32[32,64,127]{2,1,0:T(8,128)}) fusion(f32[32,64,128]{2,1,0:T(8,128)S(1)} %fusion.19, f32[32,64,128]{2,1,0:T(8,128)S(1)} %get-tuple-element.135), kind=kLoop, calls=%fused_computation.222 | loop fusion | bytes 8323072 | tf_op jit(solution)/shard_map/slice | solution.py:56
  37.9 1.5 fusion.100
  40.8 2.7 %fusion.91 = (f32[32,64,127]{2,1,0:T(8,128)}, f32[32,64,127]{2,1,0:T(8,128)}, f32[32,64,127]{2,1,0:T(8,128)}, f32[32,64,127]{2,1,0:T(8,128)}) fusion(f32[32,64,128]{2,1,0:T(8,128)S(1)} %get-tuple-element.132, f32[32,64,128]{2,1,0:T(8,128)S(1)} %get-tuple-element.133), kind=kLoop, calls=%fused_computation.215 | loop fusion | bytes 8323072 | tf_op jit(solution)/shard_map/slice | solution.py:56
  45.6 1.4 slice_bitcast_fusion.5
  49.2 1.4 copy.610
  50.6 1.4 copy.611
  52.0 1.4 copy.608
  53.4 1.4 copy.609
  56.2 1.5 rev.15
  60.8 6.0 %fusion.88 = (f32[64,128]{1,0:T(8,128)S(1)}, f32[32,64,128]{2,1,0:T(8,128)}) fusion(f32[32,63,128]{2,1,0:T(8,128)S(1)} %copy-done.1, f32[32,1,128]{2,1,0:T(1,128)S(1)} %get-tuple-element.99, f32[32,1,128]{2,1,0:T(1,128)S(1)} %get-tuple-element.95, f32[32,63,128]{2,1,0:T(8,128)} %get-tuple-element.157, f32[32,64,127]{2,1,0:T(8,128)} %get-tuple-element.67, ...), kind=kLoop, calls=%fused_computation.213 | loop fusion | flops 6021120 | bytes 9502976 | tf_op jit(solution)/shard_map/reduce_sum | solution.py:141
  68.2 3.8 %fusion.86 = (f32[64,128]{1,0:T(8,128)S(1)}, f32[32,64,128]{2,1,0:T(8,128)}) fusion(f32[32,63,128]{2,1,0:T(8,128)S(1)} %copy-done.12, f32[32,1,128]{2,1,0:T(1,128)S(1)} %get-tuple-element.101, f32[32,1,128]{2,1,0:T(1,128)S(1)} %get-tuple-element.97, f32[32,63,128]{2,1,0:T(8,128)S(1)} %copy-done.11, f32[32,64,127]{2,1,0:T(8,128)S(1)} %copy-done.5, ...), kind=kLoop, calls=%fused_computation.212 | loop fusion | flops 6021120 | bytes 9502976 | tf_op jit(solution)/shard_map/reduce_sum | solution.py:140
  74.3 4.3 %collective-permute-start.9 = (f32[2,1,128]{2,1,0:T(1,128)S(1)}, f32[2,1,128]{2,1,0:T(1,128)S(1)}, u32[]{:S(2)}, u32[]{:S(2)}) collective-permute-start(f32[2,1,128]{2,1,0:T(1,128)S(1)} %pad_maximum_fusion.19), channel_id=1, source_target_pairs={{0,1},{1,2},{2,3},{3,4},{4,5},{5,6},{6,7},{8,9},{9,10},{10,11},{11... | collective-permute-start | bytes 3080 | tf_op jit(solution)/shard_map/ppermute | solution.py:41
  79.1 4.3 %collective-permute-start.5 = (f32[2,64]{1,0:T(2,128)S(1)}, f32[2,64]{1,0:T(2,128)S(1)}, u32[]{:S(2)}, u32[]{:S(2)}) collective-permute-start(f32[2,64]{1,0:T(2,128)S(1)} %pad_maximum_fusion.17), channel_id=1, source_target_pairs={{8,0},{16,8},{24,16},{32,24},{40,32},{48,40},{56,48},{64,56},{72,6... | collective-permute-start | bytes 1544 | tf_op jit(solution)/shard_map/ppermute | solution.py:38
  86.0 3.1 %collective-permute-done.6 = f32[2,64]{1,0:T(2,128)S(1)} collective-permute-done((f32[2,64]{1,0:T(2,128)S(1)}, f32[2,64]{1,0:T(2,128)S(1)}, u32[]{:S(2)}, u32[]{:S(2)}) %collective-permute-start.6) | collective-permute-done | bytes 544 | tf_op jit(solution)/shard_map/ppermute | solution.py:39
  91.2 1.6 fusion.80
  95.7 6.0 %collective-permute-start.10 = (f32[64]{0:T(128)S(1)}, f32[64]{0:T(128)S(1)}, u32[]{:S(2)}, u32[]{:S(2)}) collective-permute-start(f32[64]{0:T(128)S(1)} %get-tuple-element.29), channel_id=1, source_target_pairs={{8,0},{16,8},{24,16},{32,24},{40,32},{48,40},{56,48},{64,56},{72,6... | collective-permute-start | bytes 776 | tf_op jit(solution)/shard_map/ppermute | solution.py:38
  102.4 4.3 %collective-permute-start.14 = (f32[1,128]{1,0:T(1,128)S(1)}, f32[1,128]{1,0:T(1,128)S(1)}, u32[]{:S(2)}, u32[]{:S(2)}) collective-permute-start(f32[1,128]{1,0:T(1,128)S(1)} %get-tuple-element.121), channel_id=1, source_target_pairs={{0,1},{1,2},{2,3},{3,4},{4,5},{5,6},{6,7},{8,9},{9,10},{10,11},{11... | collective-permute-start | bytes 1544 | tf_op jit(solution)/shard_map/ppermute | solution.py:41
  108.6 1.6 multiply_reduce_fusion.9
  110.1 1.4 pad_maximum_fusion.21
  112.2 17.4 %all-to-all-start = ((f32[128,1,2]{2,1,0:T(1,128)}), f32[128,1,2]{2,1,0:T(1,128)}, u32[]{:S(2)}, u32[]{:S(2)}) async-start(f32[128,1,2]{2,1,0:T(1,128)} %broadcast_in_dim.95), calls=%async_computation | async-start | bytes 131072 | tf_op jit(solution)/shard_map/all_to_all | solution.py:21
  129.6 2.1 fusion.92
  131.7 1.4 copy.614
  133.1 1.4 copy.615
  134.5 1.4 copy.612
  135.9 1.5 copy.613
  137.4 1.5 all-to-all-done
  148.7 4.6 %collective-permute-start.19 = (f32[1,128]{1,0:T(1,128)}, f32[1,128]{1,0:T(1,128)}, u32[]{:S(2)}, u32[]{:S(2)}) collective-permute-start(f32[1,128]{1,0:T(1,128)} %get-tuple-element.115), channel_id=1, source_target_pairs={{0,1},{1,2},{2,3},{3,4},{4,5},{5,6},{6,7},{8,9},{9,10},{10,11},{11... | collective-permute-start | bytes 1544 | tf_op jit(solution)/shard_map/ppermute | solution.py:41
  157.9 2.2 multiply_reduce_fusion.7
  160.1 2.5 %pad_maximum_fusion.22 = f32[4]{0:T(128)S(1)} fusion(f32[1]{0:T(128)} %bitcast.32, f32[1]{0:T(128)} %bitcast.31, f32[1]{0:T(128)} %bitcast.30, f32[1]{0:T(128)} %bitcast.27), kind=kLoop, calls=%fused_computation.195 | loop fusion | flops 12 | bytes 32 | tf_op jit(solution)/shard_map/stack | solution.py:182
  163.3 13.2 %all-to-all-start.1 = ((f32[128,1,4]{2,1,0:T(1,128)}), f32[128,1,4]{2,1,0:T(1,128)}, u32[]{:S(2)}, u32[]{:S(2)}) async-start(f32[128,1,4]{2,1,0:T(1,128)} %broadcast_in_dim.98), calls=%async_computation.1 | async-start | bytes 131072 | tf_op jit(solution)/shard_map/all_to_all | solution.py:21
  176.5 6.0 %add_multiply_fusion = f32[32,64,128]{2,1,0:T(8,128)} fusion(f32[32,64,128]{2,1,0:T(8,128)S(1)} %get-tuple-element.132, f32[32,63,128]{2,1,0:T(8,128)} %get-tuple-element.59, f32[32,1,128]{2,1,0:T(1,128)} %get-tuple-element.98, f32[32,1,128]{2,1,0:T(1,128)S(1)} %copy-done.28, f32[32,63,128]{2,1,0:T(8,128)} %get-tuple-element.58, ...), kind=kLoop, calls=%fused_computation.43 | loop fusion | flops 7077888 | bytes 10518528 | tf_op jit(solution)/shard_map/mul | solution.py:138
  182.5 3.4 %all-to-all-done.1 = f32[128,1,4]{2,1,0:T(1,128)} async-done(((f32[128,1,4]{2,1,0:T(1,128)}), f32[128,1,4]{2,1,0:T(1,128)}, u32[]{:S(2)}, u32[]{:S(2)}) %all-to-all-start.1) | async-done | bytes 2080 | tf_op jit(solution)/shard_map/all_to_all | solution.py:21
  191.9 1.4 fusion.64
  200.2 4.5 %collective-permute-start.24 = (f32[1,128]{1,0:T(1,128)}, f32[1,128]{1,0:T(1,128)}, u32[]{:S(2)}, u32[]{:S(2)}) collective-permute-start(f32[1,128]{1,0:T(1,128)} %get-tuple-element.109), channel_id=1, source_target_pairs={{0,1},{1,2},{2,3},{3,4},{4,5},{5,6},{6,7},{8,9},{9,10},{10,11},{11... | collective-permute-start | bytes 1544 | tf_op jit(solution)/shard_map/ppermute | solution.py:41
  205.9 1.4 copy.627
  209.2 2.2 multiply_reduce_fusion.3
  211.4 2.6 %pad_maximum_fusion.23 = f32[4]{0:T(128)S(1)} fusion(f32[1]{0:T(128)} %bitcast.41, f32[1]{0:T(128)} %bitcast.40, f32[1]{0:T(128)} %bitcast.39, f32[1]{0:T(128)} %bitcast.36), kind=kLoop, calls=%fused_computation.196 | loop fusion | flops 12 | bytes 32 | tf_op jit(solution)/shard_map/stack | solution.py:182
  214.6 11.1 %all-to-all-start.2 = ((f32[128,1,4]{2,1,0:T(1,128)}), f32[128,1,4]{2,1,0:T(1,128)S(1)}, u32[]{:S(2)}, u32[]{:S(2)}) async-start(f32[128,1,4]{2,1,0:T(1,128)} %broadcast_in_dim.101), calls=%async_computation.2 | async-start | bytes 131072 | tf_op jit(solution)/shard_map/all_to_all | solution.py:21
  225.8 5.7 %add_multiply_fusion.1 = f32[32,64,128]{2,1,0:T(8,128)} fusion(f32[32,64,128]{2,1,0:T(8,128)S(1)} %get-tuple-element.133, f32[32,63,128]{2,1,0:T(8,128)} %get-tuple-element.152, f32[32,1,128]{2,1,0:T(1,128)S(1)} %copy-done.27, f32[32,1,128]{2,1,0:T(1,128)S(1)} %copy-done.26, f32[32,63,128]{2,1,0:T(8,128)} %get-tuple-element.153, ...), kind=kLoop, calls=%fused_computation.44 | loop fusion | flops 7077888 | bytes 10518528 | tf_op jit(solution)/shard_map/mul | solution.py:138
  231.5 3.9 %all-to-all-done.2 = f32[128,1,4]{2,1,0:T(1,128)S(1)} async-done(((f32[128,1,4]{2,1,0:T(1,128)}), f32[128,1,4]{2,1,0:T(1,128)S(1)}, u32[]{:S(2)}, u32[]{:S(2)}) %all-to-all-start.2) | async-done | bytes 2080 | tf_op jit(solution)/shard_map/all_to_all | solution.py:21
  (218 shorter events, 67.8 us)
Async XLA Ops:
  10.5 45.7 %collective-permute-start.2 = (f32[129,1,128]{2,1,0:T(1,128)}, f32[129,1,128]{2,1,0:T(1,128)}, u32[]{:S(2)}, u32[]{:S(2)}) collective-permute-start(f32[129,1,128]{2,1,0:T(1,128)} %get-tuple-element.131), channel_id=1, source_target_pairs={{7,127},{15,119},{23,111},{31,103},{39,95},{47,87},{55,79},{63,71}... | collective-permute-start | bytes 198152 | tf_op jit(solution)/shard_map/ppermute | solution.py:43
  11.8 47.7 %collective-permute-start.4 = (f32[129,1,128]{2,1,0:T(1,128)}, f32[129,1,128]{2,1,0:T(1,128)S(1)}, u32[]{:S(2)}, u32[]{:S(2)}) collective-permute-start(f32[129,1,128]{2,1,0:T(1,128)} %get-tuple-element.131), channel_id=1, source_target_pairs={{0,1},{1,2},{2,3},{3,4},{4,5},{5,6},{6,7},{8,9},{9,10},{10,11},{11... | collective-permute-start | bytes 198152 | tf_op jit(solution)/shard_map/ppermute | solution.py:41
  15.7 42.0 %collective-permute-start.3 = (f32[129,1,128]{2,1,0:T(1,128)}, f32[129,1,128]{2,1,0:T(1,128)}, u32[]{:S(2)}, u32[]{:S(2)}) collective-permute-start(f32[129,1,128]{2,1,0:T(1,128)} %get-tuple-element.130), channel_id=1, source_target_pairs={{1,0},{2,1},{3,2},{4,3},{5,4},{6,5},{7,6},{9,8},{10,9},{11,10},{12... | collective-permute-start | bytes 198152 | tf_op jit(solution)/shard_map/ppermute | solution.py:40
  25.8 17.7 %collective-permute-start = (f32[129,64]{1,0:T(8,128)}, f32[129,64]{1,0:T(8,128)S(1)}, u32[]{:S(2)}, u32[]{:S(2)}) collective-permute-start(f32[129,64]{1,0:T(8,128)} %dynamic-update-slice.19), channel_id=1, source_target_pairs={{8,0},{16,8},{24,16},{32,24},{40,32},{48,40},{56,48},{64,56},{72,6... | collective-permute-start | bytes 99080 | tf_op jit(solution)/shard_map/ppermute | solution.py:38
  28.7 16.9 %collective-permute-start.1 = (f32[129,64]{1,0:T(8,128)}, f32[129,64]{1,0:T(8,128)}, u32[]{:S(2)}, u32[]{:S(2)}) collective-permute-start(f32[129,64]{1,0:T(8,128)} %dynamic-update-slice.14), channel_id=1, source_target_pairs={{0,8},{8,16},{16,24},{24,32},{32,40},{40,48},{48,56},{56,64},{64,7... | collective-permute-start | bytes 99080 | tf_op jit(solution)/shard_map/ppermute | solution.py:39
  53.4 7.3 %copy-start.1 = (f32[32,63,128]{2,1,0:T(8,128)S(1)}, f32[32,63,128]{2,1,0:T(8,128)}, u32[]{:S(2)}) copy-start(f32[32,63,128]{2,1,0:T(8,128)} %get-tuple-element.156) | copy-start | bytes 3096580
  56.2 1.5 copy-start.32
  60.7 6.3 %copy-start.3 = (f32[32,64,1]{2,1,0:T(8,128)S(1)}, f32[32,64,1]{2,1,0:T(8,128)}, u32[]{:S(2)}) copy-start(f32[32,64,1]{2,1,0:T(8,128)} %copy.608) | copy-start | bytes 24580
  60.7 6.3 %copy-start.4 = (f32[32,64,1]{2,1,0:T(8,128)S(1)}, f32[32,64,1]{2,1,0:T(8,128)}, u32[]{:S(2)}) copy-start(f32[32,64,1]{2,1,0:T(8,128)} %copy.609) | copy-start | bytes 24580
  60.7 6.3 %copy-start.5 = (f32[32,64,127]{2,1,0:T(8,128)S(1)}, f32[32,64,127]{2,1,0:T(8,128)}, u32[]{:S(2)}) copy-start(f32[32,64,127]{2,1,0:T(8,128)} %get-tuple-element.154) | copy-start | bytes 3121156
  60.7 6.3 %copy-start.6 = (f32[32,64,127]{2,1,0:T(8,128)S(1)}, f32[32,64,127]{2,1,0:T(8,128)}, u32[]{:S(2)}) copy-start(f32[32,64,127]{2,1,0:T(8,128)} %get-tuple-element.155) | copy-start | bytes 3121156
  60.7 6.3 %copy-start.7 = (f32[32,64,128]{2,1,0:T(8,128)S(1)}, f32[32,64,128]{2,1,0:T(8,128)}, u32[]{:S(2)}) copy-start(f32[32,64,128]{2,1,0:T(8,128)} %param.9) | copy-start | bytes 3145732
  60.8 6.3 %copy-start.8 = (f32[32,64,128]{2,1,0:T(8,128)S(1)}, f32[32,64,128]{2,1,0:T(8,128)}, u32[]{:S(2)}) copy-start(f32[32,64,128]{2,1,0:T(8,128)} %param.8) | copy-start | bytes 3145732
  60.8 6.3 %copy-start.9 = (f32[32,64,1]{2,1,0:T(8,128)S(1)}, f32[32,64,1]{2,1,0:T(8,128)}, u32[]{:S(2)}) copy-start(f32[32,64,1]{2,1,0:T(8,128)} %fusion.119) | copy-start | bytes 24580
  60.8 6.3 %copy-start.10 = (f32[32,64,1]{2,1,0:T(8,128)S(1)}, f32[32,64,1]{2,1,0:T(8,128)}, u32[]{:S(2)}) copy-start(f32[32,64,1]{2,1,0:T(8,128)} %fusion.120) | copy-start | bytes 24580
  60.8 6.8 %copy-start.11 = (f32[32,63,128]{2,1,0:T(8,128)S(1)}, f32[32,63,128]{2,1,0:T(8,128)}, u32[]{:S(2)}) copy-start(f32[32,63,128]{2,1,0:T(8,128)} %get-tuple-element.74) | copy-start | bytes 3096580
  60.8 7.1 %copy-start.12 = (f32[32,63,128]{2,1,0:T(8,128)S(1)}, f32[32,63,128]{2,1,0:T(8,128)}, u32[]{:S(2)}) copy-start(f32[32,63,128]{2,1,0:T(8,128)} %get-tuple-element.75) | copy-start | bytes 3096580
  60.8 7.4 %copy-start.13 = (f32[32,64,127]{2,1,0:T(8,128)S(1)}, f32[32,64,127]{2,1,0:T(8,128)}, u32[]{:S(2)}) copy-start(f32[32,64,127]{2,1,0:T(8,128)} %get-tuple-element.70) | copy-start | bytes 3121156
  73.6 16.3 %collective-permute-start.7 = (f32[2,1,128]{2,1,0:T(1,128)S(1)}, f32[2,1,128]{2,1,0:T(1,128)S(1)}, u32[]{:S(2)}, u32[]{:S(2)}) collective-permute-start(f32[2,1,128]{2,1,0:T(1,128)S(1)} %pad_maximum_fusion.19), channel_id=1, source_target_pairs={{7,127},{15,119},{23,111},{31,103},{39,95},{47,87},{55,79},{63,71}... | collective-permute-start | bytes 3080 | tf_op jit(solution)/shard_map/ppermute | solution.py:43
  74.3 15.7 %collective-permute-start.9 = (f32[2,1,128]{2,1,0:T(1,128)S(1)}, f32[2,1,128]{2,1,0:T(1,128)S(1)}, u32[]{:S(2)}, u32[]{:S(2)}) collective-permute-start(f32[2,1,128]{2,1,0:T(1,128)S(1)} %pad_maximum_fusion.19), channel_id=1, source_target_pairs={{0,1},{1,2},{2,3},{3,4},{4,5},{5,6},{6,7},{8,9},{9,10},{10,11},{11... | collective-permute-start | bytes 3080 | tf_op jit(solution)/shard_map/ppermute | solution.py:41
  79.1 6.2 %collective-permute-start.5 = (f32[2,64]{1,0:T(2,128)S(1)}, f32[2,64]{1,0:T(2,128)S(1)}, u32[]{:S(2)}, u32[]{:S(2)}) collective-permute-start(f32[2,64]{1,0:T(2,128)S(1)} %pad_maximum_fusion.17), channel_id=1, source_target_pairs={{8,0},{16,8},{24,16},{32,24},{40,32},{48,40},{56,48},{64,56},{72,6... | collective-permute-start | bytes 1544 | tf_op jit(solution)/shard_map/ppermute | solution.py:38
  83.4 5.7 %collective-permute-start.6 = (f32[2,64]{1,0:T(2,128)S(1)}, f32[2,64]{1,0:T(2,128)S(1)}, u32[]{:S(2)}, u32[]{:S(2)}) collective-permute-start(f32[2,64]{1,0:T(2,128)S(1)} %pad_maximum_fusion.18), channel_id=1, source_target_pairs={{0,8},{8,16},{16,24},{24,32},{32,40},{40,48},{48,56},{56,64},{64,7... | collective-permute-start | bytes 1544 | tf_op jit(solution)/shard_map/ppermute | solution.py:39
  83.4 6.6 %collective-permute-start.8 = (f32[2,1,128]{2,1,0:T(1,128)S(1)}, f32[2,1,128]{2,1,0:T(1,128)S(1)}, u32[]{:S(2)}, u32[]{:S(2)}) collective-permute-start(f32[2,1,128]{2,1,0:T(1,128)S(1)} %pad_maximum_fusion.20), channel_id=1, source_target_pairs={{1,0},{2,1},{3,2},{4,3},{5,4},{6,5},{7,6},{9,8},{10,9},{11,10},{12... | collective-permute-start | bytes 3080 | tf_op jit(solution)/shard_map/ppermute | solution.py:40
  93.7 13.1 %collective-permute-start.12 = (f32[1,128]{1,0:T(1,128)S(1)}, f32[1,128]{1,0:T(1,128)S(1)}, u32[]{:S(2)}, u32[]{:S(2)}) collective-permute-start(f32[1,128]{1,0:T(1,128)S(1)} %get-tuple-element.121), channel_id=1, source_target_pairs={{7,127},{15,119},{23,111},{31,103},{39,95},{47,87},{55,79},{63,71}... | collective-permute-start | bytes 1544 | tf_op jit(solution)/shard_map/ppermute | solution.py:43
  94.4 12.5 %collective-permute-start.13 = (f32[1,128]{1,0:T(1,128)S(1)}, f32[1,128]{1,0:T(1,128)S(1)}, u32[]{:S(2)}, u32[]{:S(2)}) collective-permute-start(f32[1,128]{1,0:T(1,128)S(1)} %get-tuple-element.120), channel_id=1, source_target_pairs={{1,0},{2,1},{3,2},{4,3},{5,4},{6,5},{7,6},{9,8},{10,9},{11,10},{12... | collective-permute-start | bytes 1544 | tf_op jit(solution)/shard_map/ppermute | solution.py:40
  95.7 10.9 %collective-permute-start.10 = (f32[64]{0:T(128)S(1)}, f32[64]{0:T(128)S(1)}, u32[]{:S(2)}, u32[]{:S(2)}) collective-permute-start(f32[64]{0:T(128)S(1)} %get-tuple-element.29), channel_id=1, source_target_pairs={{8,0},{16,8},{24,16},{32,24},{40,32},{48,40},{56,48},{64,56},{72,6... | collective-permute-start | bytes 776 | tf_op jit(solution)/shard_map/ppermute | solution.py:38
  101.7 5.0 %collective-permute-start.11 = (f32[64]{0:T(128)S(1)}, f32[64]{0:T(128)S(1)}, u32[]{:S(2)}, u32[]{:S(2)}) collective-permute-start(f32[64]{0:T(128)S(1)} %get-tuple-element.28), channel_id=1, source_target_pairs={{0,8},{8,16},{16,24},{24,32},{32,40},{40,48},{48,56},{56,64},{64,7... | collective-permute-start | bytes 776 | tf_op jit(solution)/shard_map/ppermute | solution.py:39
  102.4 5.0 %collective-permute-start.14 = (f32[1,128]{1,0:T(1,128)S(1)}, f32[1,128]{1,0:T(1,128)S(1)}, u32[]{:S(2)}, u32[]{:S(2)}) collective-permute-start(f32[1,128]{1,0:T(1,128)S(1)} %get-tuple-element.121), channel_id=1, source_target_pairs={{0,1},{1,2},{2,3},{3,4},{4,5},{5,6},{6,7},{8,9},{9,10},{10,11},{11... | collective-permute-start | bytes 1544 | tf_op jit(solution)/shard_map/ppermute | solution.py:41
  112.2 26.7 %all-to-all-start = ((f32[128,1,2]{2,1,0:T(1,128)}), f32[128,1,2]{2,1,0:T(1,128)}, u32[]{:S(2)}, u32[]{:S(2)}) async-start(f32[128,1,2]{2,1,0:T(1,128)} %broadcast_in_dim.95), calls=%async_computation | async-start | bytes 131072 | tf_op jit(solution)/shard_map/all_to_all | solution.py:21
  129.6 2.1 copy-start.23
  143.8 12.2 %collective-permute-start.17 = (f32[1,128]{1,0:T(1,128)}, f32[1,128]{1,0:T(1,128)}, u32[]{:S(2)}, u32[]{:S(2)}) collective-permute-start(f32[1,128]{1,0:T(1,128)} %get-tuple-element.115), channel_id=1, source_target_pairs={{7,127},{15,119},{23,111},{31,103},{39,95},{47,87},{55,79},{63,71}... | collective-permute-start | bytes 1544 | tf_op jit(solution)/shard_map/ppermute | solution.py:43
  145.0 12.3 %collective-permute-start.18 = (f32[1,128]{1,0:T(1,128)}, f32[1,128]{1,0:T(1,128)}, u32[]{:S(2)}, u32[]{:S(2)}) collective-permute-start(f32[1,128]{1,0:T(1,128)} %get-tuple-element.114), channel_id=1, source_target_pairs={{1,0},{2,1},{3,2},{4,3},{5,4},{6,5},{7,6},{9,8},{10,9},{11,10},{12... | collective-permute-start | bytes 1544 | tf_op jit(solution)/shard_map/ppermute | solution.py:40
  146.2 7.1 %collective-permute-start.15 = (f32[64]{0:T(128)S(1)}, f32[64]{0:T(128)S(1)}, u32[]{:S(2)}, u32[]{:S(2)}) collective-permute-start(f32[64]{0:T(128)S(1)} %get-tuple-element.25), channel_id=1, source_target_pairs={{8,0},{16,8},{24,16},{32,24},{40,32},{48,40},{56,48},{64,56},{72,6... | collective-permute-start | bytes 776 | tf_op jit(solution)/shard_map/ppermute | solution.py:38
  147.2 7.5 %collective-permute-start.16 = (f32[64]{0:T(128)}, f32[64]{0:T(128)}, u32[]{:S(2)}, u32[]{:S(2)}) collective-permute-start(f32[64]{0:T(128)} %get-tuple-element.24), channel_id=1, source_target_pairs={{0,8},{8,16},{16,24},{24,32},{32,40},{40,48},{48,56},{56,64},{64,7... | collective-permute-start | bytes 776 | tf_op jit(solution)/shard_map/ppermute | solution.py:39
  148.7 9.2 %collective-permute-start.19 = (f32[1,128]{1,0:T(1,128)}, f32[1,128]{1,0:T(1,128)}, u32[]{:S(2)}, u32[]{:S(2)}) collective-permute-start(f32[1,128]{1,0:T(1,128)} %get-tuple-element.115), channel_id=1, source_target_pairs={{0,1},{1,2},{2,3},{3,4},{4,5},{5,6},{6,7},{8,9},{9,10},{10,11},{11... | collective-permute-start | bytes 1544 | tf_op jit(solution)/shard_map/ppermute | solution.py:41
  163.3 13.2 %copy-start.17 = (f32[32,1,128]{2,1,0:T(1,128)S(1)}, f32[32,1,128]{2,1,0:T(1,128)}, u32[]{:S(2)}) copy-start(f32[32,1,128]{2,1,0:T(1,128)} %copy-done.16) | copy-start | bytes 49156
  163.3 13.2 %copy-start.28 = (f32[32,1,128]{2,1,0:T(1,128)S(1)}, f32[32,1,128]{2,1,0:T(1,128)}, u32[]{:S(2)}) copy-start(f32[32,1,128]{2,1,0:T(1,128)} %get-tuple-element.94) | copy-start | bytes 49156
  163.3 22.6 %all-to-all-start.1 = ((f32[128,1,4]{2,1,0:T(1,128)}), f32[128,1,4]{2,1,0:T(1,128)}, u32[]{:S(2)}, u32[]{:S(2)}) async-start(f32[128,1,4]{2,1,0:T(1,128)} %broadcast_in_dim.98), calls=%async_computation.1 | async-start | bytes 131072 | tf_op jit(solution)/shard_map/all_to_all | solution.py:21
  182.5 43.2 %copy-start.2 = (f32[32,63,128]{2,1,0:T(8,128)S(1)}, f32[32,63,128]{2,1,0:T(8,128)}, u32[]{:S(2)}) copy-start(f32[32,63,128]{2,1,0:T(8,128)} %get-tuple-element.157) | copy-start | bytes 3096580
  195.3 12.0 %collective-permute-start.22 = (f32[1,128]{1,0:T(1,128)}, f32[1,128]{1,0:T(1,128)}, u32[]{:S(2)}, u32[]{:S(2)}) collective-permute-start(f32[1,128]{1,0:T(1,128)} %get-tuple-element.109), channel_id=1, source_target_pairs={{7,127},{15,119},{23,111},{31,103},{39,95},{47,87},{55,79},{63,71}... | collective-permute-start | bytes 1544 | tf_op jit(solution)/shard_map/ppermute | solution.py:43
  196.5 12.1 %collective-permute-start.23 = (f32[1,128]{1,0:T(1,128)}, f32[1,128]{1,0:T(1,128)}, u32[]{:S(2)}, u32[]{:S(2)}) collective-permute-start(f32[1,128]{1,0:T(1,128)} %get-tuple-element.108), channel_id=1, source_target_pairs={{1,0},{2,1},{3,2},{4,3},{5,4},{6,5},{7,6},{9,8},{10,9},{11,10},{12... | collective-permute-start | bytes 1544 | tf_op jit(solution)/shard_map/ppermute | solution.py:40
  197.8 7.0 %collective-permute-start.20 = (f32[64]{0:T(128)S(1)}, f32[64]{0:T(128)S(1)}, u32[]{:S(2)}, u32[]{:S(2)}) collective-permute-start(f32[64]{0:T(128)S(1)} %get-tuple-element.19), channel_id=1, source_target_pairs={{8,0},{16,8},{24,16},{32,24},{40,32},{48,40},{56,48},{64,56},{72,6... | collective-permute-start | bytes 776 | tf_op jit(solution)/shard_map/ppermute | solution.py:38
  198.7 7.2 %collective-permute-start.21 = (f32[64]{0:T(128)}, f32[64]{0:T(128)}, u32[]{:S(2)}, u32[]{:S(2)}) collective-permute-start(f32[64]{0:T(128)} %get-tuple-element.18), channel_id=1, source_target_pairs={{0,8},{8,16},{16,24},{24,32},{32,40},{40,48},{48,56},{56,64},{64,7... | collective-permute-start | bytes 776 | tf_op jit(solution)/shard_map/ppermute | solution.py:39
  200.2 8.9 %collective-permute-start.24 = (f32[1,128]{1,0:T(1,128)}, f32[1,128]{1,0:T(1,128)}, u32[]{:S(2)}, u32[]{:S(2)}) collective-permute-start(f32[1,128]{1,0:T(1,128)} %get-tuple-element.109), channel_id=1, source_target_pairs={{0,1},{1,2},{2,3},{3,4},{4,5},{5,6},{6,7},{8,9},{9,10},{10,11},{11... | collective-permute-start | bytes 1544 | tf_op jit(solution)/shard_map/ppermute | solution.py:41
  214.6 11.1 %copy-start.18 = (f32[32,1,128]{2,1,0:T(1,128)S(1)}, f32[32,1,128]{2,1,0:T(1,128)}, u32[]{:S(2)}) copy-start(f32[32,1,128]{2,1,0:T(1,128)} %copy-done.16) | copy-start | bytes 49156
  214.6 11.1 %copy-start.26 = (f32[32,1,128]{2,1,0:T(1,128)S(1)}, f32[32,1,128]{2,1,0:T(1,128)}, u32[]{:S(2)}) copy-start(f32[32,1,128]{2,1,0:T(1,128)} %get-tuple-element.96) | copy-start | bytes 49156
  214.6 11.2 %copy-start.27 = (f32[32,1,128]{2,1,0:T(1,128)S(1)}, f32[32,1,128]{2,1,0:T(1,128)}, u32[]{:S(2)}) copy-start(f32[32,1,128]{2,1,0:T(1,128)} %get-tuple-element.100) | copy-start | bytes 49156
  214.6 20.8 %all-to-all-start.2 = ((f32[128,1,4]{2,1,0:T(1,128)}), f32[128,1,4]{2,1,0:T(1,128)S(1)}, u32[]{:S(2)}, u32[]{:S(2)}) async-start(f32[128,1,4]{2,1,0:T(1,128)} %broadcast_in_dim.101), calls=%async_computation.2 | async-start | bytes 131072 | tf_op jit(solution)/shard_map/all_to_all | solution.py:21
  (21 other events, 17.9 us)

commit v3 on v2

--- a/solution.py
+++ b/solution.py
@@ -168,7 +168,7 @@
     precond = residual / diag
     direction = precond
     image = apply(direction, halos(direction, unit))
-    pair = allsum(jnp.stack([jnp.sum(residual * precond), jnp.sum(direction * image)]))
+    pair = allsum(jnp.sum(jnp.stack([residual * precond, direction * image]), axis=(1, 2)))
     product_now = pair[0]
     curvature = pair[1]
     for step in range(ITERS):
@@ -179,13 +179,11 @@
             precond = residual / diag
             image_z = apply(precond, halos(precond, unit))
             sums = allsum(
-                jnp.stack(
-                    [
-                        jnp.sum(residual * precond),
-                        jnp.sum(precond * image_z),
-                        jnp.sum(precond * image),
-                        jnp.sum(direction * image_z),
-                    ]
+                jnp.sum(
+                    jnp.stack(
+                        [residual * precond, precond * image_z, precond * image, direction * image_z]
+                    ),
+                    axis=(1, 2),
                 )
             )
             product_next = sums[0]

time: 243 us -> 228 us (0.938)
  other arithmetic: 53.4 us -> 42.9 us
  local copies, waits for them, and re-layouts: 73.9 us -> 69.1 us
    reduce_sum x3, other arithmetic: 6.02 us -> 0.35 us  [the longest x2 0.24 us: local(): jnp.sum(jnp.stack([residual * precond, precond * image_z, precond * image...]
    div x3 -> x0, other arithmetic: 3.04 us -> none  [local(): precond = residual / diag]
    unnamed x94 -> x96, local copies, waits for them, and re-layouts: 13.7 us -> 14.1 us
    another operation x3 -> x8, other arithmetic: 6.44 us -> 6.48 us  [the longest x6 3.92 us: local(): jnp.stack([residual * precond, precond * image_z, precond * image, direct...]
where the time goes in v3:
time: 228 us; the launch traced here: 226 us
  starting transfers between devices  90.5 us (40%)
  local copies, waits for them, and re-layouts  69.1 us (30%)
  other arithmetic  42.9 us (19%)
  waiting for transfers between devices  12.6 us (6%)
  between operations  11.3 us (5%)
    all_to_all x3, starting transfers between devices, allsum(): gathered = lax.all_to_all(spread, ('lon', 'lat'), 0, 0, tiled=True)  41 us
    ppermute x5, starting transfers between devices, halos(): lax.ppermute(last_row, 'lat', [(i, i + 1) for i in range(lat_count - 1)])  21.5 us
    unnamed x96, local copies, waits for them, and re-layouts  14.1 us
    ppermute x5, starting transfers between devices, halos(): lax.ppermute(first_col, 'lon', [((i + 1) % lon_count, i) for i in range(l...  13.1 us
    mul x2, other arithmetic, local(): marine_snapshot * (tracer + time_step * (-flux + diffusivity * laplace(tr...  11.7 us
    slice x6, local copies, waits for them, and re-layouts, around(): cells[..., :, 1:]  9.2 us
    all_to_all x3, waiting for transfers between devices, allsum(): gathered = lax.all_to_all(spread, ('lon', 'lat'), 0, 0, tiled=True)  9.01 us
    broadcast_in_dim x8, local copies, waits for them, and re-layouts, around(): west[..., None]  7.89 us
  transfers between devices with their start and end apart: 28, of which 5 were waited for; matrix products, arithmetic and copies ran while one was open for 29% of the time, Pallas kernels for 0%

profile of v3, /device:TPU:1, one launch (start us, length us, event | category | flops | bytes accessed | tf_op | source)
XLA Modules:
  0.0 226.4 jit_solution(8262943657250202077)
XLA Ops:
  1.4 3.8 %broadcast_multiply_fusion.1 = (f32[32,64,128]{2,1,0:T(8,128)S(1)}, f32[32,64,128]{2,1,0:T(8,128)S(1)}, f32[32,64,128]{2,1,0:T(8,128)}, f32[32,64,128]{2,1,0:T(8,128)S(1)}) fusion(f32[32,64,128]{2,1,0:T(8,128)} %param.11, f32[64,128]{1,0:T(8,128)S(1)} %convert_element_type.17, f32[32,64,128]{2,1,0:T(8,128)} %param.10, f32[32,64,128]{2,1,0:T(8,128)} %param.9, ...), kind=kLoop, calls=%fused_computation.52 | loop fusion | flops 1048576 | bytes 8421376 | tf_op jit(solution)/shard_map/mul | solution.py:82
  6.9 1.6 constant_dynamic-update-slice_fusion.16
  11.7 3.9 %collective-permute-start.4 = (f32[129,1,128]{2,1,0:T(1,128)}, f32[129,1,128]{2,1,0:T(1,128)S(1)}, u32[]{:S(2)}, u32[]{:S(2)}) collective-permute-start(f32[129,1,128]{2,1,0:T(1,128)} %get-tuple-element.129), channel_id=1, source_target_pairs={{0,1},{1,2},{2,3},{3,4},{4,5},{5,6},{6,7},{8,9},{9,10},{10,11},{11... | collective-permute-start | bytes 198152 | tf_op jit(solution)/shard_map/ppermute | solution.py:41
  15.6 1.3 collective-permute-start.3
  16.9 3.3 %slice_reduce_fusion.2 = (f32[32,64]{1,0:T(8,128)S(1)}, f32[32,64]{1,0:T(8,128)S(1)}, f32[32,64]{1,0:T(8,128)S(1)}, f32[32,64]{1,0:T(8,128)S(1)}) fusion(f32[32,64,128]{2,1,0:T(8,128)} %get-tuple-element.132, f32[32,64,128]{2,1,0:T(8,128)S(1)} %get-tuple-element.133), kind=kLoop, calls=%fused_computation.2 | loop fusion | bytes 65536 | tf_op jit(solution)/shard_map/slice | solution.py:32
  20.1 1.7 slice_reduce_fusion
  27.3 1.3 dynamic-update-slice.14
  28.6 1.5 collective-permute-start.1
  31.4 1.7 fusion.95
  33.1 2.1 fusion.94
  35.2 2.7 %fusion.97 = (f32[32,64,127]{2,1,0:T(8,128)}, f32[32,64,127]{2,1,0:T(8,128)}, f32[32,64,127]{2,1,0:T(8,128)}, f32[32,64,127]{2,1,0:T(8,128)}) fusion(f32[32,64,128]{2,1,0:T(8,128)S(1)} %fusion.19, f32[32,64,128]{2,1,0:T(8,128)S(1)} %get-tuple-element.133), kind=kLoop, calls=%fused_computation.220 | loop fusion | bytes 8323072 | tf_op jit(solution)/shard_map/slice | solution.py:56
  37.8 1.5 fusion.99
  40.6 2.8 %fusion.90 = (f32[32,64,127]{2,1,0:T(8,128)}, f32[32,64,127]{2,1,0:T(8,128)}, f32[32,64,127]{2,1,0:T(8,128)}, f32[32,64,127]{2,1,0:T(8,128)}) fusion(f32[32,64,128]{2,1,0:T(8,128)S(1)} %get-tuple-element.130, f32[32,64,128]{2,1,0:T(8,128)S(1)} %get-tuple-element.131), kind=kLoop, calls=%fused_computation.213 | loop fusion | bytes 8323072 | tf_op jit(solution)/shard_map/slice | solution.py:56
  45.5 1.4 slice_bitcast_fusion.5
  49.1 1.4 copy.610
  50.4 1.4 copy.611
  51.9 1.4 copy.608
  53.2 1.4 copy.609
  56.0 1.5 rev.15
  60.7 6.0 %fusion.87 = (f32[64,128]{1,0:T(8,128)S(1)}, f32[32,64,128]{2,1,0:T(8,128)}) fusion(f32[32,63,128]{2,1,0:T(8,128)S(1)} %copy-done.1, f32[32,1,128]{2,1,0:T(1,128)S(1)} %get-tuple-element.95, f32[32,1,128]{2,1,0:T(1,128)S(1)} %get-tuple-element.91, f32[32,63,128]{2,1,0:T(8,128)} %get-tuple-element.155, f32[32,64,127]{2,1,0:T(8,128)} %get-tuple-element.63, ...), kind=kLoop, calls=%fused_computation.211 | loop fusion | flops 6021120 | bytes 9502976 | tf_op jit(solution)/shard_map/reduce_sum | solution.py:141
  68.0 3.8 %fusion.85 = (f32[64,128]{1,0:T(8,128)S(1)}, f32[32,64,128]{2,1,0:T(8,128)}) fusion(f32[32,63,128]{2,1,0:T(8,128)S(1)} %copy-done.12, f32[32,1,128]{2,1,0:T(1,128)S(1)} %get-tuple-element.97, f32[32,1,128]{2,1,0:T(1,128)S(1)} %get-tuple-element.93, f32[32,63,128]{2,1,0:T(8,128)S(1)} %copy-done.11, f32[32,64,127]{2,1,0:T(8,128)S(1)} %copy-done.5, ...), kind=kLoop, calls=%fused_computation.210 | loop fusion | flops 6021120 | bytes 9502976 | tf_op jit(solution)/shard_map/reduce_sum | solution.py:140
  74.1 4.3 %collective-permute-start.9 = (f32[2,1,128]{2,1,0:T(1,128)S(1)}, f32[2,1,128]{2,1,0:T(1,128)S(1)}, u32[]{:S(2)}, u32[]{:S(2)}) collective-permute-start(f32[2,1,128]{2,1,0:T(1,128)S(1)} %pad_maximum_fusion.19), channel_id=1, source_target_pairs={{0,1},{1,2},{2,3},{3,4},{4,5},{5,6},{6,7},{8,9},{9,10},{10,11},{11... | collective-permute-start | bytes 3080 | tf_op jit(solution)/shard_map/ppermute | solution.py:41
  78.9 4.3 %collective-permute-start.5 = (f32[2,64]{1,0:T(2,128)S(1)}, f32[2,64]{1,0:T(2,128)S(1)}, u32[]{:S(2)}, u32[]{:S(2)}) collective-permute-start(f32[2,64]{1,0:T(2,128)S(1)} %pad_maximum_fusion.17), channel_id=1, source_target_pairs={{8,0},{16,8},{24,16},{32,24},{40,32},{48,40},{56,48},{64,56},{72,6... | collective-permute-start | bytes 1544 | tf_op jit(solution)/shard_map/ppermute | solution.py:38
  83.2 1.3 collective-permute-start.8
  85.8 3.1 %collective-permute-done.6 = f32[2,64]{1,0:T(2,128)S(1)} collective-permute-done((f32[2,64]{1,0:T(2,128)S(1)}, f32[2,64]{1,0:T(2,128)S(1)}, u32[]{:S(2)}, u32[]{:S(2)}) %collective-permute-start.6) | collective-permute-done | bytes 544 | tf_op jit(solution)/shard_map/ppermute | solution.py:39
  91.0 1.7 multiply_bitcast_fusion.9
  94.2 1.3 collective-permute-start.13
  95.5 6.0 %collective-permute-start.10 = (f32[64]{0:T(128)S(1)}, f32[64]{0:T(128)S(1)}, u32[]{:S(2)}, u32[]{:S(2)}) collective-permute-start(f32[64]{0:T(128)S(1)} %get-tuple-element.19), channel_id=1, source_target_pairs={{8,0},{16,8},{24,16},{32,24},{40,32},{48,40},{56,48},{64,56},{72,6... | collective-permute-start | bytes 776 | tf_op jit(solution)/shard_map/ppermute | solution.py:38
  102.2 4.3 %collective-permute-start.14 = (f32[1,128]{1,0:T(1,128)S(1)}, f32[1,128]{1,0:T(1,128)S(1)}, u32[]{:S(2)}, u32[]{:S(2)}) collective-permute-start(f32[1,128]{1,0:T(1,128)S(1)} %get-tuple-element.119), channel_id=1, source_target_pairs={{0,1},{1,2},{2,3},{3,4},{4,5},{5,6},{6,7},{8,9},{9,10},{10,11},{11... | collective-permute-start | bytes 1544 | tf_op jit(solution)/shard_map/ppermute | solution.py:41
  110.1 16.9 %all-to-all-start = ((f32[128,1,2]{2,1,0:T(1,128)}), f32[128,1,2]{2,1,0:T(1,128)S(1)}, u32[]{:S(2)}, u32[]{:S(2)}) async-start(f32[128,1,2]{2,1,0:T(1,128)} %broadcast_in_dim.95), calls=%async_computation | async-start | bytes 131072 | tf_op jit(solution)/shard_map/all_to_all | solution.py:21
  127.0 2.1 fusion.91
  129.1 1.4 copy.614
  130.5 1.4 copy.615
  131.9 1.4 copy.612
  133.4 1.5 copy.613
  134.8 1.8 all-to-all-done
  137.2 1.4 fusion.117
  142.8 1.3 collective-permute-start.18
  146.6 4.5 %collective-permute-start.19 = (f32[1,128]{1,0:T(1,128)S(1)}, f32[1,128]{1,0:T(1,128)}, u32[]{:S(2)}, u32[]{:S(2)}) collective-permute-start(f32[1,128]{1,0:T(1,128)S(1)} %get-tuple-element.113), channel_id=1, source_target_pairs={{0,1},{1,2},{2,3},{3,4},{4,5},{5,6},{6,7},{8,9},{9,10},{10,11},{11... | collective-permute-start | bytes 1544 | tf_op jit(solution)/shard_map/ppermute | solution.py:41
  155.2 13.0 %all-to-all-start.1 = ((f32[128,1,4]{2,1,0:T(1,128)}), f32[128,1,4]{2,1,0:T(1,128)}, u32[]{:S(2)}, u32[]{:S(2)}) async-start(f32[128,1,4]{2,1,0:T(1,128)} %broadcast_in_dim.98), calls=%async_computation.1 | async-start | bytes 131072 | tf_op jit(solution)/shard_map/all_to_all | solution.py:21
  168.2 6.0 %add_multiply_fusion = f32[32,64,128]{2,1,0:T(8,128)} fusion(f32[32,64,128]{2,1,0:T(8,128)S(1)} %get-tuple-element.130, f32[32,63,128]{2,1,0:T(8,128)} %get-tuple-element.55, f32[32,1,128]{2,1,0:T(1,128)} %get-tuple-element.94, f32[32,1,128]{2,1,0:T(1,128)S(1)} %copy-done.31, f32[32,63,128]{2,1,0:T(8,128)} %get-tuple-element.54, ...), kind=kLoop, calls=%fused_computation.43 | loop fusion | flops 7077888 | bytes 10518528 | tf_op jit(solution)/shard_map/mul | solution.py:138
  174.3 3.4 %all-to-all-done.1 = f32[128,1,4]{2,1,0:T(1,128)} async-done(((f32[128,1,4]{2,1,0:T(1,128)}), f32[128,1,4]{2,1,0:T(1,128)}, u32[]{:S(2)}, u32[]{:S(2)}) %all-to-all-start.1) | async-done | bytes 2080 | tf_op jit(solution)/shard_map/all_to_all | solution.py:21
  183.9 1.4 multiply_bitcast_fusion.3
  187.4 1.3 collective-permute-start.23
  191.1 4.6 %collective-permute-start.24 = (f32[1,128]{1,0:T(1,128)S(1)}, f32[1,128]{1,0:T(1,128)}, u32[]{:S(2)}, u32[]{:S(2)}) collective-permute-start(f32[1,128]{1,0:T(1,128)S(1)} %get-tuple-element.106), channel_id=1, source_target_pairs={{0,1},{1,2},{2,3},{3,4},{4,5},{5,6},{6,7},{8,9},{9,10},{10,11},{11... | collective-permute-start | bytes 1544 | tf_op jit(solution)/shard_map/ppermute | solution.py:41
  199.7 11.1 %all-to-all-start.2 = ((f32[128,1,4]{2,1,0:T(1,128)}), f32[128,1,4]{2,1,0:T(1,128)S(1)}, u32[]{:S(2)}, u32[]{:S(2)}) async-start(f32[128,1,4]{2,1,0:T(1,128)} %broadcast_in_dim.101), calls=%async_computation.2 | async-start | bytes 131072 | tf_op jit(solution)/shard_map/all_to_all | solution.py:21
  210.8 5.7 %add_multiply_fusion.1 = f32[32,64,128]{2,1,0:T(8,128)} fusion(f32[32,64,128]{2,1,0:T(8,128)S(1)} %get-tuple-element.131, f32[32,63,128]{2,1,0:T(8,128)} %get-tuple-element.150, f32[32,1,128]{2,1,0:T(1,128)S(1)} %copy-done.30, f32[32,1,128]{2,1,0:T(1,128)S(1)} %copy-done.29, f32[32,63,128]{2,1,0:T(8,128)} %get-tuple-element.151, ...), kind=kLoop, calls=%fused_computation.44 | loop fusion | flops 7077888 | bytes 10518528 | tf_op jit(solution)/shard_map/mul | solution.py:138
  216.5 3.9 %all-to-all-done.2 = f32[128,1,4]{2,1,0:T(1,128)S(1)} async-done(((f32[128,1,4]{2,1,0:T(1,128)}), f32[128,1,4]{2,1,0:T(1,128)S(1)}, u32[]{:S(2)}, u32[]{:S(2)}) %all-to-all-start.2) | async-done | bytes 2080 | tf_op jit(solution)/shard_map/all_to_all | solution.py:21
  (222 shorter events, 57.5 us)
Async XLA Ops:
  10.4 45.7 %collective-permute-start.2 = (f32[129,1,128]{2,1,0:T(1,128)}, f32[129,1,128]{2,1,0:T(1,128)}, u32[]{:S(2)}, u32[]{:S(2)}) collective-permute-start(f32[129,1,128]{2,1,0:T(1,128)} %get-tuple-element.129), channel_id=1, source_target_pairs={{7,127},{15,119},{23,111},{31,103},{39,95},{47,87},{55,79},{63,71}... | collective-permute-start | bytes 198152 | tf_op jit(solution)/shard_map/ppermute | solution.py:43
  11.7 47.7 %collective-permute-start.4 = (f32[129,1,128]{2,1,0:T(1,128)}, f32[129,1,128]{2,1,0:T(1,128)S(1)}, u32[]{:S(2)}, u32[]{:S(2)}) collective-permute-start(f32[129,1,128]{2,1,0:T(1,128)} %get-tuple-element.129), channel_id=1, source_target_pairs={{0,1},{1,2},{2,3},{3,4},{4,5},{5,6},{6,7},{8,9},{9,10},{10,11},{11... | collective-permute-start | bytes 198152 | tf_op jit(solution)/shard_map/ppermute | solution.py:41
  15.6 42.0 %collective-permute-start.3 = (f32[129,1,128]{2,1,0:T(1,128)}, f32[129,1,128]{2,1,0:T(1,128)}, u32[]{:S(2)}, u32[]{:S(2)}) collective-permute-start(f32[129,1,128]{2,1,0:T(1,128)} %get-tuple-element.128), channel_id=1, source_target_pairs={{1,0},{2,1},{3,2},{4,3},{5,4},{6,5},{7,6},{9,8},{10,9},{11,10},{12... | collective-permute-start | bytes 198152 | tf_op jit(solution)/shard_map/ppermute | solution.py:40
  25.7 17.7 %collective-permute-start = (f32[129,64]{1,0:T(8,128)}, f32[129,64]{1,0:T(8,128)S(1)}, u32[]{:S(2)}, u32[]{:S(2)}) collective-permute-start(f32[129,64]{1,0:T(8,128)} %dynamic-update-slice.19), channel_id=1, source_target_pairs={{8,0},{16,8},{24,16},{32,24},{40,32},{48,40},{56,48},{64,56},{72,6... | collective-permute-start | bytes 99080 | tf_op jit(solution)/shard_map/ppermute | solution.py:38
  28.6 16.9 %collective-permute-start.1 = (f32[129,64]{1,0:T(8,128)}, f32[129,64]{1,0:T(8,128)}, u32[]{:S(2)}, u32[]{:S(2)}) collective-permute-start(f32[129,64]{1,0:T(8,128)} %dynamic-update-slice.14), channel_id=1, source_target_pairs={{0,8},{8,16},{16,24},{24,32},{32,40},{40,48},{48,56},{56,64},{64,7... | collective-permute-start | bytes 99080 | tf_op jit(solution)/shard_map/ppermute | solution.py:39
  53.2 7.3 %copy-start.1 = (f32[32,63,128]{2,1,0:T(8,128)S(1)}, f32[32,63,128]{2,1,0:T(8,128)}, u32[]{:S(2)}) copy-start(f32[32,63,128]{2,1,0:T(8,128)} %get-tuple-element.154) | copy-start | bytes 3096580
  60.6 6.3 %copy-start.3 = (f32[32,64,1]{2,1,0:T(8,128)S(1)}, f32[32,64,1]{2,1,0:T(8,128)}, u32[]{:S(2)}) copy-start(f32[32,64,1]{2,1,0:T(8,128)} %copy.608) | copy-start | bytes 24580
  60.6 6.3 %copy-start.4 = (f32[32,64,1]{2,1,0:T(8,128)S(1)}, f32[32,64,1]{2,1,0:T(8,128)}, u32[]{:S(2)}) copy-start(f32[32,64,1]{2,1,0:T(8,128)} %copy.609) | copy-start | bytes 24580
  60.6 6.3 %copy-start.5 = (f32[32,64,127]{2,1,0:T(8,128)S(1)}, f32[32,64,127]{2,1,0:T(8,128)}, u32[]{:S(2)}) copy-start(f32[32,64,127]{2,1,0:T(8,128)} %get-tuple-element.152) | copy-start | bytes 3121156
  60.6 6.3 %copy-start.6 = (f32[32,64,127]{2,1,0:T(8,128)S(1)}, f32[32,64,127]{2,1,0:T(8,128)}, u32[]{:S(2)}) copy-start(f32[32,64,127]{2,1,0:T(8,128)} %get-tuple-element.153) | copy-start | bytes 3121156
  60.6 6.3 %copy-start.7 = (f32[32,64,128]{2,1,0:T(8,128)S(1)}, f32[32,64,128]{2,1,0:T(8,128)}, u32[]{:S(2)}) copy-start(f32[32,64,128]{2,1,0:T(8,128)} %param.9) | copy-start | bytes 3145732
  60.6 6.3 %copy-start.8 = (f32[32,64,128]{2,1,0:T(8,128)S(1)}, f32[32,64,128]{2,1,0:T(8,128)}, u32[]{:S(2)}) copy-start(f32[32,64,128]{2,1,0:T(8,128)} %param.8) | copy-start | bytes 3145732
  60.6 6.3 %copy-start.9 = (f32[32,64,1]{2,1,0:T(8,128)S(1)}, f32[32,64,1]{2,1,0:T(8,128)}, u32[]{:S(2)}) copy-start(f32[32,64,1]{2,1,0:T(8,128)} %fusion.118) | copy-start | bytes 24580
  60.6 6.3 %copy-start.10 = (f32[32,64,1]{2,1,0:T(8,128)S(1)}, f32[32,64,1]{2,1,0:T(8,128)}, u32[]{:S(2)}) copy-start(f32[32,64,1]{2,1,0:T(8,128)} %fusion.119) | copy-start | bytes 24580
  60.6 6.8 %copy-start.11 = (f32[32,63,128]{2,1,0:T(8,128)S(1)}, f32[32,63,128]{2,1,0:T(8,128)}, u32[]{:S(2)}) copy-start(f32[32,63,128]{2,1,0:T(8,128)} %get-tuple-element.70) | copy-start | bytes 3096580
  60.6 7.1 %copy-start.12 = (f32[32,63,128]{2,1,0:T(8,128)S(1)}, f32[32,63,128]{2,1,0:T(8,128)}, u32[]{:S(2)}) copy-start(f32[32,63,128]{2,1,0:T(8,128)} %get-tuple-element.71) | copy-start | bytes 3096580
  60.7 7.4 %copy-start.13 = (f32[32,64,127]{2,1,0:T(8,128)S(1)}, f32[32,64,127]{2,1,0:T(8,128)}, u32[]{:S(2)}) copy-start(f32[32,64,127]{2,1,0:T(8,128)} %get-tuple-element.66) | copy-start | bytes 3121156
  73.4 16.2 %collective-permute-start.7 = (f32[2,1,128]{2,1,0:T(1,128)S(1)}, f32[2,1,128]{2,1,0:T(1,128)S(1)}, u32[]{:S(2)}, u32[]{:S(2)}) collective-permute-start(f32[2,1,128]{2,1,0:T(1,128)S(1)} %pad_maximum_fusion.19), channel_id=1, source_target_pairs={{7,127},{15,119},{23,111},{31,103},{39,95},{47,87},{55,79},{63,71}... | collective-permute-start | bytes 3080 | tf_op jit(solution)/shard_map/ppermute | solution.py:43
  74.1 15.7 %collective-permute-start.9 = (f32[2,1,128]{2,1,0:T(1,128)S(1)}, f32[2,1,128]{2,1,0:T(1,128)S(1)}, u32[]{:S(2)}, u32[]{:S(2)}) collective-permute-start(f32[2,1,128]{2,1,0:T(1,128)S(1)} %pad_maximum_fusion.19), channel_id=1, source_target_pairs={{0,1},{1,2},{2,3},{3,4},{4,5},{5,6},{6,7},{8,9},{9,10},{10,11},{11... | collective-permute-start | bytes 3080 | tf_op jit(solution)/shard_map/ppermute | solution.py:41
  78.9 6.2 %collective-permute-start.5 = (f32[2,64]{1,0:T(2,128)S(1)}, f32[2,64]{1,0:T(2,128)S(1)}, u32[]{:S(2)}, u32[]{:S(2)}) collective-permute-start(f32[2,64]{1,0:T(2,128)S(1)} %pad_maximum_fusion.17), channel_id=1, source_target_pairs={{8,0},{16,8},{24,16},{32,24},{40,32},{48,40},{56,48},{64,56},{72,6... | collective-permute-start | bytes 1544 | tf_op jit(solution)/shard_map/ppermute | solution.py:38
  83.2 5.7 %collective-permute-start.6 = (f32[2,64]{1,0:T(2,128)S(1)}, f32[2,64]{1,0:T(2,128)S(1)}, u32[]{:S(2)}, u32[]{:S(2)}) collective-permute-start(f32[2,64]{1,0:T(2,128)S(1)} %pad_maximum_fusion.18), channel_id=1, source_target_pairs={{0,8},{8,16},{16,24},{24,32},{32,40},{40,48},{48,56},{56,64},{64,7... | collective-permute-start | bytes 1544 | tf_op jit(solution)/shard_map/ppermute | solution.py:39
  83.2 6.6 %collective-permute-start.8 = (f32[2,1,128]{2,1,0:T(1,128)S(1)}, f32[2,1,128]{2,1,0:T(1,128)S(1)}, u32[]{:S(2)}, u32[]{:S(2)}) collective-permute-start(f32[2,1,128]{2,1,0:T(1,128)S(1)} %pad_maximum_fusion.20), channel_id=1, source_target_pairs={{1,0},{2,1},{3,2},{4,3},{5,4},{6,5},{7,6},{9,8},{10,9},{11,10},{12... | collective-permute-start | bytes 3080 | tf_op jit(solution)/shard_map/ppermute | solution.py:40
  93.6 13.1 %collective-permute-start.12 = (f32[1,128]{1,0:T(1,128)S(1)}, f32[1,128]{1,0:T(1,128)S(1)}, u32[]{:S(2)}, u32[]{:S(2)}) collective-permute-start(f32[1,128]{1,0:T(1,128)S(1)} %get-tuple-element.119), channel_id=1, source_target_pairs={{7,127},{15,119},{23,111},{31,103},{39,95},{47,87},{55,79},{63,71}... | collective-permute-start | bytes 1544 | tf_op jit(solution)/shard_map/ppermute | solution.py:43
  94.2 12.5 %collective-permute-start.13 = (f32[1,128]{1,0:T(1,128)S(1)}, f32[1,128]{1,0:T(1,128)S(1)}, u32[]{:S(2)}, u32[]{:S(2)}) collective-permute-start(f32[1,128]{1,0:T(1,128)S(1)} %get-tuple-element.118), channel_id=1, source_target_pairs={{1,0},{2,1},{3,2},{4,3},{5,4},{6,5},{7,6},{9,8},{10,9},{11,10},{12... | collective-permute-start | bytes 1544 | tf_op jit(solution)/shard_map/ppermute | solution.py:40
  95.5 10.9 %collective-permute-start.10 = (f32[64]{0:T(128)S(1)}, f32[64]{0:T(128)S(1)}, u32[]{:S(2)}, u32[]{:S(2)}) collective-permute-start(f32[64]{0:T(128)S(1)} %get-tuple-element.19), channel_id=1, source_target_pairs={{8,0},{16,8},{24,16},{32,24},{40,32},{48,40},{56,48},{64,56},{72,6... | collective-permute-start | bytes 776 | tf_op jit(solution)/shard_map/ppermute | solution.py:38
  101.6 5.0 %collective-permute-start.11 = (f32[64]{0:T(128)S(1)}, f32[64]{0:T(128)S(1)}, u32[]{:S(2)}, u32[]{:S(2)}) collective-permute-start(f32[64]{0:T(128)S(1)} %get-tuple-element.18), channel_id=1, source_target_pairs={{0,8},{8,16},{16,24},{24,32},{32,40},{40,48},{48,56},{56,64},{64,7... | collective-permute-start | bytes 776 | tf_op jit(solution)/shard_map/ppermute | solution.py:39
  102.2 5.0 %collective-permute-start.14 = (f32[1,128]{1,0:T(1,128)S(1)}, f32[1,128]{1,0:T(1,128)S(1)}, u32[]{:S(2)}, u32[]{:S(2)}) collective-permute-start(f32[1,128]{1,0:T(1,128)S(1)} %get-tuple-element.119), channel_id=1, source_target_pairs={{0,1},{1,2},{2,3},{3,4},{4,5},{5,6},{6,7},{8,9},{9,10},{10,11},{11... | collective-permute-start | bytes 1544 | tf_op jit(solution)/shard_map/ppermute | solution.py:41
  110.1 26.5 %all-to-all-start = ((f32[128,1,2]{2,1,0:T(1,128)}), f32[128,1,2]{2,1,0:T(1,128)S(1)}, u32[]{:S(2)}, u32[]{:S(2)}) async-start(f32[128,1,2]{2,1,0:T(1,128)} %broadcast_in_dim.95), calls=%async_computation | async-start | bytes 131072 | tf_op jit(solution)/shard_map/all_to_all | solution.py:21
  134.8 5.3 %copy-start.22 = (f32[64,128]{1,0:T(8,128)S(1)}, f32[64,128]{1,0:T(8,128)}, u32[]{:S(2)}) copy-start(f32[64,128]{1,0:T(8,128)} %get-tuple-element.38) | copy-start | bytes 98308
  141.6 10.3 %collective-permute-start.17 = (f32[1,128]{1,0:T(1,128)S(1)}, f32[1,128]{1,0:T(1,128)}, u32[]{:S(2)}, u32[]{:S(2)}) collective-permute-start(f32[1,128]{1,0:T(1,128)S(1)} %get-tuple-element.113), channel_id=1, source_target_pairs={{7,127},{15,119},{23,111},{31,103},{39,95},{47,87},{55,79},{63,71}... | collective-permute-start | bytes 1544 | tf_op jit(solution)/shard_map/ppermute | solution.py:43
  142.8 9.8 %collective-permute-start.18 = (f32[1,128]{1,0:T(1,128)S(1)}, f32[1,128]{1,0:T(1,128)S(1)}, u32[]{:S(2)}, u32[]{:S(2)}) collective-permute-start(f32[1,128]{1,0:T(1,128)S(1)} %get-tuple-element.112), channel_id=1, source_target_pairs={{1,0},{2,1},{3,2},{4,3},{5,4},{6,5},{7,6},{9,8},{10,9},{11,10},{12... | collective-permute-start | bytes 1544 | tf_op jit(solution)/shard_map/ppermute | solution.py:40
  144.1 7.0 %collective-permute-start.15 = (f32[64]{0:T(128)S(1)}, f32[64]{0:T(128)S(1)}, u32[]{:S(2)}, u32[]{:S(2)}) collective-permute-start(f32[64]{0:T(128)S(1)} %get-tuple-element.17), channel_id=1, source_target_pairs={{8,0},{16,8},{24,16},{32,24},{40,32},{48,40},{56,48},{64,56},{72,6... | collective-permute-start | bytes 776 | tf_op jit(solution)/shard_map/ppermute | solution.py:38
  145.0 6.3 %collective-permute-start.16 = (f32[64]{0:T(128)S(1)}, f32[64]{0:T(128)S(1)}, u32[]{:S(2)}, u32[]{:S(2)}) collective-permute-start(f32[64]{0:T(128)S(1)} %get-tuple-element.16), channel_id=1, source_target_pairs={{0,8},{8,16},{16,24},{24,32},{32,40},{40,48},{48,56},{56,64},{64,7... | collective-permute-start | bytes 776 | tf_op jit(solution)/shard_map/ppermute | solution.py:39
  146.6 6.1 %collective-permute-start.19 = (f32[1,128]{1,0:T(1,128)S(1)}, f32[1,128]{1,0:T(1,128)}, u32[]{:S(2)}, u32[]{:S(2)}) collective-permute-start(f32[1,128]{1,0:T(1,128)S(1)} %get-tuple-element.113), channel_id=1, source_target_pairs={{0,1},{1,2},{2,3},{3,4},{4,5},{5,6},{6,7},{8,9},{9,10},{10,11},{11... | collective-permute-start | bytes 1544 | tf_op jit(solution)/shard_map/ppermute | solution.py:41
  155.2 13.1 %copy-start.17 = (f32[32,1,128]{2,1,0:T(1,128)S(1)}, f32[32,1,128]{2,1,0:T(1,128)}, u32[]{:S(2)}) copy-start(f32[32,1,128]{2,1,0:T(1,128)} %copy-done.16) | copy-start | bytes 49156
  155.2 13.1 %copy-start.31 = (f32[32,1,128]{2,1,0:T(1,128)S(1)}, f32[32,1,128]{2,1,0:T(1,128)}, u32[]{:S(2)}) copy-start(f32[32,1,128]{2,1,0:T(1,128)} %get-tuple-element.90) | copy-start | bytes 49156
  155.2 22.4 %all-to-all-start.1 = ((f32[128,1,4]{2,1,0:T(1,128)}), f32[128,1,4]{2,1,0:T(1,128)}, u32[]{:S(2)}, u32[]{:S(2)}) async-start(f32[128,1,4]{2,1,0:T(1,128)} %broadcast_in_dim.98), calls=%async_computation.1 | async-start | bytes 131072 | tf_op jit(solution)/shard_map/all_to_all | solution.py:21
  174.2 36.5 %copy-start.2 = (f32[32,63,128]{2,1,0:T(8,128)S(1)}, f32[32,63,128]{2,1,0:T(8,128)}, u32[]{:S(2)}) copy-start(f32[32,63,128]{2,1,0:T(8,128)} %get-tuple-element.155) | copy-start | bytes 3096580
  186.2 10.3 %collective-permute-start.22 = (f32[1,128]{1,0:T(1,128)S(1)}, f32[1,128]{1,0:T(1,128)}, u32[]{:S(2)}, u32[]{:S(2)}) collective-permute-start(f32[1,128]{1,0:T(1,128)S(1)} %get-tuple-element.106), channel_id=1, source_target_pairs={{7,127},{15,119},{23,111},{31,103},{39,95},{47,87},{55,79},{63,71}... | collective-permute-start | bytes 1544 | tf_op jit(solution)/shard_map/ppermute | solution.py:43
  187.4 9.8 %collective-permute-start.23 = (f32[1,128]{1,0:T(1,128)S(1)}, f32[1,128]{1,0:T(1,128)S(1)}, u32[]{:S(2)}, u32[]{:S(2)}) collective-permute-start(f32[1,128]{1,0:T(1,128)S(1)} %get-tuple-element.105), channel_id=1, source_target_pairs={{1,0},{2,1},{3,2},{4,3},{5,4},{6,5},{7,6},{9,8},{10,9},{11,10},{12... | collective-permute-start | bytes 1544 | tf_op jit(solution)/shard_map/ppermute | solution.py:40
  188.6 7.0 %collective-permute-start.20 = (f32[64]{0:T(128)S(1)}, f32[64]{0:T(128)S(1)}, u32[]{:S(2)}, u32[]{:S(2)}) collective-permute-start(f32[64]{0:T(128)S(1)} %get-tuple-element.15), channel_id=1, source_target_pairs={{8,0},{16,8},{24,16},{32,24},{40,32},{48,40},{56,48},{64,56},{72,6... | collective-permute-start | bytes 776 | tf_op jit(solution)/shard_map/ppermute | solution.py:38
  189.6 6.2 %collective-permute-start.21 = (f32[64]{0:T(128)S(1)}, f32[64]{0:T(128)S(1)}, u32[]{:S(2)}, u32[]{:S(2)}) collective-permute-start(f32[64]{0:T(128)S(1)} %get-tuple-element.14), channel_id=1, source_target_pairs={{0,8},{8,16},{16,24},{24,32},{32,40},{40,48},{48,56},{56,64},{64,7... | collective-permute-start | bytes 776 | tf_op jit(solution)/shard_map/ppermute | solution.py:39
  191.1 6.1 %collective-permute-start.24 = (f32[1,128]{1,0:T(1,128)S(1)}, f32[1,128]{1,0:T(1,128)}, u32[]{:S(2)}, u32[]{:S(2)}) collective-permute-start(f32[1,128]{1,0:T(1,128)S(1)} %get-tuple-element.106), channel_id=1, source_target_pairs={{0,1},{1,2},{2,3},{3,4},{4,5},{5,6},{6,7},{8,9},{9,10},{10,11},{11... | collective-permute-start | bytes 1544 | tf_op jit(solution)/shard_map/ppermute | solution.py:41
  199.7 11.1 %copy-start.18 = (f32[32,1,128]{2,1,0:T(1,128)S(1)}, f32[32,1,128]{2,1,0:T(1,128)}, u32[]{:S(2)}) copy-start(f32[32,1,128]{2,1,0:T(1,128)} %copy-done.16) | copy-start | bytes 49156
  199.7 11.1 %copy-start.29 = (f32[32,1,128]{2,1,0:T(1,128)S(1)}, f32[32,1,128]{2,1,0:T(1,128)}, u32[]{:S(2)}) copy-start(f32[32,1,128]{2,1,0:T(1,128)} %get-tuple-element.92) | copy-start | bytes 49156
  199.7 11.1 %copy-start.30 = (f32[32,1,128]{2,1,0:T(1,128)S(1)}, f32[32,1,128]{2,1,0:T(1,128)}, u32[]{:S(2)}) copy-start(f32[32,1,128]{2,1,0:T(1,128)} %get-tuple-element.96) | copy-start | bytes 49156
  199.7 20.7 %all-to-all-start.2 = ((f32[128,1,4]{2,1,0:T(1,128)}), f32[128,1,4]{2,1,0:T(1,128)S(1)}, u32[]{:S(2)}, u32[]{:S(2)}) async-start(f32[128,1,4]{2,1,0:T(1,128)} %broadcast_in_dim.101), calls=%async_computation.2 | async-start | bytes 131072 | tf_op jit(solution)/shard_map/all_to_all | solution.py:21
  220.4 4.7 %copy-start.15 = (f32[64,128]{1,0:T(8,128)S(1)}, f32[64,128]{1,0:T(8,128)}, u32[]{:S(2)}) copy-start(f32[64,128]{1,0:T(8,128)} %get-tuple-element.33) | copy-start | bytes 98308
  (22 other events, 24.8 us)

commit v4 on v3

--- a/solution.py
+++ b/solution.py
@@ -2,6 +2,10 @@
 import jax.numpy as jnp
 from jax import lax
 from jax.sharding import PartitionSpec as P
+from jax.experimental import pallas as pl
+from jax.experimental.pallas import tpu as pltpu
+
+INTERPRET = False
 
 BLK = 16
 ITERS = 3
@@ -22,19 +26,9 @@
     return jnp.sum(gathered, axis=0)
 
 
-def halos(cells, parity):
-    if not isinstance(cells, (list, tuple)):
-        cells = [cells]
+def exchange(first_col, last_col, first_row, last_row, parity):
     lon_count = lax.axis_size("lon")
     lat_count = lax.axis_size("lat")
-
-    def edge(index):
-        return jnp.concatenate([item[index] for item in cells], axis=0)
-
-    first_col = edge((Ellipsis, slice(None), 0))
-    last_col = edge((Ellipsis, slice(None), -1))
-    first_row = edge((Ellipsis, slice(0, 1), slice(None)))
-    last_row = edge((Ellipsis, slice(-1, None), slice(None)))
     east = lax.ppermute(first_col, "lon", [((i + 1) % lon_count, i) for i in range(lon_count)])
     west = lax.ppermute(last_col, "lon", [(i, (i + 1) % lon_count) for i in range(lon_count)])
     north = lax.ppermute(first_row, "lat", [(i + 1, i) for i in range(lat_count - 1)])
@@ -50,14 +44,108 @@
     return east, west, north, south
 
 
+def halos(cells, parity):
+    return exchange(cells[..., :, 0], cells[..., :, -1], cells[..., 0, :], cells[..., -1, :], parity)
+
+
 def around(cells, halo):
     east, west, north, south = halo
     return (
         jnp.concatenate([cells[..., :, 1:], east[..., None]], axis=-1),
         jnp.concatenate([west[..., None], cells[..., :, :-1]], axis=-1),
-        jnp.concatenate([cells[..., 1:, :], north], axis=-2),
-        jnp.concatenate([south, cells[..., :-1, :]], axis=-2),
-    )
+        jnp.concatenate([cells[..., 1:, :], north[..., None, :]], axis=-2),
+        jnp.concatenate([south[..., None, :], cells[..., :-1, :]], axis=-2),
+    )
+
+
+def column_kernel(
+    u_ref, v_ref, t_ref, s_ref, m_ref, f_ref, he_ref, hw_ref, hn_ref, hs_ref,
+    un_ref, vn_ref, tn_ref, sn_ref, um_ref, vm_ref,
+):
+    levels, height, breadth = u_ref.shape
+    marine = m_ref[...]
+    coriolis = f_ref[...]
+    row = lax.broadcasted_iota(jnp.int32, (height, breadth), 0)
+    col = lax.broadcasted_iota(jnp.int32, (height, breadth), 1)
+    last_row = row == height - 1
+    first_row = row == 0
+    last_col = col == breadth - 1
+    first_col = col == 0
+
+    def near(q, e, w, n, s):
+        return (
+            jnp.where(last_col, e, pltpu.roll(q, breadth - 1, 1)),
+            jnp.where(first_col, w, pltpu.roll(q, 1, 1)),
+            jnp.where(last_row, n, pltpu.roll(q, height - 1, 0)),
+            jnp.where(first_row, s, pltpu.roll(q, 1, 0)),
+        )
+
+    def side(index):
+        return he_ref[index], hw_ref[index], hn_ref[index], hs_ref[index]
+
+    def body(level, carry):
+        pressure, pe, pw, pn, ps, zonal_sum, merid_sum = carry
+        zonal = u_ref[level] * marine
+        merid = v_ref[level] * marine
+        enthalpy_content = t_ref[level] * marine
+        salt = s_ref[level] * marine
+        halo_u = side(level)
+        halo_v = side(levels + level)
+        halo_t = side(2 * levels + level)
+        halo_s = side(3 * levels + level)
+        pressure = pressure + (haline * salt - thermal * enthalpy_content)
+        pe = pe + (haline * halo_s[0] - thermal * halo_t[0])
+        pw = pw + (haline * halo_s[1] - thermal * halo_t[1])
+        pn = pn + (haline * halo_s[2] - thermal * halo_t[2])
+        ps = ps + (haline * halo_s[3] - thermal * halo_t[3])
+        near_p = near(pressure, pe, pw, pn, ps)
+        near_u = near(zonal, *halo_u)
+        near_v = near(merid, *halo_v)
+        near_t = near(enthalpy_content, *halo_t)
+        near_s = near(salt, *halo_s)
+        zonal_new = marine * (
+            zonal
+            + time_step
+            * (coriolis * merid - 0.5 * (near_p[0] - near_p[1]) + viscosity * laplace(zonal, near_u))
+        )
+        merid_new = marine * (
+            merid
+            + time_step
+            * (-coriolis * zonal - 0.5 * (near_p[2] - near_p[3]) + viscosity * laplace(merid, near_v))
+        )
+        un_ref[level] = zonal_new
+        vn_ref[level] = merid_new
+        for tracer, near_q, out_ref in ((enthalpy_content, near_t, tn_ref), (salt, near_s, sn_ref)):
+            flux = 0.5 * (
+                near_u[0] * near_q[0]
+                - near_u[1] * near_q[1]
+                + near_v[2] * near_q[2]
+                - near_v[3] * near_q[3]
+            )
+            out_ref[level] = marine * (
+                tracer + time_step * (-flux + diffusivity * laplace(tracer, near_q))
+            )
+        return pressure, pe, pw, pn, ps, zonal_sum + zonal_new, merid_sum + merid_new
+
+    blank = jnp.zeros((height, breadth), jnp.float32)
+    blank_col = jnp.zeros((height, 1), jnp.float32)
+    blank_row = jnp.zeros((1, breadth), jnp.float32)
+    carry = lax.fori_loop(
+        0, levels, body, (blank, blank_col, blank_col, blank_row, blank_row, blank, blank)
+    )
+    um_ref[...] = carry[5] / levels
+    vm_ref[...] = carry[6] / levels
+
+
+def column_step(u, v, t, s, marine, coriolis, he, hw, hn, hs):
+    levels, height, breadth = u.shape
+    field = jax.ShapeDtypeStruct((levels, height, breadth), jnp.float32)
+    plane = jax.ShapeDtypeStruct((height, breadth), jnp.float32)
+    return pl.pallas_call(
+        column_kernel,
+        out_shape=(field, field, field, field, plane, plane),
+        interpret=INTERPRET,
+    )(u, v, t, s, marine, coriolis, he, hw, hn, hs)
 
 
 def laplace(field, near):
@@ -76,72 +164,55 @@
 ):
     level_fields, height, breadth = zonal_current.shape
     marine_snapshot = marine_indicator.astype(jnp.float32)
-    zonal = zonal_current * marine_snapshot
-    merid = meridional_current * marine_snapshot
-    enthalpy_content = warmth_anomaly * marine_snapshot
-    salt = brine_anomaly * marine_snapshot
     kept = jnp.repeat(
         jnp.repeat(retained_tile_indicator.astype(jnp.float32), BLK, axis=0), BLK, axis=1
     )
     open_cells = marine_snapshot * kept
     column = seabed_thickness * open_cells
 
-    stack = [zonal, merid, enthalpy_content, salt, column[None]]
+    raw = (zonal_current, meridional_current, warmth_anomaly, brine_anomaly)
+
+    def edges(index_field, index_mask, plane):
+        return jnp.concatenate(
+            [item[index_field] * marine_snapshot[index_mask] for item in raw] + [plane[index_mask][None]],
+            axis=0,
+        )
+
     parity = jnp.concatenate(
         [
             -jnp.ones((2 * level_fields,), jnp.float32),
             jnp.ones((2 * level_fields + 1,), jnp.float32),
         ]
-    )[:, None, None]
-    halo_all = halos(stack, parity)
-
-    def part(first, count):
-        return tuple(item[first : first + count] for item in halo_all)
-
-    near_u = around(zonal, part(0, level_fields))
-    near_v = around(merid, part(level_fields, level_fields))
-    halo_t = part(2 * level_fields, level_fields)
-    halo_s = part(3 * level_fields, level_fields)
-    near_t = around(enthalpy_content, halo_t)
-    near_s = around(salt, halo_s)
+    )[:, None]
+    halo_all = exchange(
+        edges((slice(None), slice(None), 0), (slice(None), 0), column),
+        edges((slice(None), slice(None), -1), (slice(None), -1), column),
+        edges((slice(None), 0, slice(None)), (0, slice(None)), column),
+        edges((slice(None), -1, slice(None)), (-1, slice(None)), column),
+        parity,
+    )
     halo_c = tuple(item[4 * level_fields] for item in halo_all)
     near_c = around(column, halo_c)
-
-    pressure = jnp.cumsum(haline * salt - thermal * enthalpy_content, axis=0)
-    halo_p = tuple(
-        jnp.cumsum(haline * halo_s[side] - thermal * halo_t[side], axis=0) for side in range(4)
-    )
-    near_p = around(pressure, halo_p)
 
     total_rows = height * lax.axis_size("lat")
     rows_global = (lax.axis_index("lat") * height + jnp.arange(height)).astype(jnp.float32)
     coriolis = (2.0 * (rows_global + 0.5) / total_rows - 1.0)[:, None]
-    zonal_next = marine_snapshot * (
-        zonal
-        + time_step
-        * (coriolis * merid - 0.5 * (near_p[0] - near_p[1]) + viscosity * laplace(zonal, near_u))
-    )
-    merid_next = marine_snapshot * (
-        merid
-        + time_step
-        * (-coriolis * zonal - 0.5 * (near_p[2] - near_p[3]) + viscosity * laplace(merid, near_v))
-    )
-    tracers = []
-    for tracer, near_q in ((enthalpy_content, near_t), (salt, near_s)):
-        flux = 0.5 * (
-            near_u[0] * near_q[0]
-            - near_u[1] * near_q[1]
-            + near_v[2] * near_q[2]
-            - near_v[3] * near_q[3]
-        )
-        tracers.append(
-            marine_snapshot * (tracer + time_step * (-flux + diffusivity * laplace(tracer, near_q)))
-        )
-    zonal_mean = jnp.sum(zonal_next, axis=0) / level_fields
-    merid_mean = jnp.sum(merid_next, axis=0) / level_fields
+    zonal_next, merid_next, warm_next, brine_next, zonal_mean, merid_mean = column_step(
+        zonal_current,
+        meridional_current,
+        warmth_anomaly,
+        brine_anomaly,
+        marine_snapshot,
+        jnp.broadcast_to(coriolis, (height, breadth)),
+        halo_all[0][..., None],
+        halo_all[1][..., None],
+        halo_all[2][:, None, :],
+        halo_all[3][:, None, :],
+    )
+    tracers = [warm_next, brine_next]
 
     means = jnp.stack([zonal_mean, merid_mean], axis=0)
-    halo_m = halos([zonal_mean[None], merid_mean[None]], -jnp.ones((2, 1, 1), jnp.float32))
+    halo_m = halos(means, -jnp.ones((2, 1), jnp.float32))
     near_m = around(means, halo_m)
     rhs = (
         -source_gain

time: 228 us -> 217 us (0.952)
  blocking collectives: 0 us -> 75.8 us
  starting transfers between devices: 90.5 us -> 41.3 us
  other arithmetic: 42.9 us -> 14.9 us
  local copies, waits for them, and re-layouts: 69.1 us -> 43.9 us
  Pallas kernels: 0 us -> 15 us
    all_to_all x0 -> x3, blocking collectives: none -> 75.8 us  [allsum(): gathered = lax.all_to_all(spread, ('lon', 'lat'), 0, 0, tiled=True)]
    all_to_all x3 -> x0, starting transfers between devices: 41 us -> none  [allsum(): gathered = lax.all_to_all(spread, ('lon', 'lat'), 0, 0, tiled=True)]
    mul x3 -> x1, other arithmetic: 15.5 us -> 0.09 us  [edges(): item[index_field] * marine_snapshot[index_mask]]
    pallas_call x0 -> x1, Pallas kernels: none -> 15 us  [column_step(): pl.pallas_call(column_kernel, out_shape=(field, field, field, field, plan...]
    broadcast_in_dim x0 -> x5, local copies, waits for them, and re-layouts: none -> 13.7 us  [the longest x1 5.82 us: local(): halo_all[1][..., None]]
    ppermute x25, waiting for transfers between devices: 3.55 us -> 13.8 us  [the longest x5 6.21 us: exchange(): lax.ppermute(first_col, 'lon', [((i + 1) % lon_count, i) for i in range(l...]
    reduce_sum x2 -> x0, other arithmetic: 9.84 us -> none  [the longest x1 6 us: local(): merid_mean = jnp.sum(merid_next, axis=0) / level_fields]
    all_to_all x3 -> x0, waiting for transfers between devices: 9.01 us -> none  [allsum(): gathered = lax.all_to_all(spread, ('lon', 'lat'), 0, 0, tiled=True)]
  transfers between devices with their start and end apart: 28 -> 25, of which waited for: 5 -> 7; matrix products, arithmetic and copies ran while one was open for 29% -> 18% of each run, Pallas kernels for 0% -> 0%
where the time goes in v4:
time: 217 us; the launch traced here: 216 us
  blocking collectives  75.8 us (35%)
  local copies, waits for them, and re-layouts  43.9 us (20%)
  starting transfers between devices  41.3 us (19%)
  Pallas kernels  15 us (7%)
  other arithmetic  14.9 us (7%)
  waiting for transfers between devices  13.8 us (6%)
  between operations  11.1 us (5%)
    all_to_all x3, blocking collectives, allsum(): gathered = lax.all_to_all(spread, ('lon', 'lat'), 0, 0, tiled=True)  75.8 us
    ppermute x5, starting transfers between devices, exchange(): lax.ppermute(last_row, 'lat', [(i, i + 1) for i in range(lat_count - 1)])  16.8 us
    pallas_call x1, Pallas kernels, column_step(): pl.pallas_call(column_kernel, out_shape=(field, field, field, field, plan...  15 us
    slice x8, local copies, waits for them, and re-layouts, edges(): item[index_field] * marine_snapshot[index_mask]  11 us
    unnamed x22, local copies, waits for them, and re-layouts  10.9 us
    ppermute x5, starting transfers between devices, exchange(): lax.ppermute(first_col, 'lon', [((i + 1) % lon_count, i) for i in range(l...  9.65 us
    ppermute x5, starting transfers between devices, exchange(): lax.ppermute(first_row, 'lat', [(i + 1, i) for i in range(lat_count - 1)])  6.42 us
    ppermute x5, waiting for transfers between devices, exchange(): lax.ppermute(first_col, 'lon', [((i + 1) % lon_count, i) for i in range(l...  6.21 us
  transfers between devices with their start and end apart: 25, of which 7 were waited for; matrix products, arithmetic and copies ran while one was open for 18% of the time, Pallas kernels for 0%

profile of v4, /device:TPU:1, one launch (start us, length us, event | category | flops | bytes accessed | tf_op | source)
XLA Modules:
  0.0 215.8 jit_solution(2621547499247187675)
XLA Ops:
  2.4 1.0 fusion.50
  3.4 1.0 fusion.49
  4.4 1.0 fusion.48
  5.4 1.0 fusion.47
  9.7 1.3 dynamic-update-slice.9
  11.0 3.9 %collective-permute-start.4 = (f32[129,128]{1,0:T(8,128)}, f32[129,128]{1,0:T(8,128)S(1)}, u32[]{:S(2)}, u32[]{:S(2)}) collective-permute-start(f32[129,128]{1,0:T(8,128)} %dynamic-update-slice.9), channel_id=1, source_target_pairs={{0,1},{1,2},{2,3},{3,4},{4,5},{5,6},{6,7},{8,9},{9,10},{10,11},{11... | collective-permute-start | bytes 198152 | tf_op jit(solution)/shard_map/ppermute | solution.py:35
  14.9 1.3 collective-permute-start.2
  18.6 1.3 dynamic-update-slice.4
  19.9 1.3 collective-permute-start.3
  21.4 3.3 %fusion.54 = (f32[32,64,1]{2,1,0:T(8,128)}, f32[32,64,1]{2,1,0:T(8,128)}) fusion(f32[32,64,128]{2,1,0:T(8,128)} %u_ref.1), kind=kLoop, calls=%fused_computation.143 | loop fusion | bytes 32768 | tf_op jit(solution)/shard_map/slice | solution.py:177
  24.8 1.7 fusion.53
  26.4 1.7 fusion.52
  28.5 1.9 copy.198
  30.4 1.8 copy.194
  32.1 1.8 copy.199
  33.9 1.8 copy.195
  35.7 1.8 copy.200
  39.5 1.0 collective-permute-start
  40.7 1.6 collective-permute-start.1
  42.4 1.7 collective-permute-done
  44.0 3.3 %collective-permute-done.1 = f32[129,64]{0,1:T(8,128)S(1)} collective-permute-done((f32[129,64]{0,1:T(8,128)S(1)}, f32[129,64]{0,1:T(8,128)S(1)}, u32[]{:S(2)}, u32[]{:S(2)}) %collective-permute-start.1) | collective-permute-done | bytes 33056 | tf_op jit(solution)/shard_map/ppermute | solution.py:33
  47.3 5.8 %copy.173.hw_ref = f32[129,64,1]{2,1,0:T(8,128)} copy(f32[129,64,1]{0,1,2:T(8,128)S(1)} %bitcast.145) | data formatting | bytes 66048 | tf_op jit(solution)/shard_map/broadcast_in_dim | solution.py:208
  53.1 5.8 %copy.172.he_ref = f32[129,64,1]{2,1,0:T(8,128)} copy(f32[129,64,1]{0,1,2:T(8,128)S(1)} %bitcast.144) | data formatting | bytes 66048 | tf_op jit(solution)/shard_map/broadcast_in_dim | solution.py:207
  58.9 1.0 rev.15
  60.0 1.0 multiply_select_fusion
  63.0 15.0 %shard_map.127 = (f32[32,64,128]{2,1,0:T(8,128)}, f32[32,64,128]{2,1,0:T(8,128)}, f32[32,64,128]{2,1,0:T(8,128)}, f32[32,64,128]{2,1,0:T(8,128)}, f32[64,128]{1,0:T(8,128)}, /*index=5*/f32[64,128]{1,0:T(8,128)}) custom-call(f32[32,64,128]{2,1,0:T(8,128)} %u_ref.1, f32[32,64,128]{2,1,0:T(8,128)} %v_ref.1, f32[32,64,128]{2,1,0:T(8,128)} %t_ref.1, ...), custom_call_target="tpu_custom_call" | custom-call | tf_op jit(solution)/shard_map/pallas_call | solution.py:144
  78.1 1.0 fusion.2
  79.8 0.9 fusion
  80.7 1.3 collective-permute-start.8
  82.7 6.6 %collective-permute-start.5 = (f32[2,64]{1,0:T(2,128)S(1)}, f32[2,64]{1,0:T(2,128)S(1)}, u32[]{:S(2)}, u32[]{:S(2)}) collective-permute-start(f32[2,64]{1,0:T(2,128)S(1)} %get-tuple-element.18), channel_id=1, source_target_pairs={{8,0},{16,8},{24,16},{32,24},{40,32},{48,40},{56,48},{64,56},{72,6... | collective-permute-start | bytes 1544 | tf_op jit(solution)/shard_map/ppermute | solution.py:32
  90.1 4.6 %collective-permute-start.9 = (f32[2,128]{1,0:T(2,128)S(1)}, f32[2,128]{1,0:T(2,128)S(1)}, u32[]{:S(2)}, u32[]{:S(2)}) collective-permute-start(f32[2,128]{1,0:T(2,128)S(1)} %bitcast.157), channel_id=1, source_target_pairs={{0,1},{1,2},{2,3},{3,4},{4,5},{5,6},{6,7},{8,9},{9,10},{10,11},{11... | collective-permute-start | bytes 3080 | tf_op jit(solution)/shard_map/ppermute | solution.py:35
  95.4 0.9 multiply_bitcast_fusion.9
  96.5 3.9 %collective-permute-start.14 = (f32[128]{0:T(128)S(1)}, f32[128]{0:T(128)S(1)}, u32[]{:S(2)}, u32[]{:S(2)}) collective-permute-start(f32[128]{0:T(128)S(1)} %get-tuple-element.89), channel_id=1, source_target_pairs={{0,1},{1,2},{2,3},{3,4},{4,5},{5,6},{6,7},{8,9},{9,10},{10,11},{11... | collective-permute-start | bytes 1544 | tf_op jit(solution)/shard_map/ppermute | solution.py:35
  101.3 2.0 collective-permute-start.10
  103.3 1.3 collective-permute-start.13
  105.0 2.9 %collective-permute-done.13 = f32[128]{0:T(128)S(1)} collective-permute-done((f32[128]{0:T(128)S(1)}, f32[128]{0:T(128)S(1)}, u32[]{:S(2)}, u32[]{:S(2)}) %collective-permute-start.13) | collective-permute-done | bytes 544 | tf_op jit(solution)/shard_map/ppermute | solution.py:34
  108.2 29.9 %all_to_all.18 = f32[128,1,2]{2,1,0:T(1,128)S(1)} all-to-all(f32[128,1,2]{2,1,0:T(1,128)S(1)} %broadcast_in_dim.96), channel_id=1, replica_groups=mesh['lon'=16,'lat'=8] {'lon','lat'}, dimensions={0} | all-to-all | bytes 2048 | tf_op jit(solution)/shard_map/all_to_all | solution.py:25
  140.4 2.2 %collective-permute-start.19 = (f32[128]{0:T(128)S(1)}, f32[128]{0:T(128)S(1)}, u32[]{:S(2)}, u32[]{:S(2)}) collective-permute-start(f32[128]{0:T(128)S(1)} %get-tuple-element.83), channel_id=1, source_target_pairs={{0,1},{1,2},{2,3},{3,4},{4,5},{5,6},{6,7},{8,9},{9,10},{10,11},{11... | collective-permute-start | bytes 1544 | tf_op jit(solution)/shard_map/ppermute | solution.py:35
  143.2 1.3 collective-permute-start.16
  144.6 1.3 collective-permute-start.18
  145.9 1.6 collective-permute-done.15
  147.8 1.0 collective-permute-done.18
  149.1 22.8 %all_to_all.19 = f32[128,1,4]{2,1,0:T(1,128)S(1)} all-to-all(f32[128,1,4]{2,1,0:T(1,128)S(1)} %broadcast_in_dim.101), channel_id=1, replica_groups=mesh['lon'=16,'lat'=8] {'lon','lat'}, dimensions={0} | all-to-all | bytes 4096 | tf_op jit(solution)/shard_map/all_to_all | solution.py:25
  177.7 2.2 %collective-permute-start.24 = (f32[128]{0:T(128)S(1)}, f32[128]{0:T(128)S(1)}, u32[]{:S(2)}, u32[]{:S(2)}) collective-permute-start(f32[128]{0:T(128)S(1)} %get-tuple-element.76), channel_id=1, source_target_pairs={{0,1},{1,2},{2,3},{3,4},{4,5},{5,6},{6,7},{8,9},{9,10},{10,11},{11... | collective-permute-start | bytes 1544 | tf_op jit(solution)/shard_map/ppermute | solution.py:35
  180.6 1.3 collective-permute-start.23
  181.9 1.3 collective-permute-start.21
  183.3 2.9 %collective-permute-done.20 = f32[64]{0:T(128)S(1)} collective-permute-done((f32[64]{0:T(128)S(1)}, f32[64]{0:T(128)S(1)}, u32[]{:S(2)}, u32[]{:S(2)}) %collective-permute-start.20) | collective-permute-done | bytes 288 | tf_op jit(solution)/shard_map/ppermute | solution.py:32
  186.8 23.0 %all_to_all.20 = f32[128,1,4]{2,1,0:T(1,128)S(1)} all-to-all(f32[128,1,4]{2,1,0:T(1,128)S(1)} %broadcast_in_dim.106), channel_id=1, replica_groups=mesh['lon'=16,'lat'=8] {'lon','lat'}, dimensions={0} | all-to-all | bytes 4096 | tf_op jit(solution)/shard_map/all_to_all | solution.py:25
  (129 shorter events, 23.6 us)
Async XLA Ops:
  0.6 24.1 %copy-start = (f32[32,64,128]{2,1,0:T(8,128)S(1)}, f32[32,64,128]{2,1,0:T(8,128)}, u32[]{:S(2)}) copy-start(f32[32,64,128]{2,1,0:T(8,128)} %v_ref.1) | copy-start | bytes 3145732
  2.4 24.0 %copy-start.4 = (f32[64,128]{1,0:T(8,128)}, f32[64,128]{1,0:T(8,128)S(1)}, u32[]{:S(2)}) copy-start(f32[64,128]{1,0:T(8,128)S(1)} %convert_element_type.13.m_ref) | copy-start | bytes 98308
  11.0 50.7 %collective-permute-start.4 = (f32[129,128]{1,0:T(8,128)}, f32[129,128]{1,0:T(8,128)S(1)}, u32[]{:S(2)}, u32[]{:S(2)}) collective-permute-start(f32[129,128]{1,0:T(8,128)} %dynamic-update-slice.9), channel_id=1, source_target_pairs={{0,1},{1,2},{2,3},{3,4},{4,5},{5,6},{6,7},{8,9},{9,10},{10,11},{11... | collective-permute-start | bytes 198152 | tf_op jit(solution)/shard_map/ppermute | solution.py:35
  14.9 44.0 %collective-permute-start.2 = (f32[129,128]{1,0:T(8,128)}, f32[129,128]{1,0:T(8,128)}, u32[]{:S(2)}, u32[]{:S(2)}) collective-permute-start(f32[129,128]{1,0:T(8,128)} %dynamic-update-slice.9), channel_id=1, source_target_pairs={{7,127},{15,119},{23,111},{31,103},{39,95},{47,87},{55,79},{63,71}... | collective-permute-start | bytes 198152 | tf_op jit(solution)/shard_map/ppermute | solution.py:37
  19.9 40.1 %collective-permute-start.3 = (f32[129,128]{1,0:T(8,128)}, f32[129,128]{1,0:T(8,128)}, u32[]{:S(2)}, u32[]{:S(2)}) collective-permute-start(f32[129,128]{1,0:T(8,128)} %dynamic-update-slice.4), channel_id=1, source_target_pairs={{1,0},{2,1},{3,2},{4,3},{5,4},{6,5},{7,6},{9,8},{10,9},{11,10},{12... | collective-permute-start | bytes 198152 | tf_op jit(solution)/shard_map/ppermute | solution.py:34
  21.4 5.1 %copy-start.1 = (f32[32,64,128]{2,1,0:T(8,128)S(1)}, f32[32,64,128]{2,1,0:T(8,128)}, u32[]{:S(2)}) copy-start(f32[32,64,128]{2,1,0:T(8,128)} %t_ref.1) | copy-start | bytes 3145732
  24.8 3.3 %copy-start.2 = (f32[32,64,128]{2,1,0:T(8,128)S(1)}, f32[32,64,128]{2,1,0:T(8,128)}, u32[]{:S(2)}) copy-start(f32[32,64,128]{2,1,0:T(8,128)} %s_ref.1) | copy-start | bytes 3145732
  28.5 9.0 %copy-start.3 = (f32[32,64,1]{2,1,0:T(8,128)S(1)}, f32[32,64,1]{2,1,0:T(8,128)}, u32[]{:S(2)}) copy-start(f32[32,64,1]{2,1,0:T(8,128)} %get-tuple-element.61) | copy-start | bytes 24580
  39.5 4.5 %collective-permute-start = (f32[129,64]{0,1:T(8,128)S(1)}, f32[129,64]{0,1:T(8,128)S(1)}, u32[]{:S(2)}, u32[]{:S(2)}) collective-permute-start(f32[129,64]{0,1:T(8,128)S(1)} %concatenate.72), channel_id=1, source_target_pairs={{8,0},{16,8},{24,16},{32,24},{40,32},{48,40},{56,48},{64,56},{72,6... | collective-permute-start | bytes 99080 | tf_op jit(solution)/shard_map/ppermute | solution.py:32
  40.7 6.6 %collective-permute-start.1 = (f32[129,64]{0,1:T(8,128)S(1)}, f32[129,64]{0,1:T(8,128)S(1)}, u32[]{:S(2)}, u32[]{:S(2)}) collective-permute-start(f32[129,64]{0,1:T(8,128)S(1)} %concatenate.73), channel_id=1, source_target_pairs={{0,8},{8,16},{16,24},{24,32},{32,40},{40,48},{48,56},{56,64},{64,7... | collective-permute-start | bytes 99080 | tf_op jit(solution)/shard_map/ppermute | solution.py:33
  47.3 12.7 %copy-start.6 = (f32[129]{0:T(256)S(1)}, f32[129]{0:T(256)}, u32[]{:S(2)}) copy-start(f32[129]{0:T(256)} %constant.8.clone.1) | copy-start | bytes 1552
  63.0 32.4 %copy-start.5 = (f32[64,128]{1,0:T(8,128)S(1)}, f32[64,128]{1,0:T(8,128)}, u32[]{:S(2)}) copy-start(f32[64,128]{1,0:T(8,128)} %param.15) | copy-start | bytes 98308
  80.7 14.4 %collective-permute-start.8 = (f32[2,128]{1,0:T(2,128)S(1)}, f32[2,128]{1,0:T(2,128)S(1)}, u32[]{:S(2)}, u32[]{:S(2)}) collective-permute-start(f32[2,128]{1,0:T(2,128)S(1)} %bitcast.158), channel_id=1, source_target_pairs={{1,0},{2,1},{3,2},{4,3},{5,4},{6,5},{7,6},{9,8},{10,9},{11,10},{12... | collective-permute-start | bytes 3080 | tf_op jit(solution)/shard_map/ppermute | solution.py:34
  82.0 13.0 %collective-permute-start.7 = (f32[2,128]{1,0:T(2,128)S(1)}, f32[2,128]{1,0:T(2,128)S(1)}, u32[]{:S(2)}, u32[]{:S(2)}) collective-permute-start(f32[2,128]{1,0:T(2,128)S(1)} %bitcast.156), channel_id=1, source_target_pairs={{7,127},{15,119},{23,111},{31,103},{39,95},{47,87},{55,79},{63,71}... | collective-permute-start | bytes 3080 | tf_op jit(solution)/shard_map/ppermute | solution.py:37
  82.7 12.2 %collective-permute-start.5 = (f32[2,64]{1,0:T(2,128)S(1)}, f32[2,64]{1,0:T(2,128)S(1)}, u32[]{:S(2)}, u32[]{:S(2)}) collective-permute-start(f32[2,64]{1,0:T(2,128)S(1)} %get-tuple-element.18), channel_id=1, source_target_pairs={{8,0},{16,8},{24,16},{32,24},{40,32},{48,40},{56,48},{64,56},{72,6... | collective-permute-start | bytes 1544 | tf_op jit(solution)/shard_map/ppermute | solution.py:32
  89.3 5.4 %collective-permute-start.6 = (f32[2,64]{1,0:T(2,128)S(1)}, f32[2,64]{1,0:T(2,128)S(1)}, u32[]{:S(2)}, u32[]{:S(2)}) collective-permute-start(f32[2,64]{1,0:T(2,128)S(1)} %get-tuple-element.19), channel_id=1, source_target_pairs={{0,8},{8,16},{16,24},{24,32},{32,40},{40,48},{48,56},{56,64},{64,7... | collective-permute-start | bytes 1544 | tf_op jit(solution)/shard_map/ppermute | solution.py:33
  90.1 5.3 %collective-permute-start.9 = (f32[2,128]{1,0:T(2,128)S(1)}, f32[2,128]{1,0:T(2,128)S(1)}, u32[]{:S(2)}, u32[]{:S(2)}) collective-permute-start(f32[2,128]{1,0:T(2,128)S(1)} %bitcast.157), channel_id=1, source_target_pairs={{0,1},{1,2},{2,3},{3,4},{4,5},{5,6},{6,7},{8,9},{9,10},{10,11},{11... | collective-permute-start | bytes 3080 | tf_op jit(solution)/shard_map/ppermute | solution.py:35
  96.5 11.4 %collective-permute-start.14 = (f32[128]{0:T(128)S(1)}, f32[128]{0:T(128)S(1)}, u32[]{:S(2)}, u32[]{:S(2)}) collective-permute-start(f32[128]{0:T(128)S(1)} %get-tuple-element.89), channel_id=1, source_target_pairs={{0,1},{1,2},{2,3},{3,4},{4,5},{5,6},{6,7},{8,9},{9,10},{10,11},{11... | collective-permute-start | bytes 1544 | tf_op jit(solution)/shard_map/ppermute | solution.py:35
  100.4 4.5 %collective-permute-start.12 = (f32[128]{0:T(128)S(1)}, f32[128]{0:T(128)S(1)}, u32[]{:S(2)}, u32[]{:S(2)}) collective-permute-start(f32[128]{0:T(128)S(1)} %get-tuple-element.89), channel_id=1, source_target_pairs={{7,127},{15,119},{23,111},{31,103},{39,95},{47,87},{55,79},{63,71}... | collective-permute-start | bytes 1544 | tf_op jit(solution)/shard_map/ppermute | solution.py:37
  101.1 3.7 %collective-permute-start.11 = (f32[64]{0:T(128)S(1)}, f32[64]{0:T(128)S(1)}, u32[]{:S(2)}, u32[]{:S(2)}) collective-permute-start(f32[64]{0:T(128)S(1)} %get-tuple-element.24), channel_id=1, source_target_pairs={{0,8},{8,16},{16,24},{24,32},{32,40},{40,48},{48,56},{56,64},{64,7... | collective-permute-start | bytes 776 | tf_op jit(solution)/shard_map/ppermute | solution.py:33
  101.3 3.4 %collective-permute-start.10 = (f32[64]{0:T(128)S(1)}, f32[64]{0:T(128)S(1)}, u32[]{:S(2)}, u32[]{:S(2)}) collective-permute-start(f32[64]{0:T(128)S(1)} %get-tuple-element.25), channel_id=1, source_target_pairs={{8,0},{16,8},{24,16},{32,24},{40,32},{48,40},{56,48},{64,56},{72,6... | collective-permute-start | bytes 776 | tf_op jit(solution)/shard_map/ppermute | solution.py:32
  103.3 4.6 %collective-permute-start.13 = (f32[128]{0:T(128)S(1)}, f32[128]{0:T(128)S(1)}, u32[]{:S(2)}, u32[]{:S(2)}) collective-permute-start(f32[128]{0:T(128)S(1)} %get-tuple-element.88), channel_id=1, source_target_pairs={{1,0},{2,1},{3,2},{4,3},{5,4},{6,5},{7,6},{9,8},{10,9},{11,10},{12... | collective-permute-start | bytes 1544 | tf_op jit(solution)/shard_map/ppermute | solution.py:34
  140.4 8.5 %collective-permute-start.19 = (f32[128]{0:T(128)S(1)}, f32[128]{0:T(128)S(1)}, u32[]{:S(2)}, u32[]{:S(2)}) collective-permute-start(f32[128]{0:T(128)S(1)} %get-tuple-element.83), channel_id=1, source_target_pairs={{0,1},{1,2},{2,3},{3,4},{4,5},{5,6},{6,7},{8,9},{9,10},{10,11},{11... | collective-permute-start | bytes 1544 | tf_op jit(solution)/shard_map/ppermute | solution.py:35
  142.6 5.2 %collective-permute-start.17 = (f32[128]{0:T(128)S(1)}, f32[128]{0:T(128)S(1)}, u32[]{:S(2)}, u32[]{:S(2)}) collective-permute-start(f32[128]{0:T(128)S(1)} %get-tuple-element.83), channel_id=1, source_target_pairs={{7,127},{15,119},{23,111},{31,103},{39,95},{47,87},{55,79},{63,71}... | collective-permute-start | bytes 1544 | tf_op jit(solution)/shard_map/ppermute | solution.py:37
  143.2 4.4 %collective-permute-start.16 = (f32[64]{0:T(128)S(1)}, f32[64]{0:T(128)S(1)}, u32[]{:S(2)}, u32[]{:S(2)}) collective-permute-start(f32[64]{0:T(128)S(1)} %get-tuple-element.22), channel_id=1, source_target_pairs={{0,8},{8,16},{16,24},{24,32},{32,40},{40,48},{48,56},{56,64},{64,7... | collective-permute-start | bytes 776 | tf_op jit(solution)/shard_map/ppermute | solution.py:33
  144.6 3.0 %collective-permute-start.15 = (f32[64]{0:T(128)S(1)}, f32[64]{0:T(128)S(1)}, u32[]{:S(2)}, u32[]{:S(2)}) collective-permute-start(f32[64]{0:T(128)S(1)} %get-tuple-element.23), channel_id=1, source_target_pairs={{8,0},{16,8},{24,16},{32,24},{40,32},{48,40},{56,48},{64,56},{72,6... | collective-permute-start | bytes 776 | tf_op jit(solution)/shard_map/ppermute | solution.py:32
  144.6 4.3 %collective-permute-start.18 = (f32[128]{0:T(128)S(1)}, f32[128]{0:T(128)S(1)}, u32[]{:S(2)}, u32[]{:S(2)}) collective-permute-start(f32[128]{0:T(128)S(1)} %get-tuple-element.82), channel_id=1, source_target_pairs={{1,0},{2,1},{3,2},{4,3},{5,4},{6,5},{7,6},{9,8},{10,9},{11,10},{12... | collective-permute-start | bytes 1544 | tf_op jit(solution)/shard_map/ppermute | solution.py:34
  177.7 8.8 %collective-permute-start.24 = (f32[128]{0:T(128)S(1)}, f32[128]{0:T(128)S(1)}, u32[]{:S(2)}, u32[]{:S(2)}) collective-permute-start(f32[128]{0:T(128)S(1)} %get-tuple-element.76), channel_id=1, source_target_pairs={{0,1},{1,2},{2,3},{3,4},{4,5},{5,6},{6,7},{8,9},{9,10},{10,11},{11... | collective-permute-start | bytes 1544 | tf_op jit(solution)/shard_map/ppermute | solution.py:35
  179.9 6.5 %collective-permute-start.22 = (f32[128]{0:T(128)S(1)}, f32[128]{0:T(128)S(1)}, u32[]{:S(2)}, u32[]{:S(2)}) collective-permute-start(f32[128]{0:T(128)S(1)} %get-tuple-element.76), channel_id=1, source_target_pairs={{7,127},{15,119},{23,111},{31,103},{39,95},{47,87},{55,79},{63,71}... | collective-permute-start | bytes 1544 | tf_op jit(solution)/shard_map/ppermute | solution.py:37
  180.6 5.9 %collective-permute-start.23 = (f32[128]{0:T(128)S(1)}, f32[128]{0:T(128)S(1)}, u32[]{:S(2)}, u32[]{:S(2)}) collective-permute-start(f32[128]{0:T(128)S(1)} %get-tuple-element.75), channel_id=1, source_target_pairs={{1,0},{2,1},{3,2},{4,3},{5,4},{6,5},{7,6},{9,8},{10,9},{11,10},{12... | collective-permute-start | bytes 1544 | tf_op jit(solution)/shard_map/ppermute | solution.py:34
  181.9 4.4 %collective-permute-start.21 = (f32[64]{0:T(128)S(1)}, f32[64]{0:T(128)S(1)}, u32[]{:S(2)}, u32[]{:S(2)}) collective-permute-start(f32[64]{0:T(128)S(1)} %get-tuple-element.20), channel_id=1, source_target_pairs={{0,8},{8,16},{16,24},{24,32},{32,40},{40,48},{48,56},{56,64},{64,7... | collective-permute-start | bytes 776 | tf_op jit(solution)/shard_map/ppermute | solution.py:33
  183.2 3.0 %collective-permute-start.20 = (f32[64]{0:T(128)S(1)}, f32[64]{0:T(128)S(1)}, u32[]{:S(2)}, u32[]{:S(2)}) collective-permute-start(f32[64]{0:T(128)S(1)} %get-tuple-element.21), channel_id=1, source_target_pairs={{8,0},{16,8},{24,16},{32,24},{40,32},{48,40},{56,48},{64,56},{72,6... | collective-permute-start | bytes 776 | tf_op jit(solution)/shard_map/ppermute | solution.py:32

commit v5 on v4

--- a/solution.py
+++ b/solution.py
@@ -81,7 +81,12 @@
         )
 
     def side(index):
-        return he_ref[index], hw_ref[index], hn_ref[index], hs_ref[index]
+        return (
+            he_ref[:, index : index + 1],
+            hw_ref[:, index : index + 1],
+            hn_ref[index : index + 1, :],
+            hs_ref[index : index + 1, :],
+        )
 
     def body(level, carry):
         pressure, pe, pw, pn, ps, zonal_sum, merid_sum = carry
@@ -130,9 +135,9 @@
     blank = jnp.zeros((height, breadth), jnp.float32)
     blank_col = jnp.zeros((height, 1), jnp.float32)
     blank_row = jnp.zeros((1, breadth), jnp.float32)
-    carry = lax.fori_loop(
-        0, levels, body, (blank, blank_col, blank_col, blank_row, blank_row, blank, blank)
-    )
+    carry = (blank, blank_col, blank_col, blank_row, blank_row, blank, blank)
+    for level in range(levels):
+        carry = body(level, carry)
     um_ref[...] = carry[5] / levels
     vm_ref[...] = carry[6] / levels
 
@@ -172,10 +177,15 @@
 
     raw = (zonal_current, meridional_current, warmth_anomaly, brine_anomaly)
 
-    def edges(index_field, index_mask, plane):
+    def row_edges(at):
         return jnp.concatenate(
-            [item[index_field] * marine_snapshot[index_mask] for item in raw] + [plane[index_mask][None]],
-            axis=0,
+            [item[:, at, :] * marine_snapshot[at] for item in raw] + [column[at][None]], axis=0
+        )
+
+    def col_edges(at):
+        return jnp.concatenate(
+            [(item[:, :, at] * marine_snapshot[:, at]).T for item in raw] + [column[:, at][:, None]],
+            axis=1,
         )
 
     parity = jnp.concatenate(
@@ -184,14 +194,13 @@
             jnp.ones((2 * level_fields + 1,), jnp.float32),
         ]
     )[:, None]
-    halo_all = exchange(
-        edges((slice(None), slice(None), 0), (slice(None), 0), column),
-        edges((slice(None), slice(None), -1), (slice(None), -1), column),
-        edges((slice(None), 0, slice(None)), (0, slice(None)), column),
-        edges((slice(None), -1, slice(None)), (-1, slice(None)), column),
-        parity,
-    )
-    halo_c = tuple(item[4 * level_fields] for item in halo_all)
+    halo_all = exchange(col_edges(0), col_edges(-1), row_edges(0), row_edges(-1), parity)
+    halo_c = (
+        halo_all[0][:, 4 * level_fields],
+        halo_all[1][:, 4 * level_fields],
+        halo_all[2][4 * level_fields],
+        halo_all[3][4 * level_fields],
+    )
     near_c = around(column, halo_c)
 
     total_rows = height * lax.axis_size("lat")
@@ -204,10 +213,10 @@
         brine_anomaly,
         marine_snapshot,
         jnp.broadcast_to(coriolis, (height, breadth)),
-        halo_all[0][..., None],
-        halo_all[1][..., None],
-        halo_all[2][:, None, :],
-        halo_all[3][:, None, :],
+        halo_all[0],
+        halo_all[1],
+        halo_all[2],
+        halo_all[3],
     )
     tracers = [warm_next, brine_next]
 

time: 217 us -> 197 us (0.908)
  local copies, waits for them, and re-layouts: 43.9 us -> 28.7 us
  other arithmetic: 14.9 us -> 11.7 us
    broadcast_in_dim x4 -> x0, local copies, waits for them, and re-layouts: 13 us -> none  [the longest x1 5.82 us: local(): halo_all[1][..., None]]
    another operation x3, other arithmetic: 2.41 us -> 0.09 us  [local(): means = jnp.stack([zonal_mean, merid_mean], axis=0)]
    slice x12 -> x18, local copies, waits for them, and re-layouts: 11.2 us -> 10.2 us  [the longest x4 5.06 us: col_edges(): item[:, :, at] * marine_snapshot[:, at]]
    unnamed x22 -> x34, local copies, waits for them, and re-layouts: 10.9 us -> 10.5 us
  transfers between devices with their start and end apart: 25 -> 25, of which waited for: 7 -> 6; matrix products, arithmetic and copies ran while one was open for 18% -> 12% of each run, Pallas kernels for 0% -> 0%
where the time goes in v5:
time: 197 us; the launch traced here: 196 us
  blocking collectives  74.4 us (38%)
  starting transfers between devices  41.9 us (21%)
  local copies, waits for them, and re-layouts  28.7 us (15%)
  Pallas kernels  15.2 us (8%)
  waiting for transfers between devices  13.3 us (7%)
  other arithmetic  11.7 us (6%)
  between operations  10.8 us (5%)
    all_to_all x3, blocking collectives, allsum(): gathered = lax.all_to_all(spread, ('lon', 'lat'), 0, 0, tiled=True)  74.4 us
    ppermute x5, starting transfers between devices, exchange(): lax.ppermute(last_row, 'lat', [(i, i + 1) for i in range(lat_count - 1)])  17.2 us
    pallas_call x1, Pallas kernels, column_step(): pl.pallas_call(column_kernel, out_shape=(field, field, field, field, plan...  15.2 us
    unnamed x34, local copies, waits for them, and re-layouts  10.5 us
    ppermute x5, starting transfers between devices, exchange(): lax.ppermute(first_col, 'lon', [((i + 1) % lon_count, i) for i in range(l...  10.5 us
    ppermute x5, starting transfers between devices, exchange(): lax.ppermute(first_row, 'lat', [(i + 1, i) for i in range(lat_count - 1)])  6.42 us
    ppermute x5, waiting for transfers between devices, exchange(): lax.ppermute(first_col, 'lon', [((i + 1) % lon_count, i) for i in range(l...  6.05 us
    slice x4, local copies, waits for them, and re-layouts, col_edges(): item[:, :, at] * marine_snapshot[:, at]  5.06 us
  transfers between devices with their start and end apart: 25, of which 6 were waited for; matrix products, arithmetic and copies ran while one was open for 12% of the time, Pallas kernels for 0%

profile of v5, /device:TPU:1, one launch (start us, length us, event | category | flops | bytes accessed | tf_op | source)
XLA Modules:
  0.0 196.0 jit_solution(15354016657268910768)
XLA Ops:
  0.7 0.8 convert_element_type.15
  1.7 1.0 fusion.58
  2.7 1.0 fusion.57
  3.7 1.0 fusion.56
  4.7 1.0 fusion.55
  5.8 0.8 fusion.54
  9.0 1.3 dynamic-update-slice.9
  10.3 4.5 %collective-permute-start.4 = (f32[129,128]{1,0:T(8,128)}, f32[129,128]{1,0:T(8,128)}, u32[]{:S(2)}, u32[]{:S(2)}) collective-permute-start(f32[129,128]{1,0:T(8,128)} %dynamic-update-slice.9), channel_id=1, source_target_pairs={{0,1},{1,2},{2,3},{3,4},{4,5},{5,6},{6,7},{8,9},{9,10},{10,11},{11... | collective-permute-start | bytes 198152 | tf_op jit(solution)/shard_map/ppermute | solution.py:35
  17.9 1.3 dynamic-update-slice.4
  19.2 1.3 collective-permute-start.3
  20.7 1.7 fusion.62
  22.4 1.3 fusion.61
  23.7 1.7 fusion.60
  25.8 1.8 copy.138
  27.6 1.8 copy.134
  30.0 1.9 copy.135
  31.8 1.8 copy.140
  35.7 1.0 collective-permute-start
  36.8 1.8 collective-permute-start.1
  38.7 1.5 collective-permute-done.he_ref
  40.2 3.5 %collective-permute-done.1.hw_ref = f32[64,129]{1,0:T(8,128)S(1)} collective-permute-done((f32[64,129]{1,0:T(8,128)S(1)}, f32[64,129]{1,0:T(8,128)S(1)}, u32[]{:S(2)}, u32[]{:S(2)}) %collective-permute-start.1) | collective-permute-done | bytes 33056 | tf_op jit(solution)/shard_map/ppermute | solution.py:33
  44.3 1.6 multiply_select_fusion.hn_ref
  45.9 0.7 broadcast_in_dim.69.f_ref
  46.6 15.2 %shard_map.127 = (f32[32,64,128]{2,1,0:T(8,128)}, f32[32,64,128]{2,1,0:T(8,128)}, f32[32,64,128]{2,1,0:T(8,128)}, f32[32,64,128]{2,1,0:T(8,128)}, f32[64,128]{1,0:T(8,128)}, /*index=5*/f32[64,128]{1,0:T(8,128)}) custom-call(f32[32,64,128]{2,1,0:T(8,128)} %u_ref.1, f32[32,64,128]{2,1,0:T(8,128)} %v_ref.1, f32[32,64,128]{2,1,0:T(8,128)} %t_ref.1, ...), custom_call_target="tpu_custom_call" | custom-call | tf_op jit(solution)/shard_map/pallas_call | solution.py:149
  61.8 1.0 fusion.2
  62.9 1.3 collective-permute-start.8
  64.2 0.7 collective-permute-start.7
  64.9 6.6 %collective-permute-start.5 = (f32[2,64]{1,0:T(2,128)S(1)}, f32[2,64]{1,0:T(2,128)S(1)}, u32[]{:S(2)}, u32[]{:S(2)}) collective-permute-start(f32[2,64]{1,0:T(2,128)S(1)} %get-tuple-element.18), channel_id=1, source_target_pairs={{8,0},{16,8},{24,16},{32,24},{40,32},{48,40},{56,48},{64,56},{72,6... | collective-permute-start | bytes 1544 | tf_op jit(solution)/shard_map/ppermute | solution.py:32
  71.5 4.6 %collective-permute-start.9 = (f32[2,128]{1,0:T(2,128)S(1)}, f32[2,128]{1,0:T(2,128)S(1)}, u32[]{:S(2)}, u32[]{:S(2)}) collective-permute-start(f32[2,128]{1,0:T(2,128)S(1)} %bitcast.175), channel_id=1, source_target_pairs={{0,1},{1,2},{2,3},{3,4},{4,5},{5,6},{6,7},{8,9},{9,10},{10,11},{11... | collective-permute-start | bytes 3080 | tf_op jit(solution)/shard_map/ppermute | solution.py:35
  76.2 0.7 slice.352
  78.2 3.6 %collective-permute-start.14 = (f32[128]{0:T(128)S(1)}, f32[128]{0:T(128)S(1)}, u32[]{:S(2)}, u32[]{:S(2)}) collective-permute-start(f32[128]{0:T(128)S(1)} %get-tuple-element.89), channel_id=1, source_target_pairs={{0,1},{1,2},{2,3},{3,4},{4,5},{5,6},{6,7},{8,9},{9,10},{10,11},{11... | collective-permute-start | bytes 1544 | tf_op jit(solution)/shard_map/ppermute | solution.py:35
  81.8 0.7 collective-permute-start.12
  82.6 2.9 %collective-permute-start.10 = (f32[64]{0:T(128)S(1)}, f32[64]{0:T(128)S(1)}, u32[]{:S(2)}, u32[]{:S(2)}) collective-permute-start(f32[64]{0:T(128)S(1)} %get-tuple-element.25), channel_id=1, source_target_pairs={{8,0},{16,8},{24,16},{32,24},{40,32},{48,40},{56,48},{64,56},{72,6... | collective-permute-start | bytes 776 | tf_op jit(solution)/shard_map/ppermute | solution.py:32
  85.5 1.3 collective-permute-start.13
  87.1 2.7 %collective-permute-done.13 = f32[128]{0:T(128)S(1)} collective-permute-done((f32[128]{0:T(128)S(1)}, f32[128]{0:T(128)S(1)}, u32[]{:S(2)}, u32[]{:S(2)}) %collective-permute-start.13) | collective-permute-done | bytes 544 | tf_op jit(solution)/shard_map/ppermute | solution.py:34
  90.1 28.5 %all_to_all.18 = f32[128,1,2]{2,1,0:T(1,128)S(1)} all-to-all(f32[128,1,2]{2,1,0:T(1,128)S(1)} %broadcast_in_dim.80), channel_id=1, replica_groups=mesh['lon'=16,'lat'=8] {'lon','lat'}, dimensions={0} | all-to-all | bytes 2048 | tf_op jit(solution)/shard_map/all_to_all | solution.py:25
  120.9 2.2 %collective-permute-start.19 = (f32[128]{0:T(128)S(1)}, f32[128]{0:T(128)S(1)}, u32[]{:S(2)}, u32[]{:S(2)}) collective-permute-start(f32[128]{0:T(128)S(1)} %get-tuple-element.83), channel_id=1, source_target_pairs={{0,1},{1,2},{2,3},{3,4},{4,5},{5,6},{6,7},{8,9},{9,10},{10,11},{11... | collective-permute-start | bytes 1544 | tf_op jit(solution)/shard_map/ppermute | solution.py:35
  123.1 0.7 collective-permute-start.17
  123.8 1.3 collective-permute-start.16
  125.1 1.3 collective-permute-start.18
  126.5 1.6 collective-permute-done.15
  128.4 1.0 collective-permute-done.18
  129.7 22.8 %all_to_all.19 = f32[128,1,4]{2,1,0:T(1,128)S(1)} all-to-all(f32[128,1,4]{2,1,0:T(1,128)S(1)} %broadcast_in_dim.85), channel_id=1, replica_groups=mesh['lon'=16,'lat'=8] {'lon','lat'}, dimensions={0} | all-to-all | bytes 4096 | tf_op jit(solution)/shard_map/all_to_all | solution.py:25
  158.1 2.2 %collective-permute-start.24 = (f32[128]{0:T(128)S(1)}, f32[128]{0:T(128)S(1)}, u32[]{:S(2)}, u32[]{:S(2)}) collective-permute-start(f32[128]{0:T(128)S(1)} %get-tuple-element.76), channel_id=1, source_target_pairs={{0,1},{1,2},{2,3},{3,4},{4,5},{5,6},{6,7},{8,9},{9,10},{10,11},{11... | collective-permute-start | bytes 1544 | tf_op jit(solution)/shard_map/ppermute | solution.py:35
  161.0 1.3 collective-permute-start.23
  162.3 1.3 collective-permute-start.21
  163.6 2.9 %collective-permute-done.20 = f32[64]{0:T(128)S(1)} collective-permute-done((f32[64]{0:T(128)S(1)}, f32[64]{0:T(128)S(1)}, u32[]{:S(2)}, u32[]{:S(2)}) %collective-permute-start.20) | collective-permute-done | bytes 288 | tf_op jit(solution)/shard_map/ppermute | solution.py:32
  167.2 23.0 %all_to_all.20 = f32[128,1,4]{2,1,0:T(1,128)S(1)} all-to-all(f32[128,1,4]{2,1,0:T(1,128)S(1)} %broadcast_in_dim.90), channel_id=1, replica_groups=mesh['lon'=16,'lat'=8] {'lon','lat'}, dimensions={0} | all-to-all | bytes 4096 | tf_op jit(solution)/shard_map/all_to_all | solution.py:25
  (140 shorter events, 17.9 us)
Async XLA Ops:
  0.6 1.0 copy-start.10
  0.6 20.1 %copy-start = (f32[32,64,128]{2,1,0:T(8,128)S(1)}, f32[32,64,128]{2,1,0:T(8,128)}, u32[]{:S(2)}) copy-start(f32[32,64,128]{2,1,0:T(8,128)} %u_ref.1) | copy-start | bytes 3145732
  1.7 18.8 %copy-start.7 = (f32[64,128]{1,0:T(8,128)}, f32[64,128]{1,0:T(8,128)S(1)}, u32[]{:S(2)}) copy-start(f32[64,128]{1,0:T(8,128)S(1)} %convert_element_type.13.m_ref) | copy-start | bytes 98308
  10.3 35.7 %collective-permute-start.4 = (f32[129,128]{1,0:T(8,128)}, f32[129,128]{1,0:T(8,128)}, u32[]{:S(2)}, u32[]{:S(2)}) collective-permute-start(f32[129,128]{1,0:T(8,128)} %dynamic-update-slice.9), channel_id=1, source_target_pairs={{0,1},{1,2},{2,3},{3,4},{4,5},{5,6},{6,7},{8,9},{9,10},{10,11},{11... | collective-permute-start | bytes 198152 | tf_op jit(solution)/shard_map/ppermute | solution.py:35
  14.8 28.8 %collective-permute-start.2 = (f32[129,128]{1,0:T(8,128)}, f32[129,128]{1,0:T(8,128)S(1)}, u32[]{:S(2)}, u32[]{:S(2)}) collective-permute-start(f32[129,128]{1,0:T(8,128)} %dynamic-update-slice.9), channel_id=1, source_target_pairs={{7,127},{15,119},{23,111},{31,103},{39,95},{47,87},{55,79},{63,71}... | collective-permute-start | bytes 198152 | tf_op jit(solution)/shard_map/ppermute | solution.py:37
  19.2 25.1 %collective-permute-start.3 = (f32[129,128]{1,0:T(8,128)}, f32[129,128]{1,0:T(8,128)}, u32[]{:S(2)}, u32[]{:S(2)}) collective-permute-start(f32[129,128]{1,0:T(8,128)} %dynamic-update-slice.4), channel_id=1, source_target_pairs={{1,0},{2,1},{3,2},{4,3},{5,4},{6,5},{7,6},{9,8},{10,9},{11,10},{12... | collective-permute-start | bytes 198152 | tf_op jit(solution)/shard_map/ppermute | solution.py:34
  20.7 1.7 copy-start.1
  22.4 1.3 copy-start.2
  23.7 1.7 copy-start.3
  30.0 3.6 %copy-start.4 = (f32[32,64,1]{2,1,0:T(8,128)S(1)}, f32[32,64,1]{2,1,0:T(8,128)}, u32[]{:S(2)}) copy-start(f32[32,64,1]{2,1,0:T(8,128)} %get-tuple-element.61) | copy-start | bytes 24580
  35.7 4.5 %collective-permute-start = (f32[64,129]{1,0:T(8,128)S(1)}, f32[64,129]{1,0:T(8,128)S(1)}, u32[]{:S(2)}, u32[]{:S(2)}) collective-permute-start(f32[64,129]{1,0:T(8,128)S(1)} %concatenate.72), channel_id=1, source_target_pairs={{8,0},{16,8},{24,16},{32,24},{40,32},{48,40},{56,48},{64,56},{72,6... | collective-permute-start | bytes 99080 | tf_op jit(solution)/shard_map/ppermute | solution.py:32
  36.8 6.8 %collective-permute-start.1 = (f32[64,129]{1,0:T(8,128)S(1)}, f32[64,129]{1,0:T(8,128)S(1)}, u32[]{:S(2)}, u32[]{:S(2)}) collective-permute-start(f32[64,129]{1,0:T(8,128)S(1)} %concatenate.73), channel_id=1, source_target_pairs={{0,8},{8,16},{16,24},{24,32},{32,40},{40,48},{48,56},{56,64},{64,7... | collective-permute-start | bytes 99080 | tf_op jit(solution)/shard_map/ppermute | solution.py:33
  40.2 3.5 %copy-start.8 = (f32[64,129]{1,0:T(8,128)}, f32[64,129]{1,0:T(8,128)S(1)}, u32[]{:S(2)}) copy-start(f32[64,129]{1,0:T(8,128)S(1)} %collective-permute-done.he_ref) | copy-start | bytes 99076
  43.6 0.6 copy-start.9
  43.6 0.7 copy-start.12
  61.8 1.0 copy-start.5
  61.8 1.0 copy-start.6
  62.9 14.3 %collective-permute-start.8 = (f32[2,128]{1,0:T(2,128)S(1)}, f32[2,128]{1,0:T(2,128)S(1)}, u32[]{:S(2)}, u32[]{:S(2)}) collective-permute-start(f32[2,128]{1,0:T(2,128)S(1)} %bitcast.176), channel_id=1, source_target_pairs={{1,0},{2,1},{3,2},{4,3},{5,4},{6,5},{7,6},{9,8},{10,9},{11,10},{12... | collective-permute-start | bytes 3080 | tf_op jit(solution)/shard_map/ppermute | solution.py:34
  64.2 12.9 %collective-permute-start.7 = (f32[2,128]{1,0:T(2,128)S(1)}, f32[2,128]{1,0:T(2,128)S(1)}, u32[]{:S(2)}, u32[]{:S(2)}) collective-permute-start(f32[2,128]{1,0:T(2,128)S(1)} %bitcast.174), channel_id=1, source_target_pairs={{7,127},{15,119},{23,111},{31,103},{39,95},{47,87},{55,79},{63,71}... | collective-permute-start | bytes 3080 | tf_op jit(solution)/shard_map/ppermute | solution.py:37
  64.9 12.1 %collective-permute-start.5 = (f32[2,64]{1,0:T(2,128)S(1)}, f32[2,64]{1,0:T(2,128)S(1)}, u32[]{:S(2)}, u32[]{:S(2)}) collective-permute-start(f32[2,64]{1,0:T(2,128)S(1)} %get-tuple-element.18), channel_id=1, source_target_pairs={{8,0},{16,8},{24,16},{32,24},{40,32},{48,40},{56,48},{64,56},{72,6... | collective-permute-start | bytes 1544 | tf_op jit(solution)/shard_map/ppermute | solution.py:32
  71.5 5.3 %collective-permute-start.6 = (f32[2,64]{1,0:T(2,128)S(1)}, f32[2,64]{1,0:T(2,128)S(1)}, u32[]{:S(2)}, u32[]{:S(2)}) collective-permute-start(f32[2,64]{1,0:T(2,128)S(1)} %get-tuple-element.19), channel_id=1, source_target_pairs={{0,8},{8,16},{16,24},{24,32},{32,40},{40,48},{48,56},{56,64},{64,7... | collective-permute-start | bytes 1544 | tf_op jit(solution)/shard_map/ppermute | solution.py:33
  71.5 5.7 %collective-permute-start.9 = (f32[2,128]{1,0:T(2,128)S(1)}, f32[2,128]{1,0:T(2,128)S(1)}, u32[]{:S(2)}, u32[]{:S(2)}) collective-permute-start(f32[2,128]{1,0:T(2,128)S(1)} %bitcast.175), channel_id=1, source_target_pairs={{0,1},{1,2},{2,3},{3,4},{4,5},{5,6},{6,7},{8,9},{9,10},{10,11},{11... | collective-permute-start | bytes 3080 | tf_op jit(solution)/shard_map/ppermute | solution.py:35
  76.9 0.8 copy-start.11
  77.0 0.8 slice-start.1
  77.0 0.8 slice-start.2
  77.2 0.6 slice-start
  78.2 11.7 %collective-permute-start.14 = (f32[128]{0:T(128)S(1)}, f32[128]{0:T(128)S(1)}, u32[]{:S(2)}, u32[]{:S(2)}) collective-permute-start(f32[128]{0:T(128)S(1)} %get-tuple-element.89), channel_id=1, source_target_pairs={{0,1},{1,2},{2,3},{3,4},{4,5},{5,6},{6,7},{8,9},{9,10},{10,11},{11... | collective-permute-start | bytes 1544 | tf_op jit(solution)/shard_map/ppermute | solution.py:35
  81.8 5.2 %collective-permute-start.12 = (f32[128]{0:T(128)S(1)}, f32[128]{0:T(128)S(1)}, u32[]{:S(2)}, u32[]{:S(2)}) collective-permute-start(f32[128]{0:T(128)S(1)} %get-tuple-element.89), channel_id=1, source_target_pairs={{7,127},{15,119},{23,111},{31,103},{39,95},{47,87},{55,79},{63,71}... | collective-permute-start | bytes 1544 | tf_op jit(solution)/shard_map/ppermute | solution.py:37
  82.5 4.4 %collective-permute-start.11 = (f32[64]{0:T(128)S(1)}, f32[64]{0:T(128)S(1)}, u32[]{:S(2)}, u32[]{:S(2)}) collective-permute-start(f32[64]{0:T(128)S(1)} %get-tuple-element.24), channel_id=1, source_target_pairs={{0,8},{8,16},{16,24},{24,32},{32,40},{40,48},{48,56},{56,64},{64,7... | collective-permute-start | bytes 776 | tf_op jit(solution)/shard_map/ppermute | solution.py:33
  82.6 4.2 %collective-permute-start.10 = (f32[64]{0:T(128)S(1)}, f32[64]{0:T(128)S(1)}, u32[]{:S(2)}, u32[]{:S(2)}) collective-permute-start(f32[64]{0:T(128)S(1)} %get-tuple-element.25), channel_id=1, source_target_pairs={{8,0},{16,8},{24,16},{32,24},{40,32},{48,40},{56,48},{64,56},{72,6... | collective-permute-start | bytes 776 | tf_op jit(solution)/shard_map/ppermute | solution.py:32
  85.5 4.4 %collective-permute-start.13 = (f32[128]{0:T(128)S(1)}, f32[128]{0:T(128)S(1)}, u32[]{:S(2)}, u32[]{:S(2)}) collective-permute-start(f32[128]{0:T(128)S(1)} %get-tuple-element.88), channel_id=1, source_target_pairs={{1,0},{2,1},{3,2},{4,3},{5,4},{6,5},{7,6},{9,8},{10,9},{11,10},{12... | collective-permute-start | bytes 1544 | tf_op jit(solution)/shard_map/ppermute | solution.py:34
  120.9 8.5 %collective-permute-start.19 = (f32[128]{0:T(128)S(1)}, f32[128]{0:T(128)S(1)}, u32[]{:S(2)}, u32[]{:S(2)}) collective-permute-start(f32[128]{0:T(128)S(1)} %get-tuple-element.83), channel_id=1, source_target_pairs={{0,1},{1,2},{2,3},{3,4},{4,5},{5,6},{6,7},{8,9},{9,10},{10,11},{11... | collective-permute-start | bytes 1544 | tf_op jit(solution)/shard_map/ppermute | solution.py:35
  123.1 5.2 %collective-permute-start.17 = (f32[128]{0:T(128)S(1)}, f32[128]{0:T(128)S(1)}, u32[]{:S(2)}, u32[]{:S(2)}) collective-permute-start(f32[128]{0:T(128)S(1)} %get-tuple-element.83), channel_id=1, source_target_pairs={{7,127},{15,119},{23,111},{31,103},{39,95},{47,87},{55,79},{63,71}... | collective-permute-start | bytes 1544 | tf_op jit(solution)/shard_map/ppermute | solution.py:37
  123.8 4.4 %collective-permute-start.16 = (f32[64]{0:T(128)S(1)}, f32[64]{0:T(128)S(1)}, u32[]{:S(2)}, u32[]{:S(2)}) collective-permute-start(f32[64]{0:T(128)S(1)} %get-tuple-element.22), channel_id=1, source_target_pairs={{0,8},{8,16},{16,24},{24,32},{32,40},{40,48},{48,56},{56,64},{64,7... | collective-permute-start | bytes 776 | tf_op jit(solution)/shard_map/ppermute | solution.py:33
  125.1 3.0 %collective-permute-start.15 = (f32[64]{0:T(128)S(1)}, f32[64]{0:T(128)S(1)}, u32[]{:S(2)}, u32[]{:S(2)}) collective-permute-start(f32[64]{0:T(128)S(1)} %get-tuple-element.23), channel_id=1, source_target_pairs={{8,0},{16,8},{24,16},{32,24},{40,32},{48,40},{56,48},{64,56},{72,6... | collective-permute-start | bytes 776 | tf_op jit(solution)/shard_map/ppermute | solution.py:32
  125.1 4.3 %collective-permute-start.18 = (f32[128]{0:T(128)S(1)}, f32[128]{0:T(128)S(1)}, u32[]{:S(2)}, u32[]{:S(2)}) collective-permute-start(f32[128]{0:T(128)S(1)} %get-tuple-element.82), channel_id=1, source_target_pairs={{1,0},{2,1},{3,2},{4,3},{5,4},{6,5},{7,6},{9,8},{10,9},{11,10},{12... | collective-permute-start | bytes 1544 | tf_op jit(solution)/shard_map/ppermute | solution.py:34
  158.1 8.8 %collective-permute-start.24 = (f32[128]{0:T(128)S(1)}, f32[128]{0:T(128)S(1)}, u32[]{:S(2)}, u32[]{:S(2)}) collective-permute-start(f32[128]{0:T(128)S(1)} %get-tuple-element.76), channel_id=1, source_target_pairs={{0,1},{1,2},{2,3},{3,4},{4,5},{5,6},{6,7},{8,9},{9,10},{10,11},{11... | collective-permute-start | bytes 1544 | tf_op jit(solution)/shard_map/ppermute | solution.py:35
  160.3 6.5 %collective-permute-start.22 = (f32[128]{0:T(128)S(1)}, f32[128]{0:T(128)S(1)}, u32[]{:S(2)}, u32[]{:S(2)}) collective-permute-start(f32[128]{0:T(128)S(1)} %get-tuple-element.76), channel_id=1, source_target_pairs={{7,127},{15,119},{23,111},{31,103},{39,95},{47,87},{55,79},{63,71}... | collective-permute-start | bytes 1544 | tf_op jit(solution)/shard_map/ppermute | solution.py:37
  161.0 5.9 %collective-permute-start.23 = (f32[128]{0:T(128)S(1)}, f32[128]{0:T(128)S(1)}, u32[]{:S(2)}, u32[]{:S(2)}) collective-permute-start(f32[128]{0:T(128)S(1)} %get-tuple-element.75), channel_id=1, source_target_pairs={{1,0},{2,1},{3,2},{4,3},{5,4},{6,5},{7,6},{9,8},{10,9},{11,10},{12... | collective-permute-start | bytes 1544 | tf_op jit(solution)/shard_map/ppermute | solution.py:34
  162.3 4.4 %collective-permute-start.21 = (f32[64]{0:T(128)S(1)}, f32[64]{0:T(128)S(1)}, u32[]{:S(2)}, u32[]{:S(2)}) collective-permute-start(f32[64]{0:T(128)S(1)} %get-tuple-element.20), channel_id=1, source_target_pairs={{0,8},{8,16},{16,24},{24,32},{32,40},{40,48},{48,56},{56,64},{64,7... | collective-permute-start | bytes 776 | tf_op jit(solution)/shard_map/ppermute | solution.py:33
  163.6 3.0 %collective-permute-start.20 = (f32[64]{0:T(128)S(1)}, f32[64]{0:T(128)S(1)}, u32[]{:S(2)}, u32[]{:S(2)}) collective-permute-start(f32[64]{0:T(128)S(1)} %get-tuple-element.21), channel_id=1, source_target_pairs={{8,0},{16,8},{24,16},{32,24},{40,32},{48,40},{56,48},{64,56},{72,6... | collective-permute-start | bytes 776 | tf_op jit(solution)/shard_map/ppermute | solution.py:32

commit v6 on v5

--- a/solution.py
+++ b/solution.py
@@ -142,6 +142,42 @@
     vm_ref[...] = carry[6] / levels
 
 
+def edge_kernel(u_ref, v_ref, t_ref, s_ref, m_ref, c_ref, cf_ref, cl_ref, rf_ref, rl_ref):
+    levels, height, breadth = u_ref.shape
+    marine = m_ref[...]
+    lane = lax.broadcasted_iota(jnp.int32, cf_ref.shape, 1)
+    first = jnp.zeros(cf_ref.shape, jnp.float32)
+    last = jnp.zeros(cf_ref.shape, jnp.float32)
+    rf_ref[...] = jnp.zeros(rf_ref.shape, jnp.float32)
+    rl_ref[...] = jnp.zeros(rl_ref.shape, jnp.float32)
+    planes = [(field, level) for field in (u_ref, v_ref, t_ref, s_ref) for level in range(levels)]
+    for index, (field, level) in enumerate(planes + [(c_ref, None)]):
+        if level is None:
+            masked = field[...]
+        else:
+            masked = field[level] * marine
+        first = jnp.where(lane == index, masked[:, 0:1], first)
+        last = jnp.where(lane == index, masked[:, breadth - 1 : breadth], last)
+        rf_ref[index : index + 1, :] = masked[0:1, :]
+        rl_ref[index : index + 1, :] = masked[height - 1 : height, :]
+    cf_ref[...] = first
+    cl_ref[...] = last
+
+
+def edge_step(u, v, t, s, marine, column):
+    levels, height, breadth = u.shape
+    count = 4 * levels + 1
+    lanes = -(-count // 128) * 128
+    rows = -(-count // 8) * 8
+    cols = jax.ShapeDtypeStruct((height, lanes), jnp.float32)
+    flat = jax.ShapeDtypeStruct((rows, breadth), jnp.float32)
+    return pl.pallas_call(
+        edge_kernel,
+        out_shape=(cols, cols, flat, flat),
+        interpret=INTERPRET,
+    )(u, v, t, s, marine, column)
+
+
 def column_step(u, v, t, s, marine, coriolis, he, hw, hn, hs):
     levels, height, breadth = u.shape
     field = jax.ShapeDtypeStruct((levels, height, breadth), jnp.float32)
@@ -175,26 +211,14 @@
     open_cells = marine_snapshot * kept
     column = seabed_thickness * open_cells
 
-    raw = (zonal_current, meridional_current, warmth_anomaly, brine_anomaly)
-
-    def row_edges(at):
-        return jnp.concatenate(
-            [item[:, at, :] * marine_snapshot[at] for item in raw] + [column[at][None]], axis=0
-        )
-
-    def col_edges(at):
-        return jnp.concatenate(
-            [(item[:, :, at] * marine_snapshot[:, at]).T for item in raw] + [column[:, at][:, None]],
-            axis=1,
-        )
-
-    parity = jnp.concatenate(
-        [
-            -jnp.ones((2 * level_fields,), jnp.float32),
-            jnp.ones((2 * level_fields + 1,), jnp.float32),
-        ]
-    )[:, None]
-    halo_all = exchange(col_edges(0), col_edges(-1), row_edges(0), row_edges(-1), parity)
+
+    edge_cols_first, edge_cols_last, edge_rows_first, edge_rows_last = edge_step(
+        zonal_current, meridional_current, warmth_anomaly, brine_anomaly, marine_snapshot, column
+    )
+    parity = jnp.where(
+        jnp.arange(edge_rows_first.shape[0]) < 2 * level_fields, -1.0, 1.0
+    ).astype(jnp.float32)[:, None]
+    halo_all = exchange(edge_cols_first, edge_cols_last, edge_rows_first, edge_rows_last, parity)
     halo_c = (
         halo_all[0][:, 4 * level_fields],
         halo_all[1][:, 4 * level_fields],

time: 197 us -> 173 us (0.88)
  local copies, waits for them, and re-layouts: 28.7 us -> 7.05 us
  other arithmetic: 11.7 us -> 5.71 us
  Pallas kernels: 15.2 us -> 21 us
    unnamed x34 -> x18, local copies, waits for them, and re-layouts: 10.5 us -> 1.15 us
    slice x11 -> x0, local copies, waits for them, and re-layouts: 9.31 us -> none  [the longest x4 5.06 us: col_edges(): item[:, :, at] * marine_snapshot[:, at]]
    pallas_call x0 -> x1, Pallas kernels: none -> 5.77 us  [edge_step(): pl.pallas_call(edge_kernel, out_shape=(cols, cols, flat, flat), interpret...]
    unnamed x8 -> x0, other arithmetic: 4.81 us -> none
    concatenate x4 -> x0, local copies, waits for them, and re-layouts: 2.75 us -> none  [the longest x2 2.56 us: row_edges(): jnp.concatenate([item[:, at, :] * marine_snapshot[at] for item in raw] +...]
    ppermute x5, starting transfers between devices: 10.5 us -> 12.9 us  [exchange(): lax.ppermute(first_col, 'lon', [((i + 1) % lon_count, i) for i in range(l...]
  transfers between devices with their start and end apart: 25 -> 25, of which waited for: 6 -> 7; matrix products, arithmetic and copies ran while one was open for 12% -> 1% of each run, Pallas kernels for 0% -> 0%
where the time goes in v6:
time: 173 us; the launch traced here: 172 us
  blocking collectives  72.7 us (42%)
  starting transfers between devices  43.2 us (25%)
  Pallas kernels  21 us (12%)
  waiting for transfers between devices  12.2 us (7%)
  between operations  10.7 us (6%)
  local copies, waits for them, and re-layouts  7.05 us (4%)
  other arithmetic  5.71 us (3%)
    all_to_all x3, blocking collectives, allsum(): gathered = lax.all_to_all(spread, ('lon', 'lat'), 0, 0, tiled=True)  72.7 us
    ppermute x5, starting transfers between devices, exchange(): lax.ppermute(last_row, 'lat', [(i, i + 1) for i in range(lat_count - 1)])  16.2 us
    pallas_call x1, Pallas kernels, column_step(): pl.pallas_call(column_kernel, out_shape=(field, field, field, field, plan...  15.2 us
    ppermute x5, starting transfers between devices, exchange(): lax.ppermute(first_col, 'lon', [((i + 1) % lon_count, i) for i in range(l...  12.9 us
    ppermute x5, starting transfers between devices, exchange(): lax.ppermute(first_row, 'lat', [(i + 1, i) for i in range(lat_count - 1)])  6.6 us
    pallas_call x1, Pallas kernels, edge_step(): pl.pallas_call(edge_kernel, out_shape=(cols, cols, flat, flat), interpret...  5.77 us
    ppermute x5, waiting for transfers between devices, exchange(): lax.ppermute(first_col, 'lon', [((i + 1) % lon_count, i) for i in range(l...  5.03 us
    ppermute x5, starting transfers between devices, exchange(): lax.ppermute(last_col, 'lon', [(i, (i + 1) % lon_count) for i in range(lo...  4.29 us
  transfers between devices with their start and end apart: 25, of which 7 were waited for; matrix products, arithmetic and copies ran while one was open for 1% of the time, Pallas kernels for 0%

profile of v6, /device:TPU:1, one launch (start us, length us, event | category | flops | bytes accessed | tf_op | source)
XLA Modules:
  0.0 172.5 jit_solution(4139187120605746809)
XLA Ops:
  0.6 0.7 convert_element_type.15
  1.6 0.6 convert_element_type.13.m_ref
  2.3 0.7 copy-done.7
  3.0 0.6 fusion.46
  3.6 5.8 %shard_map.127 = (f32[64,256]{1,0:T(8,128)}, f32[64,256]{1,0:T(8,128)}, f32[136,128]{1,0:T(8,128)}, f32[136,128]{1,0:T(8,128)}) custom-call(f32[32,64,128]{2,1,0:T(8,128)} %u_ref.3, f32[32,64,128]{2,1,0:T(8,128)} %v_ref.3, f32[32,64,128]{2,1,0:T(8,128)} %t_ref.3, f32[32,64,128]{2,1,0:T(8,128)} %s_ref.3, f32[64,128]{1,0:T(8,128)} %convert_element_type.13.m_ref, ...), custom_call_target="tpu_custom_call" | custom-call | tf_op jit(solution)/shard_map/pallas_call | solution.py:174
  9.4 3.9 %collective-permute-start.4 = (f32[136,128]{1,0:T(8,128)}, f32[136,128]{1,0:T(8,128)S(1)}, u32[]{:S(2)}, u32[]{:S(2)}) collective-permute-start(f32[136,128]{1,0:T(8,128)} %get-tuple-element.18), channel_id=1, source_target_pairs={{0,1},{1,2},{2,3},{3,4},{4,5},{5,6},{6,7},{8,9},{9,10},{10,11},{11... | collective-permute-start | bytes 208904 | tf_op jit(solution)/shard_map/ppermute | solution.py:35
  13.3 0.7 collective-permute-start.2
  14.0 1.0 collective-permute-start
  15.0 1.6 collective-permute-start.1
  16.6 1.5 collective-permute-start.3
  18.2 0.5 collective-permute-done.he_ref
  18.7 3.1 %collective-permute-done.1.hw_ref = f32[64,256]{1,0:T(8,128)S(1)} collective-permute-done((f32[64,256]{1,0:T(8,128)}, f32[64,256]{1,0:T(8,128)S(1)}, u32[]{:S(2)}, u32[]{:S(2)}) %collective-permute-start.1) | collective-permute-done | bytes 65568 | tf_op jit(solution)/shard_map/ppermute | solution.py:33
  21.8 0.2 rev.15
  22.0 0.4 copy-done.4
  22.4 0.7 multiply_select_fusion.hn_ref
  23.1 0.7 broadcast_in_dim.78.f_ref
  23.8 15.2 %shard_map.128 = (f32[32,64,128]{2,1,0:T(8,128)}, f32[32,64,128]{2,1,0:T(8,128)}, f32[32,64,128]{2,1,0:T(8,128)}, f32[32,64,128]{2,1,0:T(8,128)}, f32[64,128]{1,0:T(8,128)}, /*index=5*/f32[64,128]{1,0:T(8,128)}) custom-call(f32[32,64,128]{2,1,0:T(8,128)} %u_ref.3, f32[32,64,128]{2,1,0:T(8,128)} %v_ref.3, f32[32,64,128]{2,1,0:T(8,128)} %t_ref.3, ...), custom_call_target="tpu_custom_call" | custom-call | tf_op jit(solution)/shard_map/pallas_call | solution.py:185
  39.0 1.0 fusion.2
  40.2 1.3 collective-permute-start.8
  41.4 0.7 collective-permute-start.7
  42.1 6.6 %collective-permute-start.5 = (f32[2,64]{1,0:T(2,128)S(1)}, f32[2,64]{1,0:T(2,128)S(1)}, u32[]{:S(2)}, u32[]{:S(2)}) collective-permute-start(f32[2,64]{1,0:T(2,128)S(1)} %get-tuple-element.26), channel_id=1, source_target_pairs={{8,0},{16,8},{24,16},{32,24},{40,32},{48,40},{56,48},{64,56},{72,6... | collective-permute-start | bytes 1544 | tf_op jit(solution)/shard_map/ppermute | solution.py:32
  48.8 4.3 %collective-permute-start.9 = (f32[2,128]{1,0:T(2,128)S(1)}, f32[2,128]{1,0:T(2,128)S(1)}, u32[]{:S(2)}, u32[]{:S(2)}) collective-permute-start(f32[2,128]{1,0:T(2,128)S(1)} %bitcast.91), channel_id=1, source_target_pairs={{0,1},{1,2},{2,3},{3,4},{4,5},{5,6},{6,7},{8,9},{9,10},{10,11},{11... | collective-permute-start | bytes 3080 | tf_op jit(solution)/shard_map/ppermute | solution.py:35
  53.4 0.3 collective-permute-done.9
  54.0 0.4 slice-done
  54.5 0.2 slice_reduce_fusion.4
  54.7 3.6 %collective-permute-start.14 = (f32[128]{0:T(128)S(1)}, f32[128]{0:T(128)S(1)}, u32[]{:S(2)}, u32[]{:S(2)}) collective-permute-start(f32[128]{0:T(128)S(1)} %get-tuple-element.79), channel_id=1, source_target_pairs={{0,1},{1,2},{2,3},{3,4},{4,5},{5,6},{6,7},{8,9},{9,10},{10,11},{11... | collective-permute-start | bytes 1544 | tf_op jit(solution)/shard_map/ppermute | solution.py:35
  58.3 0.7 collective-permute-start.12
  59.1 5.2 %collective-permute-start.10 = (f32[64]{0:T(128)S(1)}, f32[64]{0:T(128)S(1)}, u32[]{:S(2)}, u32[]{:S(2)}) collective-permute-start(f32[64]{0:T(128)S(1)} %get-tuple-element.33), channel_id=1, source_target_pairs={{8,0},{16,8},{24,16},{32,24},{40,32},{48,40},{56,48},{64,56},{72,6... | collective-permute-start | bytes 776 | tf_op jit(solution)/shard_map/ppermute | solution.py:32
  64.3 1.3 collective-permute-start.13
  65.9 2.6 %collective-permute-done.13 = f32[128]{0:T(128)S(1)} collective-permute-done((f32[128]{0:T(128)S(1)}, f32[128]{0:T(128)S(1)}, u32[]{:S(2)}, u32[]{:S(2)}) %collective-permute-start.13) | collective-permute-done | bytes 544 | tf_op jit(solution)/shard_map/ppermute | solution.py:34
  68.8 26.8 %all_to_all.18 = f32[128,1,2]{2,1,0:T(1,128)S(1)} all-to-all(f32[128,1,2]{2,1,0:T(1,128)S(1)} %broadcast_in_dim.91), channel_id=1, replica_groups=mesh['lon'=16,'lat'=8] {'lon','lat'}, dimensions={0} | all-to-all | bytes 2048 | tf_op jit(solution)/shard_map/all_to_all | solution.py:25
  95.8 0.6 fusion.57
  97.9 2.2 %collective-permute-start.19 = (f32[128]{0:T(128)S(1)}, f32[128]{0:T(128)S(1)}, u32[]{:S(2)}, u32[]{:S(2)}) collective-permute-start(f32[128]{0:T(128)S(1)} %get-tuple-element.73), channel_id=1, source_target_pairs={{0,1},{1,2},{2,3},{3,4},{4,5},{5,6},{6,7},{8,9},{9,10},{10,11},{11... | collective-permute-start | bytes 1544 | tf_op jit(solution)/shard_map/ppermute | solution.py:35
  100.1 0.7 collective-permute-start.17
  100.8 1.3 collective-permute-start.16
  102.1 1.3 collective-permute-start.18
  103.5 1.6 collective-permute-done.15
  105.4 1.0 collective-permute-done.18
  106.7 22.8 %all_to_all.19 = f32[128,1,4]{2,1,0:T(1,128)S(1)} all-to-all(f32[128,1,4]{2,1,0:T(1,128)S(1)} %broadcast_in_dim.96), channel_id=1, replica_groups=mesh['lon'=16,'lat'=8] {'lon','lat'}, dimensions={0} | all-to-all | bytes 4096 | tf_op jit(solution)/shard_map/all_to_all | solution.py:25
  129.7 0.7 fusion.56
  135.1 2.2 %collective-permute-start.24 = (f32[128]{0:T(128)S(1)}, f32[128]{0:T(128)S(1)}, u32[]{:S(2)}, u32[]{:S(2)}) collective-permute-start(f32[128]{0:T(128)S(1)} %get-tuple-element.66), channel_id=1, source_target_pairs={{0,1},{1,2},{2,3},{3,4},{4,5},{5,6},{6,7},{8,9},{9,10},{10,11},{11... | collective-permute-start | bytes 1544 | tf_op jit(solution)/shard_map/ppermute | solution.py:35
  137.3 0.7 collective-permute-start.22
  137.9 1.3 collective-permute-start.23
  139.2 1.3 collective-permute-start.21
  140.6 2.9 %collective-permute-done.20 = f32[64]{0:T(128)S(1)} collective-permute-done((f32[64]{0:T(128)S(1)}, f32[64]{0:T(128)S(1)}, u32[]{:S(2)}, u32[]{:S(2)}) %collective-permute-start.20) | collective-permute-done | bytes 288 | tf_op jit(solution)/shard_map/ppermute | solution.py:32
  144.1 23.0 %all_to_all.20 = f32[128,1,4]{2,1,0:T(1,128)S(1)} all-to-all(f32[128,1,4]{2,1,0:T(1,128)S(1)} %broadcast_in_dim.101), channel_id=1, replica_groups=mesh['lon'=16,'lat'=8] {'lon','lat'}, dimensions={0} | all-to-all | bytes 4096 | tf_op jit(solution)/shard_map/all_to_all | solution.py:25
  167.3 0.7 fusion.55
  171.8 0.6 multiply_subtract_fusion
  (101 shorter events, 4.0 us)
Async XLA Ops:
  0.6 0.9 copy-start.5
  2.2 0.8 copy-start.7
  3.6 14.5 %copy-start = (f32[64,128]{1,0:T(8,128)S(1)}, f32[64,128]{1,0:T(8,128)}, u32[]{:S(2)}) copy-start(f32[64,128]{1,0:T(8,128)} %get-tuple-element.54.c_ref) | copy-start | bytes 98308
  9.4 13.8 %collective-permute-start.4 = (f32[136,128]{1,0:T(8,128)}, f32[136,128]{1,0:T(8,128)S(1)}, u32[]{:S(2)}, u32[]{:S(2)}) collective-permute-start(f32[136,128]{1,0:T(8,128)} %get-tuple-element.18), channel_id=1, source_target_pairs={{0,1},{1,2},{2,3},{3,4},{4,5},{5,6},{6,7},{8,9},{9,10},{10,11},{11... | collective-permute-start | bytes 208904 | tf_op jit(solution)/shard_map/ppermute | solution.py:35
  13.3 8.5 %collective-permute-start.2 = (f32[136,128]{1,0:T(8,128)}, f32[136,128]{1,0:T(8,128)S(1)}, u32[]{:S(2)}, u32[]{:S(2)}) collective-permute-start(f32[136,128]{1,0:T(8,128)} %get-tuple-element.18), channel_id=1, source_target_pairs={{7,127},{15,119},{23,111},{31,103},{39,95},{47,87},{55,79},{63,71}... | collective-permute-start | bytes 208904 | tf_op jit(solution)/shard_map/ppermute | solution.py:37
  14.0 4.7 %collective-permute-start = (f32[64,256]{1,0:T(8,128)}, f32[64,256]{1,0:T(8,128)S(1)}, u32[]{:S(2)}, u32[]{:S(2)}) collective-permute-start(f32[64,256]{1,0:T(8,128)} %get-tuple-element.16), channel_id=1, source_target_pairs={{8,0},{16,8},{24,16},{32,24},{40,32},{48,40},{56,48},{64,56},{72,6... | collective-permute-start | bytes 196616 | tf_op jit(solution)/shard_map/ppermute | solution.py:32
  15.0 6.8 %collective-permute-start.1 = (f32[64,256]{1,0:T(8,128)}, f32[64,256]{1,0:T(8,128)S(1)}, u32[]{:S(2)}, u32[]{:S(2)}) collective-permute-start(f32[64,256]{1,0:T(8,128)} %get-tuple-element.17), channel_id=1, source_target_pairs={{0,8},{8,16},{16,24},{24,32},{32,40},{40,48},{48,56},{56,64},{64,7... | collective-permute-start | bytes 196616 | tf_op jit(solution)/shard_map/ppermute | solution.py:33
  16.6 5.8 %collective-permute-start.3 = (f32[136,128]{1,0:T(8,128)}, f32[136,128]{1,0:T(8,128)S(1)}, u32[]{:S(2)}, u32[]{:S(2)}) collective-permute-start(f32[136,128]{1,0:T(8,128)} %get-tuple-element.19), channel_id=1, source_target_pairs={{1,0},{2,1},{3,2},{4,3},{5,4},{6,5},{7,6},{9,8},{10,9},{11,10},{12... | collective-permute-start | bytes 208904 | tf_op jit(solution)/shard_map/ppermute | solution.py:34
  18.7 3.1 %copy-start.3 = (f32[64,256]{1,0:T(8,128)}, f32[64,256]{1,0:T(8,128)S(1)}, u32[]{:S(2)}) copy-start(f32[64,256]{1,0:T(8,128)S(1)} %collective-permute-done.he_ref) | copy-start | bytes 196612
  21.8 0.6 copy-start.4
  23.1 0.7 copy-start.6
  39.0 1.0 copy-start.1
  39.0 1.0 copy-start.2
  40.2 13.3 %collective-permute-start.8 = (f32[2,128]{1,0:T(2,128)S(1)}, f32[2,128]{1,0:T(2,128)S(1)}, u32[]{:S(2)}, u32[]{:S(2)}) collective-permute-start(f32[2,128]{1,0:T(2,128)S(1)} %bitcast.92), channel_id=1, source_target_pairs={{1,0},{2,1},{3,2},{4,3},{5,4},{6,5},{7,6},{9,8},{10,9},{11,10},{12... | collective-permute-start | bytes 3080 | tf_op jit(solution)/shard_map/ppermute | solution.py:34
  41.4 11.9 %collective-permute-start.7 = (f32[2,128]{1,0:T(2,128)S(1)}, f32[2,128]{1,0:T(2,128)S(1)}, u32[]{:S(2)}, u32[]{:S(2)}) collective-permute-start(f32[2,128]{1,0:T(2,128)S(1)} %bitcast.90), channel_id=1, source_target_pairs={{7,127},{15,119},{23,111},{31,103},{39,95},{47,87},{55,79},{63,71}... | collective-permute-start | bytes 3080 | tf_op jit(solution)/shard_map/ppermute | solution.py:37
  42.1 11.0 %collective-permute-start.5 = (f32[2,64]{1,0:T(2,128)S(1)}, f32[2,64]{1,0:T(2,128)S(1)}, u32[]{:S(2)}, u32[]{:S(2)}) collective-permute-start(f32[2,64]{1,0:T(2,128)S(1)} %get-tuple-element.26), channel_id=1, source_target_pairs={{8,0},{16,8},{24,16},{32,24},{40,32},{48,40},{56,48},{64,56},{72,6... | collective-permute-start | bytes 1544 | tf_op jit(solution)/shard_map/ppermute | solution.py:32
  48.7 4.3 %collective-permute-start.6 = (f32[2,64]{1,0:T(2,128)S(1)}, f32[2,64]{1,0:T(2,128)S(1)}, u32[]{:S(2)}, u32[]{:S(2)}) collective-permute-start(f32[2,64]{1,0:T(2,128)S(1)} %get-tuple-element.27), channel_id=1, source_target_pairs={{0,8},{8,16},{16,24},{24,32},{32,40},{40,48},{48,56},{56,64},{64,7... | collective-permute-start | bytes 1544 | tf_op jit(solution)/shard_map/ppermute | solution.py:33
  48.8 5.0 %collective-permute-start.9 = (f32[2,128]{1,0:T(2,128)S(1)}, f32[2,128]{1,0:T(2,128)S(1)}, u32[]{:S(2)}, u32[]{:S(2)}) collective-permute-start(f32[2,128]{1,0:T(2,128)S(1)} %bitcast.91), channel_id=1, source_target_pairs={{0,1},{1,2},{2,3},{3,4},{4,5},{5,6},{6,7},{8,9},{9,10},{10,11},{11... | collective-permute-start | bytes 3080 | tf_op jit(solution)/shard_map/ppermute | solution.py:35
  53.0 0.8 copy-start.8
  53.2 0.8 slice-start.1
  53.2 0.8 slice-start.2
  53.7 0.6 slice-start
  53.7 0.6 slice-start.3
  54.7 13.9 %collective-permute-start.14 = (f32[128]{0:T(128)S(1)}, f32[128]{0:T(128)S(1)}, u32[]{:S(2)}, u32[]{:S(2)}) collective-permute-start(f32[128]{0:T(128)S(1)} %get-tuple-element.79), channel_id=1, source_target_pairs={{0,1},{1,2},{2,3},{3,4},{4,5},{5,6},{6,7},{8,9},{9,10},{10,11},{11... | collective-permute-start | bytes 1544 | tf_op jit(solution)/shard_map/ppermute | solution.py:35
  58.3 7.5 %collective-permute-start.12 = (f32[128]{0:T(128)S(1)}, f32[128]{0:T(128)S(1)}, u32[]{:S(2)}, u32[]{:S(2)}) collective-permute-start(f32[128]{0:T(128)S(1)} %get-tuple-element.79), channel_id=1, source_target_pairs={{7,127},{15,119},{23,111},{31,103},{39,95},{47,87},{55,79},{63,71}... | collective-permute-start | bytes 1544 | tf_op jit(solution)/shard_map/ppermute | solution.py:37
  59.0 6.7 %collective-permute-start.11 = (f32[64]{0:T(128)S(1)}, f32[64]{0:T(128)S(1)}, u32[]{:S(2)}, u32[]{:S(2)}) collective-permute-start(f32[64]{0:T(128)S(1)} %get-tuple-element.32), channel_id=1, source_target_pairs={{0,8},{8,16},{16,24},{24,32},{32,40},{40,48},{48,56},{56,64},{64,7... | collective-permute-start | bytes 776 | tf_op jit(solution)/shard_map/ppermute | solution.py:33
  59.1 6.6 %collective-permute-start.10 = (f32[64]{0:T(128)S(1)}, f32[64]{0:T(128)S(1)}, u32[]{:S(2)}, u32[]{:S(2)}) collective-permute-start(f32[64]{0:T(128)S(1)} %get-tuple-element.33), channel_id=1, source_target_pairs={{8,0},{16,8},{24,16},{32,24},{40,32},{48,40},{56,48},{64,56},{72,6... | collective-permute-start | bytes 776 | tf_op jit(solution)/shard_map/ppermute | solution.py:32
  64.3 4.3 %collective-permute-start.13 = (f32[128]{0:T(128)S(1)}, f32[128]{0:T(128)S(1)}, u32[]{:S(2)}, u32[]{:S(2)}) collective-permute-start(f32[128]{0:T(128)S(1)} %get-tuple-element.78), channel_id=1, source_target_pairs={{1,0},{2,1},{3,2},{4,3},{5,4},{6,5},{7,6},{9,8},{10,9},{11,10},{12... | collective-permute-start | bytes 1544 | tf_op jit(solution)/shard_map/ppermute | solution.py:34
  97.9 8.5 %collective-permute-start.19 = (f32[128]{0:T(128)S(1)}, f32[128]{0:T(128)S(1)}, u32[]{:S(2)}, u32[]{:S(2)}) collective-permute-start(f32[128]{0:T(128)S(1)} %get-tuple-element.73), channel_id=1, source_target_pairs={{0,1},{1,2},{2,3},{3,4},{4,5},{5,6},{6,7},{8,9},{9,10},{10,11},{11... | collective-permute-start | bytes 1544 | tf_op jit(solution)/shard_map/ppermute | solution.py:35
  100.1 5.2 %collective-permute-start.17 = (f32[128]{0:T(128)S(1)}, f32[128]{0:T(128)S(1)}, u32[]{:S(2)}, u32[]{:S(2)}) collective-permute-start(f32[128]{0:T(128)S(1)} %get-tuple-element.73), channel_id=1, source_target_pairs={{7,127},{15,119},{23,111},{31,103},{39,95},{47,87},{55,79},{63,71}... | collective-permute-start | bytes 1544 | tf_op jit(solution)/shard_map/ppermute | solution.py:37
  100.8 4.4 %collective-permute-start.16 = (f32[64]{0:T(128)S(1)}, f32[64]{0:T(128)S(1)}, u32[]{:S(2)}, u32[]{:S(2)}) collective-permute-start(f32[64]{0:T(128)S(1)} %get-tuple-element.30), channel_id=1, source_target_pairs={{0,8},{8,16},{16,24},{24,32},{32,40},{40,48},{48,56},{56,64},{64,7... | collective-permute-start | bytes 776 | tf_op jit(solution)/shard_map/ppermute | solution.py:33
  102.1 3.0 %collective-permute-start.15 = (f32[64]{0:T(128)S(1)}, f32[64]{0:T(128)S(1)}, u32[]{:S(2)}, u32[]{:S(2)}) collective-permute-start(f32[64]{0:T(128)S(1)} %get-tuple-element.31), channel_id=1, source_target_pairs={{8,0},{16,8},{24,16},{32,24},{40,32},{48,40},{56,48},{64,56},{72,6... | collective-permute-start | bytes 776 | tf_op jit(solution)/shard_map/ppermute | solution.py:32
  102.1 4.3 %collective-permute-start.18 = (f32[128]{0:T(128)S(1)}, f32[128]{0:T(128)S(1)}, u32[]{:S(2)}, u32[]{:S(2)}) collective-permute-start(f32[128]{0:T(128)S(1)} %get-tuple-element.72), channel_id=1, source_target_pairs={{1,0},{2,1},{3,2},{4,3},{5,4},{6,5},{7,6},{9,8},{10,9},{11,10},{12... | collective-permute-start | bytes 1544 | tf_op jit(solution)/shard_map/ppermute | solution.py:34
  135.1 8.8 %collective-permute-start.24 = (f32[128]{0:T(128)S(1)}, f32[128]{0:T(128)S(1)}, u32[]{:S(2)}, u32[]{:S(2)}) collective-permute-start(f32[128]{0:T(128)S(1)} %get-tuple-element.66), channel_id=1, source_target_pairs={{0,1},{1,2},{2,3},{3,4},{4,5},{5,6},{6,7},{8,9},{9,10},{10,11},{11... | collective-permute-start | bytes 1544 | tf_op jit(solution)/shard_map/ppermute | solution.py:35
  137.3 6.5 %collective-permute-start.22 = (f32[128]{0:T(128)S(1)}, f32[128]{0:T(128)S(1)}, u32[]{:S(2)}, u32[]{:S(2)}) collective-permute-start(f32[128]{0:T(128)S(1)} %get-tuple-element.66), channel_id=1, source_target_pairs={{7,127},{15,119},{23,111},{31,103},{39,95},{47,87},{55,79},{63,71}... | collective-permute-start | bytes 1544 | tf_op jit(solution)/shard_map/ppermute | solution.py:37
  137.9 5.9 %collective-permute-start.23 = (f32[128]{0:T(128)S(1)}, f32[128]{0:T(128)S(1)}, u32[]{:S(2)}, u32[]{:S(2)}) collective-permute-start(f32[128]{0:T(128)S(1)} %get-tuple-element.65), channel_id=1, source_target_pairs={{1,0},{2,1},{3,2},{4,3},{5,4},{6,5},{7,6},{9,8},{10,9},{11,10},{12... | collective-permute-start | bytes 1544 | tf_op jit(solution)/shard_map/ppermute | solution.py:34
  139.2 4.4 %collective-permute-start.21 = (f32[64]{0:T(128)S(1)}, f32[64]{0:T(128)S(1)}, u32[]{:S(2)}, u32[]{:S(2)}) collective-permute-start(f32[64]{0:T(128)S(1)} %get-tuple-element.28), channel_id=1, source_target_pairs={{0,8},{8,16},{16,24},{24,32},{32,40},{40,48},{48,56},{56,64},{64,7... | collective-permute-start | bytes 776 | tf_op jit(solution)/shard_map/ppermute | solution.py:33
  140.5 3.0 %collective-permute-start.20 = (f32[64]{0:T(128)S(1)}, f32[64]{0:T(128)S(1)}, u32[]{:S(2)}, u32[]{:S(2)}) collective-permute-start(f32[64]{0:T(128)S(1)} %get-tuple-element.29), channel_id=1, source_target_pairs={{8,0},{16,8},{24,16},{32,24},{40,32},{48,40},{56,48},{64,56},{72,6... | collective-permute-start | bytes 776 | tf_op jit(solution)/shard_map/ppermute | solution.py:32

commit v7 on v6

--- a/solution.py
+++ b/solution.py
@@ -267,35 +267,73 @@
             - weights[3] * near_x[3]
         )
 
-    solution = jnp.zeros_like(rhs)
-    residual = rhs
-    precond = residual / diag
-    direction = precond
-    image = apply(direction, halos(direction, unit))
-    pair = allsum(jnp.sum(jnp.stack([residual * precond, direction * image]), axis=(1, 2)))
-    product_now = pair[0]
-    curvature = pair[1]
-    for step in range(ITERS):
+    basis_v0 = rhs / diag
+    basis_w1 = apply(basis_v0, halos(basis_v0, unit))
+    basis_v1 = basis_w1 / diag
+    basis_w2 = apply(basis_v1, halos(basis_v1, unit))
+    gram = allsum(
+        jnp.sum(
+            jnp.stack(
+                [
+                    basis_v0 * rhs,
+                    basis_v0 * basis_w1,
+                    basis_v0 * basis_w2,
+                    basis_v1 * rhs,
+                    basis_v1 * basis_w1,
+                    basis_v1 * basis_w2,
+                ]
+            ),
+            axis=(1, 2),
+        )
+    )
+    product_now = gram[0]
+    alpha = product_now / gram[1]
+    solution = alpha * basis_v0
+    residual = rhs - alpha * basis_w1
+    direction = basis_v0
+    image = basis_w1
+    if ITERS > 1:
+        shift = -alpha
+        product_next = gram[0] + shift * (gram[1] + gram[3]) + shift * shift * gram[4]
+        beta = product_next / product_now
+        first = 1.0 + beta
+        curvature = (
+            first * first * gram[1]
+            + first * shift * (gram[2] + gram[4])
+            + shift * shift * gram[5]
+        )
+        product_now = product_next
+        alpha = product_now / curvature
+        direction = first * basis_v0 + shift * basis_v1
+        image = first * basis_w1 + shift * basis_w2
+        solution = solution + alpha * direction
+        residual = rhs + (shift - alpha * first) * basis_w1 - (alpha * shift) * basis_w2
+    for step in range(2, ITERS):
+        precond = residual / diag
+        image_z = apply(precond, halos(precond, unit))
+        sums = allsum(
+            jnp.sum(
+                jnp.stack(
+                    [
+                        residual * precond,
+                        precond * image_z,
+                        precond * image,
+                        direction * image_z,
+                        direction * image,
+                    ]
+                ),
+                axis=(1, 2),
+            )
+        )
+        product_next = sums[0]
+        beta = product_next / product_now
+        curvature = sums[1] + beta * (sums[2] + sums[3]) + beta * beta * sums[4]
+        direction = precond + beta * direction
+        image = image_z + beta * image
+        product_now = product_next
         alpha = product_now / curvature
         solution = solution + alpha * direction
         residual = residual - alpha * image
-        if step + 1 < ITERS:
-            precond = residual / diag
-            image_z = apply(precond, halos(precond, unit))
-            sums = allsum(
-                jnp.sum(
-                    jnp.stack(
-                        [residual * precond, precond * image_z, precond * image, direction * image_z]
-                    ),
-                    axis=(1, 2),
-                )
-            )
-            product_next = sums[0]
-            beta = product_next / product_now
-            curvature = sums[1] + beta * (sums[2] + sums[3]) + beta * beta * curvature
-            direction = precond + beta * direction
-            image = image_z + beta * image
-            product_now = product_next
     return (zonal_next, merid_next, tracers[0], tracers[1], solution, residual)
 
 

time: 173 us -> 158 us (0.913)
  blocking collectives: 72.7 us -> 47.4 us
  starting transfers between devices: 43.2 us -> 50.7 us
  waiting for transfers between devices: 12.2 us -> 14 us
    all_to_all x3 -> x2, blocking collectives: 72.7 us -> 47.4 us  [allsum(): gathered = lax.all_to_all(spread, ('lon', 'lat'), 0, 0, tiled=True)]
    ppermute x5, starting transfers between devices: 12.9 us -> 19.4 us  [exchange(): lax.ppermute(first_col, 'lon', [((i + 1) % lon_count, i) for i in range(l...]
    ppermute x5, waiting for transfers between devices: 3.66 us -> 8.4 us  [exchange(): lax.ppermute(first_row, 'lat', [(i + 1, i) for i in range(lat_count - 1)])]
    ppermute x5, waiting for transfers between devices: 5.03 us -> 2.12 us  [exchange(): lax.ppermute(first_col, 'lon', [((i + 1) % lon_count, i) for i in range(l...]
    ppermute x5, starting transfers between devices: 16.2 us -> 18.1 us  [exchange(): lax.ppermute(last_row, 'lat', [(i, i + 1) for i in range(lat_count - 1)])]
  transfers between devices with their start and end apart: 25 -> 25, of which waited for: 7 -> 7; matrix products, arithmetic and copies ran while one was open for 1% -> 2% of each run, Pallas kernels for 0% -> 0%
where the time goes in v7:
time: 158 us; the launch traced here: 157 us
  starting transfers between devices  50.7 us (32%)
  blocking collectives  47.4 us (30%)
  Pallas kernels  21 us (13%)
  waiting for transfers between devices  14 us (9%)
  between operations  12 us (8%)
  local copies, waits for them, and re-layouts  6.38 us (4%)
  other arithmetic  5.48 us (3%)
    all_to_all x2, blocking collectives, allsum(): gathered = lax.all_to_all(spread, ('lon', 'lat'), 0, 0, tiled=True)  47.4 us
    ppermute x5, starting transfers between devices, exchange(): lax.ppermute(first_col, 'lon', [((i + 1) % lon_count, i) for i in range(l...  19.4 us
    ppermute x5, starting transfers between devices, exchange(): lax.ppermute(last_row, 'lat', [(i, i + 1) for i in range(lat_count - 1)])  18.1 us
    pallas_call x1, Pallas kernels, column_step(): pl.pallas_call(column_kernel, out_shape=(field, field, field, field, plan...  15.2 us
    ppermute x5, waiting for transfers between devices, exchange(): lax.ppermute(first_row, 'lat', [(i + 1, i) for i in range(lat_count - 1)])  8.4 us
    ppermute x5, starting transfers between devices, exchange(): lax.ppermute(first_row, 'lat', [(i + 1, i) for i in range(lat_count - 1)])  6.59 us
    pallas_call x1, Pallas kernels, edge_step(): pl.pallas_call(edge_kernel, out_shape=(cols, cols, flat, flat), interpret...  5.77 us
    ppermute x5, starting transfers between devices, exchange(): lax.ppermute(last_row, ('lon', 'lat'), [(i * lat_count + top, (lon_count...  3.31 us
  transfers between devices with their start and end apart: 25, of which 7 were waited for; matrix products, arithmetic and copies ran while one was open for 2% of the time, Pallas kernels for 0%

profile of v7, /device:TPU:1, one launch (start us, length us, event | category | flops | bytes accessed | tf_op | source)
XLA Modules:
  0.0 156.8 jit_solution(2446139220365957108)
XLA Ops:
  0.6 0.7 convert_element_type.15
  1.6 0.6 convert_element_type.13.m_ref
  2.3 0.7 copy-done.7
  3.0 0.6 fusion.44
  3.6 5.8 %shard_map.127 = (f32[64,256]{1,0:T(8,128)}, f32[64,256]{1,0:T(8,128)}, f32[136,128]{1,0:T(8,128)}, f32[136,128]{1,0:T(8,128)}) custom-call(f32[32,64,128]{2,1,0:T(8,128)} %u_ref.3, f32[32,64,128]{2,1,0:T(8,128)} %v_ref.3, f32[32,64,128]{2,1,0:T(8,128)} %t_ref.3, f32[32,64,128]{2,1,0:T(8,128)} %s_ref.3, f32[64,128]{1,0:T(8,128)} %convert_element_type.13.m_ref, ...), custom_call_target="tpu_custom_call" | custom-call | tf_op jit(solution)/shard_map/pallas_call | solution.py:174
  9.4 3.9 %collective-permute-start.4 = (f32[136,128]{1,0:T(8,128)}, f32[136,128]{1,0:T(8,128)S(1)}, u32[]{:S(2)}, u32[]{:S(2)}) collective-permute-start(f32[136,128]{1,0:T(8,128)} %get-tuple-element.18), channel_id=1, source_target_pairs={{0,1},{1,2},{2,3},{3,4},{4,5},{5,6},{6,7},{8,9},{9,10},{10,11},{11... | collective-permute-start | bytes 208904 | tf_op jit(solution)/shard_map/ppermute | solution.py:35
  13.3 0.7 collective-permute-start.2
  14.0 1.0 collective-permute-start
  15.0 1.6 %collective-permute-start.1 = (f32[64,256]{1,0:T(8,128)}, f32[64,256]{1,0:T(8,128)S(1)}, u32[]{:S(2)}, u32[]{:S(2)}) collective-permute-start(f32[64,256]{1,0:T(8,128)} %get-tuple-element.17), channel_id=1, source_target_pairs={{0,8},{8,16},{16,24},{24,32},{32,40},{40,48},{48,56},{56,64},{64,7... | collective-permute-start | bytes 196616 | tf_op jit(solution)/shard_map/ppermute | solution.py:33
  16.6 1.5 collective-permute-start.3
  18.2 0.5 collective-permute-done.he_ref
  18.7 3.1 %collective-permute-done.1.hw_ref = f32[64,256]{1,0:T(8,128)S(1)} collective-permute-done((f32[64,256]{1,0:T(8,128)}, f32[64,256]{1,0:T(8,128)S(1)}, u32[]{:S(2)}, u32[]{:S(2)}) %collective-permute-start.1) | collective-permute-done | bytes 65568 | tf_op jit(solution)/shard_map/ppermute | solution.py:33
  21.8 0.2 rev.15
  22.0 0.4 copy-done.4
  22.4 0.7 multiply_select_fusion.hn_ref
  23.1 0.7 broadcast_in_dim.75.f_ref
  23.8 15.2 %shard_map.128 = (f32[32,64,128]{2,1,0:T(8,128)}, f32[32,64,128]{2,1,0:T(8,128)}, f32[32,64,128]{2,1,0:T(8,128)}, f32[32,64,128]{2,1,0:T(8,128)}, f32[64,128]{1,0:T(8,128)}, /*index=5*/f32[64,128]{1,0:T(8,128)}) custom-call(f32[32,64,128]{2,1,0:T(8,128)} %u_ref.3, f32[32,64,128]{2,1,0:T(8,128)} %v_ref.3, f32[32,64,128]{2,1,0:T(8,128)} %t_ref.3, ...), custom_call_target="tpu_custom_call" | custom-call | tf_op jit(solution)/shard_map/pallas_call | solution.py:185
  39.0 1.0 fusion.2
  40.1 1.3 collective-permute-start.8
  41.4 0.7 collective-permute-start.7
  42.1 6.6 %collective-permute-start.5 = (f32[2,64]{1,0:T(2,128)S(1)}, f32[2,64]{1,0:T(2,128)S(1)}, u32[]{:S(2)}, u32[]{:S(2)}) collective-permute-start(f32[2,64]{1,0:T(2,128)S(1)} %get-tuple-element.26), channel_id=1, source_target_pairs={{8,0},{16,8},{24,16},{32,24},{40,32},{48,40},{56,48},{64,56},{72,6... | collective-permute-start | bytes 1544 | tf_op jit(solution)/shard_map/ppermute | solution.py:32
  48.7 4.3 %collective-permute-start.9 = (f32[2,128]{1,0:T(2,128)S(1)}, f32[2,128]{1,0:T(2,128)S(1)}, u32[]{:S(2)}, u32[]{:S(2)}) collective-permute-start(f32[2,128]{1,0:T(2,128)S(1)} %bitcast.95), channel_id=1, source_target_pairs={{0,1},{1,2},{2,3},{3,4},{4,5},{5,6},{6,7},{8,9},{9,10},{10,11},{11... | collective-permute-start | bytes 3080 | tf_op jit(solution)/shard_map/ppermute | solution.py:35
  53.4 0.3 collective-permute-done.9
  53.9 0.4 slice-done
  54.5 0.2 slice_reduce_fusion.4
  54.7 3.6 %collective-permute-start.14 = (f32[128]{0:T(128)S(1)}, f32[128]{0:T(128)S(1)}, u32[]{:S(2)}, u32[]{:S(2)}) collective-permute-start(f32[128]{0:T(128)S(1)} %get-tuple-element.76), channel_id=1, source_target_pairs={{0,1},{1,2},{2,3},{3,4},{4,5},{5,6},{6,7},{8,9},{9,10},{10,11},{11... | collective-permute-start | bytes 1544 | tf_op jit(solution)/shard_map/ppermute | solution.py:35
  58.3 0.7 collective-permute-start.12
  59.0 5.2 %collective-permute-start.10 = (f32[64]{0:T(128)S(1)}, f32[64]{0:T(128)S(1)}, u32[]{:S(2)}, u32[]{:S(2)}) collective-permute-start(f32[64]{0:T(128)S(1)} %get-tuple-element.33), channel_id=1, source_target_pairs={{8,0},{16,8},{24,16},{32,24},{40,32},{48,40},{56,48},{64,56},{72,6... | collective-permute-start | bytes 776 | tf_op jit(solution)/shard_map/ppermute | solution.py:32
  64.2 1.3 collective-permute-start.13
  65.9 2.6 %collective-permute-done.13 = f32[128]{0:T(128)S(1)} collective-permute-done((f32[128]{0:T(128)S(1)}, f32[128]{0:T(128)S(1)}, u32[]{:S(2)}, u32[]{:S(2)}) %collective-permute-start.13) | collective-permute-done | bytes 544 | tf_op jit(solution)/shard_map/ppermute | solution.py:34
  68.7 0.2 slice_reduce_fusion.2
  68.9 4.2 %collective-permute-start.19 = (f32[128]{0:T(128)S(1)}, f32[128]{0:T(128)S(1)}, u32[]{:S(2)}, u32[]{:S(2)}) collective-permute-start(f32[128]{0:T(128)S(1)} %get-tuple-element.70), channel_id=1, source_target_pairs={{0,1},{1,2},{2,3},{3,4},{4,5},{5,6},{6,7},{8,9},{9,10},{10,11},{11... | collective-permute-start | bytes 1544 | tf_op jit(solution)/shard_map/ppermute | solution.py:35
  73.0 0.7 collective-permute-start.17
  73.7 0.3 collective-permute-start.16
  74.0 6.5 %collective-permute-start.15 = (f32[64]{0:T(128)S(1)}, f32[64]{0:T(128)S(1)}, u32[]{:S(2)}, u32[]{:S(2)}) collective-permute-start(f32[64]{0:T(128)S(1)} %get-tuple-element.31), channel_id=1, source_target_pairs={{8,0},{16,8},{24,16},{32,24},{40,32},{48,40},{56,48},{64,56},{72,6... | collective-permute-start | bytes 776 | tf_op jit(solution)/shard_map/ppermute | solution.py:32
  80.5 1.3 collective-permute-start.18
  82.2 4.7 %collective-permute-done.18 = f32[128]{0:T(128)S(1)} collective-permute-done((f32[128]{0:T(128)S(1)}, f32[128]{0:T(128)S(1)}, u32[]{:S(2)}, u32[]{:S(2)}) %collective-permute-start.18) | collective-permute-done | bytes 544 | tf_op jit(solution)/shard_map/ppermute | solution.py:34
  87.2 24.6 %all_to_all.12 = f32[128,1,6]{2,1,0:T(1,128)S(1)} all-to-all(f32[128,1,6]{2,1,0:T(1,128)S(1)} %broadcast_in_dim.92), channel_id=1, replica_groups=mesh['lon'=16,'lat'=8] {'lon','lat'}, dimensions={0} | all-to-all | bytes 6144 | tf_op jit(solution)/shard_map/all_to_all | solution.py:25
  112.0 0.7 fusion.54
  119.8 2.2 %collective-permute-start.24 = (f32[128]{0:T(128)S(1)}, f32[128]{0:T(128)S(1)}, u32[]{:S(2)}, u32[]{:S(2)}) collective-permute-start(f32[128]{0:T(128)S(1)} %get-tuple-element.64), channel_id=1, source_target_pairs={{0,1},{1,2},{2,3},{3,4},{4,5},{5,6},{6,7},{8,9},{9,10},{10,11},{11... | collective-permute-start | bytes 1544 | tf_op jit(solution)/shard_map/ppermute | solution.py:35
  122.0 0.7 collective-permute-start.22
  122.7 1.3 collective-permute-start.21
  124.0 1.3 collective-permute-start.23
  125.4 1.6 %collective-permute-done.20 = f32[64]{0:T(128)S(1)} collective-permute-done((f32[64]{0:T(128)S(1)}, f32[64]{0:T(128)S(1)}, u32[]{:S(2)}, u32[]{:S(2)}) %collective-permute-start.20) | collective-permute-done | bytes 288 | tf_op jit(solution)/shard_map/ppermute | solution.py:32
  127.3 1.0 collective-permute-done.23
  128.6 22.8 %all_to_all.13 = f32[128,1,5]{2,1,0:T(1,128)S(1)} all-to-all(f32[128,1,5]{2,1,0:T(1,128)S(1)} %broadcast_in_dim.97), channel_id=1, replica_groups=mesh['lon'=16,'lat'=8] {'lon','lat'}, dimensions={0} | all-to-all | bytes 5120 | tf_op jit(solution)/shard_map/all_to_all | solution.py:25
  151.6 0.7 fusion.53
  156.2 0.6 multiply_subtract_fusion
  (100 shorter events, 3.6 us)
Async XLA Ops:
  0.6 0.9 copy-start.5
  2.2 0.8 copy-start.7
  3.6 14.5 %copy-start = (f32[64,128]{1,0:T(8,128)S(1)}, f32[64,128]{1,0:T(8,128)}, u32[]{:S(2)}) copy-start(f32[64,128]{1,0:T(8,128)} %get-tuple-element.53.c_ref) | copy-start | bytes 98308
  9.4 13.7 %collective-permute-start.4 = (f32[136,128]{1,0:T(8,128)}, f32[136,128]{1,0:T(8,128)S(1)}, u32[]{:S(2)}, u32[]{:S(2)}) collective-permute-start(f32[136,128]{1,0:T(8,128)} %get-tuple-element.18), channel_id=1, source_target_pairs={{0,1},{1,2},{2,3},{3,4},{4,5},{5,6},{6,7},{8,9},{9,10},{10,11},{11... | collective-permute-start | bytes 208904 | tf_op jit(solution)/shard_map/ppermute | solution.py:35
  13.3 8.5 %collective-permute-start.2 = (f32[136,128]{1,0:T(8,128)}, f32[136,128]{1,0:T(8,128)S(1)}, u32[]{:S(2)}, u32[]{:S(2)}) collective-permute-start(f32[136,128]{1,0:T(8,128)} %get-tuple-element.18), channel_id=1, source_target_pairs={{7,127},{15,119},{23,111},{31,103},{39,95},{47,87},{55,79},{63,71}... | collective-permute-start | bytes 208904 | tf_op jit(solution)/shard_map/ppermute | solution.py:37
  14.0 4.7 %collective-permute-start = (f32[64,256]{1,0:T(8,128)}, f32[64,256]{1,0:T(8,128)S(1)}, u32[]{:S(2)}, u32[]{:S(2)}) collective-permute-start(f32[64,256]{1,0:T(8,128)} %get-tuple-element.16), channel_id=1, source_target_pairs={{8,0},{16,8},{24,16},{32,24},{40,32},{48,40},{56,48},{64,56},{72,6... | collective-permute-start | bytes 196616 | tf_op jit(solution)/shard_map/ppermute | solution.py:32
  15.0 6.8 %collective-permute-start.1 = (f32[64,256]{1,0:T(8,128)}, f32[64,256]{1,0:T(8,128)S(1)}, u32[]{:S(2)}, u32[]{:S(2)}) collective-permute-start(f32[64,256]{1,0:T(8,128)} %get-tuple-element.17), channel_id=1, source_target_pairs={{0,8},{8,16},{16,24},{24,32},{32,40},{40,48},{48,56},{56,64},{64,7... | collective-permute-start | bytes 196616 | tf_op jit(solution)/shard_map/ppermute | solution.py:33
  16.6 5.8 %collective-permute-start.3 = (f32[136,128]{1,0:T(8,128)}, f32[136,128]{1,0:T(8,128)S(1)}, u32[]{:S(2)}, u32[]{:S(2)}) collective-permute-start(f32[136,128]{1,0:T(8,128)} %get-tuple-element.19), channel_id=1, source_target_pairs={{1,0},{2,1},{3,2},{4,3},{5,4},{6,5},{7,6},{9,8},{10,9},{11,10},{12... | collective-permute-start | bytes 208904 | tf_op jit(solution)/shard_map/ppermute | solution.py:34
  18.7 3.1 %copy-start.3 = (f32[64,256]{1,0:T(8,128)}, f32[64,256]{1,0:T(8,128)S(1)}, u32[]{:S(2)}) copy-start(f32[64,256]{1,0:T(8,128)S(1)} %collective-permute-done.he_ref) | copy-start | bytes 196612
  21.8 0.6 copy-start.4
  23.1 0.7 copy-start.6
  39.0 1.0 copy-start.1
  39.0 1.0 copy-start.2
  40.1 13.3 %collective-permute-start.8 = (f32[2,128]{1,0:T(2,128)S(1)}, f32[2,128]{1,0:T(2,128)S(1)}, u32[]{:S(2)}, u32[]{:S(2)}) collective-permute-start(f32[2,128]{1,0:T(2,128)S(1)} %bitcast.96), channel_id=1, source_target_pairs={{1,0},{2,1},{3,2},{4,3},{5,4},{6,5},{7,6},{9,8},{10,9},{11,10},{12... | collective-permute-start | bytes 3080 | tf_op jit(solution)/shard_map/ppermute | solution.py:34
  41.4 11.9 %collective-permute-start.7 = (f32[2,128]{1,0:T(2,128)S(1)}, f32[2,128]{1,0:T(2,128)S(1)}, u32[]{:S(2)}, u32[]{:S(2)}) collective-permute-start(f32[2,128]{1,0:T(2,128)S(1)} %bitcast.94), channel_id=1, source_target_pairs={{7,127},{15,119},{23,111},{31,103},{39,95},{47,87},{55,79},{63,71}... | collective-permute-start | bytes 3080 | tf_op jit(solution)/shard_map/ppermute | solution.py:37
  42.1 11.0 %collective-permute-start.5 = (f32[2,64]{1,0:T(2,128)S(1)}, f32[2,64]{1,0:T(2,128)S(1)}, u32[]{:S(2)}, u32[]{:S(2)}) collective-permute-start(f32[2,64]{1,0:T(2,128)S(1)} %get-tuple-element.26), channel_id=1, source_target_pairs={{8,0},{16,8},{24,16},{32,24},{40,32},{48,40},{56,48},{64,56},{72,6... | collective-permute-start | bytes 1544 | tf_op jit(solution)/shard_map/ppermute | solution.py:32
  48.7 4.3 %collective-permute-start.6 = (f32[2,64]{1,0:T(2,128)S(1)}, f32[2,64]{1,0:T(2,128)S(1)}, u32[]{:S(2)}, u32[]{:S(2)}) collective-permute-start(f32[2,64]{1,0:T(2,128)S(1)} %get-tuple-element.27), channel_id=1, source_target_pairs={{0,8},{8,16},{16,24},{24,32},{32,40},{40,48},{48,56},{56,64},{64,7... | collective-permute-start | bytes 1544 | tf_op jit(solution)/shard_map/ppermute | solution.py:33
  48.7 5.0 %collective-permute-start.9 = (f32[2,128]{1,0:T(2,128)S(1)}, f32[2,128]{1,0:T(2,128)S(1)}, u32[]{:S(2)}, u32[]{:S(2)}) collective-permute-start(f32[2,128]{1,0:T(2,128)S(1)} %bitcast.95), channel_id=1, source_target_pairs={{0,1},{1,2},{2,3},{3,4},{4,5},{5,6},{6,7},{8,9},{9,10},{10,11},{11... | collective-permute-start | bytes 3080 | tf_op jit(solution)/shard_map/ppermute | solution.py:35
  53.0 0.8 copy-start.8
  53.2 0.8 slice-start.1
  53.2 0.8 slice-start.2
  53.7 0.6 slice-start
  53.7 0.6 slice-start.3
  54.7 13.9 %collective-permute-start.14 = (f32[128]{0:T(128)S(1)}, f32[128]{0:T(128)S(1)}, u32[]{:S(2)}, u32[]{:S(2)}) collective-permute-start(f32[128]{0:T(128)S(1)} %get-tuple-element.76), channel_id=1, source_target_pairs={{0,1},{1,2},{2,3},{3,4},{4,5},{5,6},{6,7},{8,9},{9,10},{10,11},{11... | collective-permute-start | bytes 1544 | tf_op jit(solution)/shard_map/ppermute | solution.py:35
  58.3 7.5 %collective-permute-start.12 = (f32[128]{0:T(128)S(1)}, f32[128]{0:T(128)S(1)}, u32[]{:S(2)}, u32[]{:S(2)}) collective-permute-start(f32[128]{0:T(128)S(1)} %get-tuple-element.76), channel_id=1, source_target_pairs={{7,127},{15,119},{23,111},{31,103},{39,95},{47,87},{55,79},{63,71}... | collective-permute-start | bytes 1544 | tf_op jit(solution)/shard_map/ppermute | solution.py:37
  58.9 6.8 %collective-permute-start.11 = (f32[64]{0:T(128)S(1)}, f32[64]{0:T(128)S(1)}, u32[]{:S(2)}, u32[]{:S(2)}) collective-permute-start(f32[64]{0:T(128)S(1)} %get-tuple-element.32), channel_id=1, source_target_pairs={{0,8},{8,16},{16,24},{24,32},{32,40},{40,48},{48,56},{56,64},{64,7... | collective-permute-start | bytes 776 | tf_op jit(solution)/shard_map/ppermute | solution.py:33
  59.0 6.6 %collective-permute-start.10 = (f32[64]{0:T(128)S(1)}, f32[64]{0:T(128)S(1)}, u32[]{:S(2)}, u32[]{:S(2)}) collective-permute-start(f32[64]{0:T(128)S(1)} %get-tuple-element.33), channel_id=1, source_target_pairs={{8,0},{16,8},{24,16},{32,24},{40,32},{48,40},{56,48},{64,56},{72,6... | collective-permute-start | bytes 776 | tf_op jit(solution)/shard_map/ppermute | solution.py:32
  64.2 4.3 %collective-permute-start.13 = (f32[128]{0:T(128)S(1)}, f32[128]{0:T(128)S(1)}, u32[]{:S(2)}, u32[]{:S(2)}) collective-permute-start(f32[128]{0:T(128)S(1)} %get-tuple-element.75), channel_id=1, source_target_pairs={{1,0},{2,1},{3,2},{4,3},{5,4},{6,5},{7,6},{9,8},{10,9},{11,10},{12... | collective-permute-start | bytes 1544 | tf_op jit(solution)/shard_map/ppermute | solution.py:34
  68.9 18.1 %collective-permute-start.19 = (f32[128]{0:T(128)S(1)}, f32[128]{0:T(128)S(1)}, u32[]{:S(2)}, u32[]{:S(2)}) collective-permute-start(f32[128]{0:T(128)S(1)} %get-tuple-element.70), channel_id=1, source_target_pairs={{0,1},{1,2},{2,3},{3,4},{4,5},{5,6},{6,7},{8,9},{9,10},{10,11},{11... | collective-permute-start | bytes 1544 | tf_op jit(solution)/shard_map/ppermute | solution.py:35
  73.0 9.1 %collective-permute-start.17 = (f32[128]{0:T(128)S(1)}, f32[128]{0:T(128)S(1)}, u32[]{:S(2)}, u32[]{:S(2)}) collective-permute-start(f32[128]{0:T(128)S(1)} %get-tuple-element.70), channel_id=1, source_target_pairs={{7,127},{15,119},{23,111},{31,103},{39,95},{47,87},{55,79},{63,71}... | collective-permute-start | bytes 1544 | tf_op jit(solution)/shard_map/ppermute | solution.py:37
  73.7 8.3 %collective-permute-start.16 = (f32[64]{0:T(128)S(1)}, f32[64]{0:T(128)S(1)}, u32[]{:S(2)}, u32[]{:S(2)}) collective-permute-start(f32[64]{0:T(128)S(1)} %get-tuple-element.30), channel_id=1, source_target_pairs={{0,8},{8,16},{16,24},{24,32},{32,40},{40,48},{48,56},{56,64},{64,7... | collective-permute-start | bytes 776 | tf_op jit(solution)/shard_map/ppermute | solution.py:33
  74.0 7.9 %collective-permute-start.15 = (f32[64]{0:T(128)S(1)}, f32[64]{0:T(128)S(1)}, u32[]{:S(2)}, u32[]{:S(2)}) collective-permute-start(f32[64]{0:T(128)S(1)} %get-tuple-element.31), channel_id=1, source_target_pairs={{8,0},{16,8},{24,16},{32,24},{40,32},{48,40},{56,48},{64,56},{72,6... | collective-permute-start | bytes 776 | tf_op jit(solution)/shard_map/ppermute | solution.py:32
  80.5 6.4 %collective-permute-start.18 = (f32[128]{0:T(128)S(1)}, f32[128]{0:T(128)S(1)}, u32[]{:S(2)}, u32[]{:S(2)}) collective-permute-start(f32[128]{0:T(128)S(1)} %get-tuple-element.69), channel_id=1, source_target_pairs={{1,0},{2,1},{3,2},{4,3},{5,4},{6,5},{7,6},{9,8},{10,9},{11,10},{12... | collective-permute-start | bytes 1544 | tf_op jit(solution)/shard_map/ppermute | solution.py:34
  119.8 8.5 %collective-permute-start.24 = (f32[128]{0:T(128)S(1)}, f32[128]{0:T(128)S(1)}, u32[]{:S(2)}, u32[]{:S(2)}) collective-permute-start(f32[128]{0:T(128)S(1)} %get-tuple-element.64), channel_id=1, source_target_pairs={{0,1},{1,2},{2,3},{3,4},{4,5},{5,6},{6,7},{8,9},{9,10},{10,11},{11... | collective-permute-start | bytes 1544 | tf_op jit(solution)/shard_map/ppermute | solution.py:35
  122.0 5.2 %collective-permute-start.22 = (f32[128]{0:T(128)S(1)}, f32[128]{0:T(128)S(1)}, u32[]{:S(2)}, u32[]{:S(2)}) collective-permute-start(f32[128]{0:T(128)S(1)} %get-tuple-element.64), channel_id=1, source_target_pairs={{7,127},{15,119},{23,111},{31,103},{39,95},{47,87},{55,79},{63,71}... | collective-permute-start | bytes 1544 | tf_op jit(solution)/shard_map/ppermute | solution.py:37
  122.7 4.4 %collective-permute-start.21 = (f32[64]{0:T(128)S(1)}, f32[64]{0:T(128)S(1)}, u32[]{:S(2)}, u32[]{:S(2)}) collective-permute-start(f32[64]{0:T(128)S(1)} %get-tuple-element.28), channel_id=1, source_target_pairs={{0,8},{8,16},{16,24},{24,32},{32,40},{40,48},{48,56},{56,64},{64,7... | collective-permute-start | bytes 776 | tf_op jit(solution)/shard_map/ppermute | solution.py:33
  124.0 3.0 %collective-permute-start.20 = (f32[64]{0:T(128)S(1)}, f32[64]{0:T(128)S(1)}, u32[]{:S(2)}, u32[]{:S(2)}) collective-permute-start(f32[64]{0:T(128)S(1)} %get-tuple-element.29), channel_id=1, source_target_pairs={{8,0},{16,8},{24,16},{32,24},{40,32},{48,40},{56,48},{64,56},{72,6... | collective-permute-start | bytes 776 | tf_op jit(solution)/shard_map/ppermute | solution.py:32
  124.0 4.3 %collective-permute-start.23 = (f32[128]{0:T(128)S(1)}, f32[128]{0:T(128)S(1)}, u32[]{:S(2)}, u32[]{:S(2)}) collective-permute-start(f32[128]{0:T(128)S(1)} %get-tuple-element.63), channel_id=1, source_target_pairs={{1,0},{2,1},{3,2},{4,3},{5,4},{6,5},{7,6},{9,8},{10,9},{11,10},{12... | collective-permute-start | bytes 1544 | tf_op jit(solution)/shard_map/ppermute | solution.py:34

commit v8 on v7

--- a/solution.py
+++ b/solution.py
@@ -145,9 +145,10 @@
 def edge_kernel(u_ref, v_ref, t_ref, s_ref, m_ref, c_ref, cf_ref, cl_ref, rf_ref, rl_ref):
     levels, height, breadth = u_ref.shape
     marine = m_ref[...]
-    lane = lax.broadcasted_iota(jnp.int32, cf_ref.shape, 1)
-    first = jnp.zeros(cf_ref.shape, jnp.float32)
-    last = jnp.zeros(cf_ref.shape, jnp.float32)
+    groups = cf_ref.shape[1] // 128
+    lane = lax.broadcasted_iota(jnp.int32, (height, 128), 1)
+    first = [jnp.zeros((height, 128), jnp.float32) for _ in range(groups)]
+    last = [jnp.zeros((height, 128), jnp.float32) for _ in range(groups)]
     rf_ref[...] = jnp.zeros(rf_ref.shape, jnp.float32)
     rl_ref[...] = jnp.zeros(rl_ref.shape, jnp.float32)
     planes = [(field, level) for field in (u_ref, v_ref, t_ref, s_ref) for level in range(levels)]
@@ -156,12 +157,14 @@
             masked = field[...]
         else:
             masked = field[level] * marine
-        first = jnp.where(lane == index, masked[:, 0:1], first)
-        last = jnp.where(lane == index, masked[:, breadth - 1 : breadth], last)
+        group, offset = divmod(index, 128)
+        first[group] = jnp.where(lane == offset, masked[:, 0:1], first[group])
+        last[group] = jnp.where(lane == offset, masked[:, breadth - 1 : breadth], last[group])
         rf_ref[index : index + 1, :] = masked[0:1, :]
         rl_ref[index : index + 1, :] = masked[height - 1 : height, :]
-    cf_ref[...] = first
-    cl_ref[...] = last
+    for group in range(groups):
+        cf_ref[:, group * 128 : (group + 1) * 128] = first[group]
+        cl_ref[:, group * 128 : (group + 1) * 128] = last[group]
 
 
 def edge_step(u, v, t, s, marine, column):

time: 158 us -> 158 us (level)
  no operation moved by 1% of the time
where the time goes in v8:
time: 158 us; the launch traced here: 157 us
  starting transfers between devices  50.7 us (32%)
  blocking collectives  47.4 us (30%)
  Pallas kernels  21 us (13%)
  waiting for transfers between devices  14 us (9%)
  between operations  12 us (8%)
  local copies, waits for them, and re-layouts  6.38 us (4%)
  other arithmetic  5.48 us (3%)
    all_to_all x2, blocking collectives, allsum(): gathered = lax.all_to_all(spread, ('lon', 'lat'), 0, 0, tiled=True)  47.4 us
    ppermute x5, starting transfers between devices, exchange(): lax.ppermute(first_col, 'lon', [((i + 1) % lon_count, i) for i in range(l...  19.4 us
    ppermute x5, starting transfers between devices, exchange(): lax.ppermute(last_row, 'lat', [(i, i + 1) for i in range(lat_count - 1)])  18.1 us
    pallas_call x1, Pallas kernels, column_step(): pl.pallas_call(column_kernel, out_shape=(field, field, field, field, plan...  15.2 us
    ppermute x5, waiting for transfers between devices, exchange(): lax.ppermute(first_row, 'lat', [(i + 1, i) for i in range(lat_count - 1)])  8.4 us
    ppermute x5, starting transfers between devices, exchange(): lax.ppermute(first_row, 'lat', [(i + 1, i) for i in range(lat_count - 1)])  6.59 us
    pallas_call x1, Pallas kernels, edge_step(): pl.pallas_call(edge_kernel, out_shape=(cols, cols, flat, flat), interpret...  5.77 us
    ppermute x5, starting transfers between devices, exchange(): lax.ppermute(last_row, ('lon', 'lat'), [(i * lat_count + top, (lon_count...  3.31 us
  transfers between devices with their start and end apart: 25, of which 7 were waited for; matrix products, arithmetic and copies ran while one was open for 2% of the time, Pallas kernels for 0%

profile of v8, /device:TPU:1, one launch (start us, length us, event | category | flops | bytes accessed | tf_op | source)
XLA Modules:
  0.0 156.8 jit_solution(5573485409435977935)
XLA Ops:
  0.6 0.7 convert_element_type.15
  1.6 0.6 convert_element_type.13.m_ref
  2.3 0.7 copy-done.7
  3.0 0.6 fusion.44
  3.6 5.8 %shard_map.127 = (f32[64,256]{1,0:T(8,128)}, f32[64,256]{1,0:T(8,128)}, f32[136,128]{1,0:T(8,128)}, f32[136,128]{1,0:T(8,128)}) custom-call(f32[32,64,128]{2,1,0:T(8,128)} %u_ref.3, f32[32,64,128]{2,1,0:T(8,128)} %v_ref.3, f32[32,64,128]{2,1,0:T(8,128)} %t_ref.3, f32[32,64,128]{2,1,0:T(8,128)} %s_ref.3, f32[64,128]{1,0:T(8,128)} %convert_element_type.13.m_ref, ...), custom_call_target="tpu_custom_call" | custom-call | tf_op jit(solution)/shard_map/pallas_call | solution.py:177
  9.4 3.9 %collective-permute-start.4 = (f32[136,128]{1,0:T(8,128)}, f32[136,128]{1,0:T(8,128)S(1)}, u32[]{:S(2)}, u32[]{:S(2)}) collective-permute-start(f32[136,128]{1,0:T(8,128)} %get-tuple-element.18), channel_id=1, source_target_pairs={{0,1},{1,2},{2,3},{3,4},{4,5},{5,6},{6,7},{8,9},{9,10},{10,11},{11... | collective-permute-start | bytes 208904 | tf_op jit(solution)/shard_map/ppermute | solution.py:35
  13.3 0.7 collective-permute-start.2
  14.0 1.0 collective-permute-start
  15.0 1.6 %collective-permute-start.1 = (f32[64,256]{1,0:T(8,128)}, f32[64,256]{1,0:T(8,128)S(1)}, u32[]{:S(2)}, u32[]{:S(2)}) collective-permute-start(f32[64,256]{1,0:T(8,128)} %get-tuple-element.17), channel_id=1, source_target_pairs={{0,8},{8,16},{16,24},{24,32},{32,40},{40,48},{48,56},{56,64},{64,7... | collective-permute-start | bytes 196616 | tf_op jit(solution)/shard_map/ppermute | solution.py:33
  16.6 1.5 collective-permute-start.3
  18.2 0.5 collective-permute-done.he_ref
  18.7 3.1 %collective-permute-done.1.hw_ref = f32[64,256]{1,0:T(8,128)S(1)} collective-permute-done((f32[64,256]{1,0:T(8,128)}, f32[64,256]{1,0:T(8,128)S(1)}, u32[]{:S(2)}, u32[]{:S(2)}) %collective-permute-start.1) | collective-permute-done | bytes 65568 | tf_op jit(solution)/shard_map/ppermute | solution.py:33
  21.8 0.2 rev.15
  22.0 0.4 copy-done.4
  22.4 0.7 multiply_select_fusion.hn_ref
  23.1 0.7 broadcast_in_dim.75.f_ref
  23.8 15.2 %shard_map.128 = (f32[32,64,128]{2,1,0:T(8,128)}, f32[32,64,128]{2,1,0:T(8,128)}, f32[32,64,128]{2,1,0:T(8,128)}, f32[32,64,128]{2,1,0:T(8,128)}, f32[64,128]{1,0:T(8,128)}, /*index=5*/f32[64,128]{1,0:T(8,128)}) custom-call(f32[32,64,128]{2,1,0:T(8,128)} %u_ref.3, f32[32,64,128]{2,1,0:T(8,128)} %v_ref.3, f32[32,64,128]{2,1,0:T(8,128)} %t_ref.3, ...), custom_call_target="tpu_custom_call" | custom-call | tf_op jit(solution)/shard_map/pallas_call | solution.py:188
  39.0 1.0 fusion.2
  40.1 1.3 collective-permute-start.8
  41.4 0.7 collective-permute-start.7
  42.1 6.6 %collective-permute-start.5 = (f32[2,64]{1,0:T(2,128)S(1)}, f32[2,64]{1,0:T(2,128)S(1)}, u32[]{:S(2)}, u32[]{:S(2)}) collective-permute-start(f32[2,64]{1,0:T(2,128)S(1)} %get-tuple-element.26), channel_id=1, source_target_pairs={{8,0},{16,8},{24,16},{32,24},{40,32},{48,40},{56,48},{64,56},{72,6... | collective-permute-start | bytes 1544 | tf_op jit(solution)/shard_map/ppermute | solution.py:32
  48.7 4.3 %collective-permute-start.9 = (f32[2,128]{1,0:T(2,128)S(1)}, f32[2,128]{1,0:T(2,128)S(1)}, u32[]{:S(2)}, u32[]{:S(2)}) collective-permute-start(f32[2,128]{1,0:T(2,128)S(1)} %bitcast.95), channel_id=1, source_target_pairs={{0,1},{1,2},{2,3},{3,4},{4,5},{5,6},{6,7},{8,9},{9,10},{10,11},{11... | collective-permute-start | bytes 3080 | tf_op jit(solution)/shard_map/ppermute | solution.py:35
  53.4 0.3 collective-permute-done.9
  53.9 0.4 slice-done
  54.7 3.6 %collective-permute-start.14 = (f32[128]{0:T(128)S(1)}, f32[128]{0:T(128)S(1)}, u32[]{:S(2)}, u32[]{:S(2)}) collective-permute-start(f32[128]{0:T(128)S(1)} %get-tuple-element.76), channel_id=1, source_target_pairs={{0,1},{1,2},{2,3},{3,4},{4,5},{5,6},{6,7},{8,9},{9,10},{10,11},{11... | collective-permute-start | bytes 1544 | tf_op jit(solution)/shard_map/ppermute | solution.py:35
  58.3 0.7 collective-permute-start.12
  59.0 5.2 %collective-permute-start.10 = (f32[64]{0:T(128)S(1)}, f32[64]{0:T(128)S(1)}, u32[]{:S(2)}, u32[]{:S(2)}) collective-permute-start(f32[64]{0:T(128)S(1)} %get-tuple-element.33), channel_id=1, source_target_pairs={{8,0},{16,8},{24,16},{32,24},{40,32},{48,40},{56,48},{64,56},{72,6... | collective-permute-start | bytes 776 | tf_op jit(solution)/shard_map/ppermute | solution.py:32
  64.2 1.3 collective-permute-start.13
  65.9 2.6 %collective-permute-done.13 = f32[128]{0:T(128)S(1)} collective-permute-done((f32[128]{0:T(128)S(1)}, f32[128]{0:T(128)S(1)}, u32[]{:S(2)}, u32[]{:S(2)}) %collective-permute-start.13) | collective-permute-done | bytes 544 | tf_op jit(solution)/shard_map/ppermute | solution.py:34
  68.7 0.2 slice_reduce_fusion.2
  68.9 4.2 %collective-permute-start.19 = (f32[128]{0:T(128)S(1)}, f32[128]{0:T(128)S(1)}, u32[]{:S(2)}, u32[]{:S(2)}) collective-permute-start(f32[128]{0:T(128)S(1)} %get-tuple-element.70), channel_id=1, source_target_pairs={{0,1},{1,2},{2,3},{3,4},{4,5},{5,6},{6,7},{8,9},{9,10},{10,11},{11... | collective-permute-start | bytes 1544 | tf_op jit(solution)/shard_map/ppermute | solution.py:35
  73.0 0.7 collective-permute-start.17
  73.7 0.3 collective-permute-start.16
  74.0 6.5 %collective-permute-start.15 = (f32[64]{0:T(128)S(1)}, f32[64]{0:T(128)S(1)}, u32[]{:S(2)}, u32[]{:S(2)}) collective-permute-start(f32[64]{0:T(128)S(1)} %get-tuple-element.31), channel_id=1, source_target_pairs={{8,0},{16,8},{24,16},{32,24},{40,32},{48,40},{56,48},{64,56},{72,6... | collective-permute-start | bytes 776 | tf_op jit(solution)/shard_map/ppermute | solution.py:32
  80.5 1.3 collective-permute-start.18
  82.2 4.7 %collective-permute-done.18 = f32[128]{0:T(128)S(1)} collective-permute-done((f32[128]{0:T(128)S(1)}, f32[128]{0:T(128)S(1)}, u32[]{:S(2)}, u32[]{:S(2)}) %collective-permute-start.18) | collective-permute-done | bytes 544 | tf_op jit(solution)/shard_map/ppermute | solution.py:34
  87.2 24.6 %all_to_all.12 = f32[128,1,6]{2,1,0:T(1,128)S(1)} all-to-all(f32[128,1,6]{2,1,0:T(1,128)S(1)} %broadcast_in_dim.92), channel_id=1, replica_groups=mesh['lon'=16,'lat'=8] {'lon','lat'}, dimensions={0} | all-to-all | bytes 6144 | tf_op jit(solution)/shard_map/all_to_all | solution.py:25
  112.0 0.7 fusion.54
  119.6 0.2 slice_reduce_fusion
  119.8 2.2 %collective-permute-start.24 = (f32[128]{0:T(128)S(1)}, f32[128]{0:T(128)S(1)}, u32[]{:S(2)}, u32[]{:S(2)}) collective-permute-start(f32[128]{0:T(128)S(1)} %get-tuple-element.64), channel_id=1, source_target_pairs={{0,1},{1,2},{2,3},{3,4},{4,5},{5,6},{6,7},{8,9},{9,10},{10,11},{11... | collective-permute-start | bytes 1544 | tf_op jit(solution)/shard_map/ppermute | solution.py:35
  122.0 0.7 collective-permute-start.22
  122.7 1.3 collective-permute-start.21
  124.0 1.3 collective-permute-start.23
  125.4 1.6 %collective-permute-done.20 = f32[64]{0:T(128)S(1)} collective-permute-done((f32[64]{0:T(128)S(1)}, f32[64]{0:T(128)S(1)}, u32[]{:S(2)}, u32[]{:S(2)}) %collective-permute-start.20) | collective-permute-done | bytes 288 | tf_op jit(solution)/shard_map/ppermute | solution.py:32
  127.3 1.0 collective-permute-done.23
  128.6 22.8 %all_to_all.13 = f32[128,1,5]{2,1,0:T(1,128)S(1)} all-to-all(f32[128,1,5]{2,1,0:T(1,128)S(1)} %broadcast_in_dim.97), channel_id=1, replica_groups=mesh['lon'=16,'lat'=8] {'lon','lat'}, dimensions={0} | all-to-all | bytes 5120 | tf_op jit(solution)/shard_map/all_to_all | solution.py:25
  151.6 0.7 fusion.53
  156.2 0.6 multiply_subtract_fusion
  (100 shorter events, 3.6 us)
Async XLA Ops:
  0.6 0.9 copy-start.5
  2.2 0.8 copy-start.7
  3.6 14.5 %copy-start = (f32[64,128]{1,0:T(8,128)S(1)}, f32[64,128]{1,0:T(8,128)}, u32[]{:S(2)}) copy-start(f32[64,128]{1,0:T(8,128)} %get-tuple-element.53.c_ref) | copy-start | bytes 98308
  9.4 13.7 %collective-permute-start.4 = (f32[136,128]{1,0:T(8,128)}, f32[136,128]{1,0:T(8,128)S(1)}, u32[]{:S(2)}, u32[]{:S(2)}) collective-permute-start(f32[136,128]{1,0:T(8,128)} %get-tuple-element.18), channel_id=1, source_target_pairs={{0,1},{1,2},{2,3},{3,4},{4,5},{5,6},{6,7},{8,9},{9,10},{10,11},{11... | collective-permute-start | bytes 208904 | tf_op jit(solution)/shard_map/ppermute | solution.py:35
  13.3 8.5 %collective-permute-start.2 = (f32[136,128]{1,0:T(8,128)}, f32[136,128]{1,0:T(8,128)S(1)}, u32[]{:S(2)}, u32[]{:S(2)}) collective-permute-start(f32[136,128]{1,0:T(8,128)} %get-tuple-element.18), channel_id=1, source_target_pairs={{7,127},{15,119},{23,111},{31,103},{39,95},{47,87},{55,79},{63,71}... | collective-permute-start | bytes 208904 | tf_op jit(solution)/shard_map/ppermute | solution.py:37
  14.0 4.7 %collective-permute-start = (f32[64,256]{1,0:T(8,128)}, f32[64,256]{1,0:T(8,128)S(1)}, u32[]{:S(2)}, u32[]{:S(2)}) collective-permute-start(f32[64,256]{1,0:T(8,128)} %get-tuple-element.16), channel_id=1, source_target_pairs={{8,0},{16,8},{24,16},{32,24},{40,32},{48,40},{56,48},{64,56},{72,6... | collective-permute-start | bytes 196616 | tf_op jit(solution)/shard_map/ppermute | solution.py:32
  15.0 6.8 %collective-permute-start.1 = (f32[64,256]{1,0:T(8,128)}, f32[64,256]{1,0:T(8,128)S(1)}, u32[]{:S(2)}, u32[]{:S(2)}) collective-permute-start(f32[64,256]{1,0:T(8,128)} %get-tuple-element.17), channel_id=1, source_target_pairs={{0,8},{8,16},{16,24},{24,32},{32,40},{40,48},{48,56},{56,64},{64,7... | collective-permute-start | bytes 196616 | tf_op jit(solution)/shard_map/ppermute | solution.py:33
  16.6 5.8 %collective-permute-start.3 = (f32[136,128]{1,0:T(8,128)}, f32[136,128]{1,0:T(8,128)S(1)}, u32[]{:S(2)}, u32[]{:S(2)}) collective-permute-start(f32[136,128]{1,0:T(8,128)} %get-tuple-element.19), channel_id=1, source_target_pairs={{1,0},{2,1},{3,2},{4,3},{5,4},{6,5},{7,6},{9,8},{10,9},{11,10},{12... | collective-permute-start | bytes 208904 | tf_op jit(solution)/shard_map/ppermute | solution.py:34
  18.7 3.1 %copy-start.3 = (f32[64,256]{1,0:T(8,128)}, f32[64,256]{1,0:T(8,128)S(1)}, u32[]{:S(2)}) copy-start(f32[64,256]{1,0:T(8,128)S(1)} %collective-permute-done.he_ref) | copy-start | bytes 196612
  21.8 0.6 copy-start.4
  23.1 0.7 copy-start.6
  39.0 1.0 copy-start.1
  39.0 1.0 copy-start.2
  40.1 13.3 %collective-permute-start.8 = (f32[2,128]{1,0:T(2,128)S(1)}, f32[2,128]{1,0:T(2,128)S(1)}, u32[]{:S(2)}, u32[]{:S(2)}) collective-permute-start(f32[2,128]{1,0:T(2,128)S(1)} %bitcast.96), channel_id=1, source_target_pairs={{1,0},{2,1},{3,2},{4,3},{5,4},{6,5},{7,6},{9,8},{10,9},{11,10},{12... | collective-permute-start | bytes 3080 | tf_op jit(solution)/shard_map/ppermute | solution.py:34
  41.4 11.9 %collective-permute-start.7 = (f32[2,128]{1,0:T(2,128)S(1)}, f32[2,128]{1,0:T(2,128)S(1)}, u32[]{:S(2)}, u32[]{:S(2)}) collective-permute-start(f32[2,128]{1,0:T(2,128)S(1)} %bitcast.94), channel_id=1, source_target_pairs={{7,127},{15,119},{23,111},{31,103},{39,95},{47,87},{55,79},{63,71}... | collective-permute-start | bytes 3080 | tf_op jit(solution)/shard_map/ppermute | solution.py:37
  42.1 11.0 %collective-permute-start.5 = (f32[2,64]{1,0:T(2,128)S(1)}, f32[2,64]{1,0:T(2,128)S(1)}, u32[]{:S(2)}, u32[]{:S(2)}) collective-permute-start(f32[2,64]{1,0:T(2,128)S(1)} %get-tuple-element.26), channel_id=1, source_target_pairs={{8,0},{16,8},{24,16},{32,24},{40,32},{48,40},{56,48},{64,56},{72,6... | collective-permute-start | bytes 1544 | tf_op jit(solution)/shard_map/ppermute | solution.py:32
  48.7 4.3 %collective-permute-start.6 = (f32[2,64]{1,0:T(2,128)S(1)}, f32[2,64]{1,0:T(2,128)S(1)}, u32[]{:S(2)}, u32[]{:S(2)}) collective-permute-start(f32[2,64]{1,0:T(2,128)S(1)} %get-tuple-element.27), channel_id=1, source_target_pairs={{0,8},{8,16},{16,24},{24,32},{32,40},{40,48},{48,56},{56,64},{64,7... | collective-permute-start | bytes 1544 | tf_op jit(solution)/shard_map/ppermute | solution.py:33
  48.7 5.0 %collective-permute-start.9 = (f32[2,128]{1,0:T(2,128)S(1)}, f32[2,128]{1,0:T(2,128)S(1)}, u32[]{:S(2)}, u32[]{:S(2)}) collective-permute-start(f32[2,128]{1,0:T(2,128)S(1)} %bitcast.95), channel_id=1, source_target_pairs={{0,1},{1,2},{2,3},{3,4},{4,5},{5,6},{6,7},{8,9},{9,10},{10,11},{11... | collective-permute-start | bytes 3080 | tf_op jit(solution)/shard_map/ppermute | solution.py:35
  53.0 0.8 copy-start.8
  53.2 0.8 slice-start.1
  53.2 0.8 slice-start.2
  53.7 0.6 slice-start
  53.7 0.6 slice-start.3
  54.7 13.9 %collective-permute-start.14 = (f32[128]{0:T(128)S(1)}, f32[128]{0:T(128)S(1)}, u32[]{:S(2)}, u32[]{:S(2)}) collective-permute-start(f32[128]{0:T(128)S(1)} %get-tuple-element.76), channel_id=1, source_target_pairs={{0,1},{1,2},{2,3},{3,4},{4,5},{5,6},{6,7},{8,9},{9,10},{10,11},{11... | collective-permute-start | bytes 1544 | tf_op jit(solution)/shard_map/ppermute | solution.py:35
  58.3 7.5 %collective-permute-start.12 = (f32[128]{0:T(128)S(1)}, f32[128]{0:T(128)S(1)}, u32[]{:S(2)}, u32[]{:S(2)}) collective-permute-start(f32[128]{0:T(128)S(1)} %get-tuple-element.76), channel_id=1, source_target_pairs={{7,127},{15,119},{23,111},{31,103},{39,95},{47,87},{55,79},{63,71}... | collective-permute-start | bytes 1544 | tf_op jit(solution)/shard_map/ppermute | solution.py:37
  58.9 6.8 %collective-permute-start.11 = (f32[64]{0:T(128)S(1)}, f32[64]{0:T(128)S(1)}, u32[]{:S(2)}, u32[]{:S(2)}) collective-permute-start(f32[64]{0:T(128)S(1)} %get-tuple-element.32), channel_id=1, source_target_pairs={{0,8},{8,16},{16,24},{24,32},{32,40},{40,48},{48,56},{56,64},{64,7... | collective-permute-start | bytes 776 | tf_op jit(solution)/shard_map/ppermute | solution.py:33
  59.0 6.6 %collective-permute-start.10 = (f32[64]{0:T(128)S(1)}, f32[64]{0:T(128)S(1)}, u32[]{:S(2)}, u32[]{:S(2)}) collective-permute-start(f32[64]{0:T(128)S(1)} %get-tuple-element.33), channel_id=1, source_target_pairs={{8,0},{16,8},{24,16},{32,24},{40,32},{48,40},{56,48},{64,56},{72,6... | collective-permute-start | bytes 776 | tf_op jit(solution)/shard_map/ppermute | solution.py:32
  64.2 4.3 %collective-permute-start.13 = (f32[128]{0:T(128)S(1)}, f32[128]{0:T(128)S(1)}, u32[]{:S(2)}, u32[]{:S(2)}) collective-permute-start(f32[128]{0:T(128)S(1)} %get-tuple-element.75), channel_id=1, source_target_pairs={{1,0},{2,1},{3,2},{4,3},{5,4},{6,5},{7,6},{9,8},{10,9},{11,10},{12... | collective-permute-start | bytes 1544 | tf_op jit(solution)/shard_map/ppermute | solution.py:34
  68.9 18.1 %collective-permute-start.19 = (f32[128]{0:T(128)S(1)}, f32[128]{0:T(128)S(1)}, u32[]{:S(2)}, u32[]{:S(2)}) collective-permute-start(f32[128]{0:T(128)S(1)} %get-tuple-element.70), channel_id=1, source_target_pairs={{0,1},{1,2},{2,3},{3,4},{4,5},{5,6},{6,7},{8,9},{9,10},{10,11},{11... | collective-permute-start | bytes 1544 | tf_op jit(solution)/shard_map/ppermute | solution.py:35
  73.0 9.1 %collective-permute-start.17 = (f32[128]{0:T(128)S(1)}, f32[128]{0:T(128)S(1)}, u32[]{:S(2)}, u32[]{:S(2)}) collective-permute-start(f32[128]{0:T(128)S(1)} %get-tuple-element.70), channel_id=1, source_target_pairs={{7,127},{15,119},{23,111},{31,103},{39,95},{47,87},{55,79},{63,71}... | collective-permute-start | bytes 1544 | tf_op jit(solution)/shard_map/ppermute | solution.py:37
  73.7 8.3 %collective-permute-start.16 = (f32[64]{0:T(128)S(1)}, f32[64]{0:T(128)S(1)}, u32[]{:S(2)}, u32[]{:S(2)}) collective-permute-start(f32[64]{0:T(128)S(1)} %get-tuple-element.30), channel_id=1, source_target_pairs={{0,8},{8,16},{16,24},{24,32},{32,40},{40,48},{48,56},{56,64},{64,7... | collective-permute-start | bytes 776 | tf_op jit(solution)/shard_map/ppermute | solution.py:33
  74.0 7.9 %collective-permute-start.15 = (f32[64]{0:T(128)S(1)}, f32[64]{0:T(128)S(1)}, u32[]{:S(2)}, u32[]{:S(2)}) collective-permute-start(f32[64]{0:T(128)S(1)} %get-tuple-element.31), channel_id=1, source_target_pairs={{8,0},{16,8},{24,16},{32,24},{40,32},{48,40},{56,48},{64,56},{72,6... | collective-permute-start | bytes 776 | tf_op jit(solution)/shard_map/ppermute | solution.py:32
  80.5 6.4 %collective-permute-start.18 = (f32[128]{0:T(128)S(1)}, f32[128]{0:T(128)S(1)}, u32[]{:S(2)}, u32[]{:S(2)}) collective-permute-start(f32[128]{0:T(128)S(1)} %get-tuple-element.69), channel_id=1, source_target_pairs={{1,0},{2,1},{3,2},{4,3},{5,4},{6,5},{7,6},{9,8},{10,9},{11,10},{12... | collective-permute-start | bytes 1544 | tf_op jit(solution)/shard_map/ppermute | solution.py:34
  119.8 8.5 %collective-permute-start.24 = (f32[128]{0:T(128)S(1)}, f32[128]{0:T(128)S(1)}, u32[]{:S(2)}, u32[]{:S(2)}) collective-permute-start(f32[128]{0:T(128)S(1)} %get-tuple-element.64), channel_id=1, source_target_pairs={{0,1},{1,2},{2,3},{3,4},{4,5},{5,6},{6,7},{8,9},{9,10},{10,11},{11... | collective-permute-start | bytes 1544 | tf_op jit(solution)/shard_map/ppermute | solution.py:35
  122.0 5.2 %collective-permute-start.22 = (f32[128]{0:T(128)S(1)}, f32[128]{0:T(128)S(1)}, u32[]{:S(2)}, u32[]{:S(2)}) collective-permute-start(f32[128]{0:T(128)S(1)} %get-tuple-element.64), channel_id=1, source_target_pairs={{7,127},{15,119},{23,111},{31,103},{39,95},{47,87},{55,79},{63,71}... | collective-permute-start | bytes 1544 | tf_op jit(solution)/shard_map/ppermute | solution.py:37
  122.7 4.4 %collective-permute-start.21 = (f32[64]{0:T(128)S(1)}, f32[64]{0:T(128)S(1)}, u32[]{:S(2)}, u32[]{:S(2)}) collective-permute-start(f32[64]{0:T(128)S(1)} %get-tuple-element.28), channel_id=1, source_target_pairs={{0,8},{8,16},{16,24},{24,32},{32,40},{40,48},{48,56},{56,64},{64,7... | collective-permute-start | bytes 776 | tf_op jit(solution)/shard_map/ppermute | solution.py:33
  124.0 3.0 %collective-permute-start.20 = (f32[64]{0:T(128)S(1)}, f32[64]{0:T(128)S(1)}, u32[]{:S(2)}, u32[]{:S(2)}) collective-permute-start(f32[64]{0:T(128)S(1)} %get-tuple-element.29), channel_id=1, source_target_pairs={{8,0},{16,8},{24,16},{32,24},{40,32},{48,40},{56,48},{64,56},{72,6... | collective-permute-start | bytes 776 | tf_op jit(solution)/shard_map/ppermute | solution.py:32
  124.0 4.3 %collective-permute-start.23 = (f32[128]{0:T(128)S(1)}, f32[128]{0:T(128)S(1)}, u32[]{:S(2)}, u32[]{:S(2)}) collective-permute-start(f32[128]{0:T(128)S(1)} %get-tuple-element.63), channel_id=1, source_target_pairs={{1,0},{2,1},{3,2},{4,3},{5,4},{6,5},{7,6},{9,8},{10,9},{11,10},{12... | collective-permute-start | bytes 1544 | tf_op jit(solution)/shard_map/ppermute | solution.py:34
